TPU v7x, 256 devices: a whole 4x4x8 slice. The times are simulated.
256 devices in a mesh: prow: 8 (over y, x_hi), pcol: 32 (over x_lo, z, core).
Axes of the slice: x: 4 (x_hi: 2, x_lo: 2; x = x_hi * 2 + x_lo), y: 4, z: 8, core: 2. Of those that a mesh axis runs over, the one named last changes fastest.
Arguments:
- covariance: float32 [8, 8, 256, 32, 2, 256], P('prow', None, None, 'pcol'), may hold values from 0 to 3, as said below
Outputs:
- factored: float32 [8, 8, 256, 32, 2, 256], P('prow', None, None, 'pcol')
Inputs may be any that keep to these rules, and one draw needn't show every extreme that they name: covariance is symmetric and positive definite.
All inputs are finite; a program needn't handle non-finite values.
Results may differ from a plain program's by a relative error of at most 0.0003.
Values sent between devices are 32-bit elements; how exact they have to be, the bound alone decides.
No kernel may reach another device: no remote copies, remote signals or barrier semaphores. Data moves between devices by JAX's collectives and lax.ppermute only.
A program may use at most 64 MiB of HBM per device.

v0:
```python
import jax
import jax.numpy as jnp
from jax import lax
from jax.sharding import PartitionSpec as P

PANELS = 2


def from_root(block, axis, owner):
    block = jnp.where(lax.axis_index(axis) == owner, block, jnp.zeros_like(block))
    return lax.psum(block, axis)


def solve_rows(factor, column):
    count, tile, _ = column.shape
    stacked = jnp.transpose(column, (2, 0, 1)).reshape(tile, count * tile)
    solved = jax.scipy.linalg.solve_triangular(factor, stacked, lower=True)
    return solved.reshape(tile, count, tile).transpose(1, 2, 0)


def outer_update(row_terms, col_terms):
    return jnp.einsum("rae,cbe->racb", row_terms, col_terms, precision=lax.Precision.HIGHEST)


def per_device(covariance):
    prows = lax.axis_size("prow")
    pcols = lax.axis_size("pcol")
    prow_at = lax.axis_index("prow")
    pcol_at = lax.axis_index("pcol")
    rt_count = covariance.shape[1]
    tile = covariance.shape[2]
    ct_count = covariance.shape[4]
    ratio = pcols // prows
    tiles = covariance.reshape(rt_count, tile, ct_count, tile)
    row_index = jnp.arange(rt_count, dtype=jnp.int32) * prows + prow_at
    col_index = jnp.arange(ct_count, dtype=jnp.int32) * pcols + pcol_at
    for panel in range(PANELS):
        tile_row = panel // prows
        tile_col = panel // pcols
        column = tiles[:, :, tile_col, :]
        keep = row_index[:, None, None]
        diagonal = from_root(column[tile_row], "prow", panel % prows)
        factor = jnp.linalg.cholesky(diagonal)
        solved = solve_rows(factor, column)
        local_rows = jnp.where(keep > panel, solved, jnp.where(keep == panel, factor[None], 0.0))
        panel_rows = from_root(local_rows, "pcol", panel % pcols)
        grouped = panel_rows.reshape(ct_count, ratio, tile, tile)
        candidate = lax.dynamic_index_in_dim(grouped, pcol_at // prows, 1, keepdims=False)
        panel_cols = from_root(candidate, "prow", pcol_at % prows)
        rows_term = jnp.where(keep > panel, panel_rows, 0.0)
        cols_term = jnp.where(col_index[:, None, None] > panel, panel_cols, 0.0)
        tiles = tiles - outer_update(rows_term, cols_term)
        owner = pcol_at == panel % pcols
        tiles = tiles.at[:, :, tile_col, :].set(
            jnp.where(owner, panel_rows, tiles[:, :, tile_col, :])
        )
        upper_mask = (row_index == panel)[:, None, None, None] & (col_index > panel)[
            None, None, :, None
        ]
        tiles = jnp.where(upper_mask, 0.0, tiles)
    return tiles.reshape(1, rt_count, tile, 1, ct_count, tile)


def solution(mesh):
    return jax.shard_map(
        per_device,
        mesh=mesh,
        in_specs=(P("prow", None, None, "pcol", None, None),),
        out_specs=P("prow", None, None, "pcol", None, None),
        check_vma=False,
    )
```

profile of v0, /device:TPU:1, one launch (start us, length us, event | category | flops | bytes accessed | tf_op | source)
XLA Modules:
  0.0 1009.2 jit_solution(12726510385687905190)
XLA Ops:
  6.5 7.2 copy.17
  13.7 1.7 fusion.25
  15.5 3.1 slice_bitcast_fusion.3
  18.6 1.9 copy.19
  20.5 83.6 %all-reduce.8.cloned.1.call-done = f32[256,256]{0,1:T(8,128)} async-done(((f32[256,256]{0,1:T(8,128)}), f32[256,256]{0,1:T(8,128)}) %all-reduce.8.cloned.1.call-update) | async-done | bytes 262160 | tf_op jit(solution)/shard_map/psum | solution.py:11
  104.1 1.1 copy.18
  105.2 1.0 fusion.27
  106.2 11.7 %cholesky.130 = f32[128,128]{1,0:T(8,128)S(1)} custom-call(f32[128,128]{1,0:T(8,128)S(1)} %cholesky.194), custom_call_target="Cholesky" | custom-call | tf_op jit(solution)/shard_map/jit(cholesky)/cholesky | solution.py:43
  118.0 9.8 custom-call.13
  128.3 11.7 %cholesky.147 = f32[128,128]{1,0:T(8,128)S(1)} custom-call(f32[128,128]{1,0:T(8,128)S(1)} %convolution_subtract_fusion.5), custom_call_target="Cholesky" | custom-call | tf_op jit(solution)/shard_map/jit(cholesky)/cholesky | solution.py:43
  142.1 3.9 while.6
  142.7 1.3 bitcast_dynamic-update-slice_fusion.4
  144.7 1.3 bitcast_dynamic-update-slice_fusion.4
  146.0 20.1 %custom-call.14 = f32[2,128,128]{1,2,0:T(8,128)S(1)} custom-call(f32[2,128,128]{2,1,0:T(8,128)S(1)} %get-tuple-element.45), custom_call_target="InvertDiagBlocksLowerTriangular" | custom-call | tf_op jit(solution)/shard_map/jit(_solve_triangular)/triangular_solve | solution.py:17
  166.2 1.1 fusion.14
  167.2 1.8 convolution_subtract_fusion.1
  169.1 1.1 fusion.40
  170.3 1.9 copy.20
  172.2 1.9 copy.21
  174.2 1.6 fusion.9
  176.0 232.6 %all-reduce.10.cloned.1.call-done = f32[8,256,256]{1,2,0:T(8,128)} async-done(((f32[8,256,256]{1,2,0:T(8,128)}), f32[8,256,256]{1,2,0:T(8,128)}) %all-reduce.10.cloned.1.call-update) | async-done | bytes 2097168 | tf_op jit(solution)/shard_map/psum | solution.py:11
  408.6 1.2 constant_dynamic-slice_fusion.3
  411.0 85.0 %all-reduce.12.cloned.1.call-done = f32[2,256,256]{2,1,0:T(8,128)} async-done(((f32[2,256,256]{2,1,0:T(8,128)}), f32[2,256,256]{2,1,0:T(8,128)}) %all-reduce.12.cloned.1.call-update) | async-done | bytes 524304 | tf_op jit(solution)/shard_map/psum | solution.py:11
  496.0 5.9 convolution_subtract_fusion.3
  502.9 2.0 copy-done
  505.7 3.1 slice_bitcast_fusion.1
  508.8 2.1 copy.29
  510.9 82.8 %all-reduce.14.cloned.1.call-done = f32[256,256]{0,1:T(8,128)} async-done(((f32[256,256]{0,1:T(8,128)}), f32[256,256]{0,1:T(8,128)}) %all-reduce.14.cloned.1.call-update) | async-done | bytes 262160 | tf_op jit(solution)/shard_map/psum | solution.py:11
  593.7 1.1 copy.28
  595.8 11.7 %cholesky.164 = f32[128,128]{1,0:T(8,128)S(1)} custom-call(f32[128,128]{1,0:T(8,128)S(1)} %cholesky.197), custom_call_target="Cholesky" | custom-call | tf_op jit(solution)/shard_map/jit(cholesky)/cholesky | solution.py:43
  607.5 9.8 custom-call.15
  617.8 11.7 %cholesky.181 = f32[128,128]{1,0:T(8,128)S(1)} custom-call(f32[128,128]{1,0:T(8,128)S(1)} %convolution_subtract_fusion.4), custom_call_target="Cholesky" | custom-call | tf_op jit(solution)/shard_map/jit(cholesky)/cholesky | solution.py:43
  632.2 4.1 while.7
  632.9 1.3 bitcast_dynamic-update-slice_fusion.5
  635.0 1.3 bitcast_dynamic-update-slice_fusion.5
  636.3 19.9 %custom-call.16 = f32[2,128,128]{1,2,0:T(8,128)S(1)} custom-call(f32[2,128,128]{2,1,0:T(8,128)S(1)} %get-tuple-element.46), custom_call_target="InvertDiagBlocksLowerTriangular" | custom-call | tf_op jit(solution)/shard_map/jit(_solve_triangular)/triangular_solve | solution.py:17
  656.2 1.1 fusion.12
  657.3 1.8 convolution_subtract_fusion
  659.1 1.1 fusion.36
  660.3 1.9 copy.30
  662.2 1.9 copy.31
  664.3 1.6 fusion.8
  666.0 232.6 %all-reduce.16.cloned.1.call-done = f32[8,256,256]{1,2,0:T(8,128)} async-done(((f32[8,256,256]{1,2,0:T(8,128)}), f32[8,256,256]{1,2,0:T(8,128)}) %all-reduce.16.cloned.1.call-update) | async-done | bytes 2097168 | tf_op jit(solution)/shard_map/psum | solution.py:11
  898.6 1.2 constant_dynamic-slice_fusion.2
  901.0 84.9 %all-reduce.18.cloned.1.call-done = f32[2,256,256]{2,1,0:T(8,128)} async-done(((f32[2,256,256]{2,1,0:T(8,128)}), f32[2,256,256]{2,1,0:T(8,128)}) %all-reduce.18.cloned.1.call-update) | async-done | bytes 524304 | tf_op jit(solution)/shard_map/psum | solution.py:11
  985.9 5.9 convolution_subtract_fusion.2
  992.3 2.6 select_bitcast_fusion
  994.9 7.2 copy.37
  (65 shorter events, 12.3 us)
Async XLA Ops:
  6.5 97.6 %all-reduce.8.cloned.1.call-start = ((), (), s32[]{:S(2)}) async-start(), calls=%async_computation | async-start | bytes 524288 | tf_op jit(solution)/shard_map/psum | solution.py:11
  15.4 393.1 %all-reduce.10.cloned.1.call-start = ((), (), s32[]{:S(2)}) async-start(), calls=%async_computation.1 | async-start | bytes 4194304 | tf_op jit(solution)/shard_map/psum | solution.py:11
  175.9 320.2 %all-reduce.12.cloned.1.call-start = ((), (), s32[]{:S(2)}) async-start(), calls=%async_computation.2 | async-start | bytes 1048576 | tf_op jit(solution)/shard_map/psum | solution.py:11
  408.6 87.5 %copy-start.1 = (f32[8,256,256]{1,2,0:T(8,128)S(1)}, f32[8,256,256]{1,2,0:T(8,128)}, u32[]{:S(2)}) copy-start(f32[8,256,256]{1,2,0:T(8,128)} %all-reduce.10.cloned.1.call-done) | copy-start | bytes 6291460
  410.9 182.8 %all-reduce.14.cloned.1.call-start = ((), (), s32[]{:S(2)}) async-start(), calls=%async_computation.3 | async-start | bytes 524288 | tf_op jit(solution)/shard_map/psum | solution.py:11
  502.9 2.0 copy-start
  505.7 392.9 %all-reduce.16.cloned.1.call-start = ((), (), s32[]{:S(2)}) async-start(), calls=%async_computation.4 | async-start | bytes 4194304 | tf_op jit(solution)/shard_map/psum | solution.py:11
  665.9 320.0 %all-reduce.18.cloned.1.call-start = ((), (), s32[]{:S(2)}) async-start(), calls=%async_computation.5 | async-start | bytes 1048576 | tf_op jit(solution)/shard_map/psum | solution.py:11
  898.6 87.3 %copy-start.2 = (f32[8,256,256]{1,2,0:T(8,128)S(1)}, f32[8,256,256]{1,2,0:T(8,128)}, u32[]{:S(2)}) copy-start(f32[8,256,256]{1,2,0:T(8,128)} %all-reduce.16.cloned.1.call-done) | copy-start | bytes 6291460
Sparse Core Ops, SparseCore 0:
  15.5 88.5 all-reduce.7
  176.0 232.5 all-reduce.9
  411.2 84.8 all-reduce.11
  505.8 87.8 all-reduce.13
  666.0 232.5 all-reduce.15
  901.1 84.8 all-reduce.17
where the time goes:
time: 1020 us; the launch traced here: 1010 us
  waiting for transfers between devices  802 us (79%)
  other arithmetic  123 us (12%)
  local copies, waits for them, and re-layouts  47.4 us (5%)
  matrix products  20.7 us (2%)
  between operations  16.6 us (2%)
    psum x6, waiting for transfers between devices, from_root(): return lax.psum(block, axis)  802 us
    another operation x13, other arithmetic, per_device(): factor = jnp.linalg.cholesky(diagonal)  68.7 us
    another operation x7, other arithmetic, solve_rows(): solved = jax.scipy.linalg.solve_triangular(factor, stacked, lower=True)  40.4 us
  transfers between devices with their start and end apart: 6, of which 6 were waited for; matrix products, arithmetic and copies ran while one was open for 1% of the time, Pallas kernels for 0%

commit v1 on v0

v1 whole, which is shorter than its diff:
```python
import jax
import jax.numpy as jnp
from jax import lax
from jax.sharding import PartitionSpec as P

PANELS = 2
HI = lax.Precision.HIGHEST


def prow_from_first_two(x, prows):
    me = lax.axis_index("prow")
    got = [x]
    for d in range(1, prows):
        got.append(lax.ppermute(x, "prow", [(0, d), (1, (1 + d) % prows)]))
    stack = jnp.stack(got)
    return stack[me], stack[(me + prows - 1) % prows]


def pcol_tree_rounds(pcols):
    zs = pcols // 4

    def idx(x, z, core):
        return (x * zs + z % zs) * 2 + core

    rounds = []
    a_have = [(0, 0)]
    b_have = [(0, 0)]
    steps_a = [("x", 0), ("z", zs // 2)]
    steps_b = [("z", zs // 2), ("x", 0)]
    s = zs // 4
    while s >= 1:
        steps_a.append(("z", s))
        steps_b.append(("z", -s))
        s //= 2
    for (ka, da), (kb, db) in zip(steps_a, steps_b):
        pairs = []
        new_a = []
        for x, z in a_have:
            t = (1 - x, z) if ka == "x" else (x, (z + da) % zs)
            pairs.append((idx(x, z, 0), idx(t[0], t[1], 0)))
            new_a.append(t)
        new_b = []
        for x, z in b_have:
            t = (1 - x, z) if kb == "x" else (x, (z + db) % zs)
            pairs.append((idx(x, z, 1), idx(t[0], t[1], 1)))
            new_b.append(t)
        a_have += new_a
        b_have += new_b
        rounds.append(pairs)
    return rounds


def pcol_broadcast_pair(buf, pcols):
    me = lax.axis_index("pcol")
    for pairs in pcol_tree_rounds(pcols):
        got = lax.ppermute(buf, "pcol", pairs)
        targets = jnp.array([t for _, t in pairs], jnp.int32)
        hit = jnp.any(targets == me)
        buf = jnp.where(hit, got, buf)
    other = lax.ppermute(buf, "pcol", [(i, i ^ 1) for i in range(pcols)])
    core0 = (me % 2) == 0
    return jnp.where(core0, buf, other), jnp.where(core0, other, buf)


def per_device(covariance):
    prows = lax.axis_size("prow")
    pcols = lax.axis_size("pcol")
    p = lax.axis_index("prow")
    q = lax.axis_index("pcol")
    rt = covariance.shape[1]
    tile = covariance.shape[2]
    ct = covariance.shape[4]
    nb = PANELS * tile
    tiles = covariance.reshape(rt, tile, ct, tile)

    t0, t1 = prow_from_first_two(tiles[0], prows)

    col0, col1 = pcol_broadcast_pair(tiles[:, :, 0, :], pcols)

    diag_a, diag_b = pcol_broadcast_pair(jnp.stack([t0[:, 0, :], t1[:, 0, :]]), pcols)
    block = jnp.concatenate(
        [
            jnp.concatenate([diag_a[0], diag_b[0]], axis=1),
            jnp.concatenate([diag_a[1], diag_b[1]], axis=1),
        ],
        axis=0,
    )
    factor = jnp.tril(jnp.linalg.cholesky(block))
    inverse = jax.scipy.linalg.solve_triangular(
        factor, jnp.eye(nb, dtype=factor.dtype), lower=True
    )

    rows_panel = jnp.concatenate([col0, col1], axis=-1)
    cols_panel = jnp.concatenate(
        [jnp.transpose(t0, (1, 2, 0)), jnp.transpose(t1, (1, 2, 0))], axis=-1
    )
    rows_solved = jnp.einsum("rak,bk->rab", rows_panel, inverse, precision=HI)
    cols_solved = jnp.einsum("cak,bk->cab", cols_panel, inverse, precision=HI)
    update = tiles - jnp.einsum("rak,cbk->racb", rows_solved, cols_solved, precision=HI)

    row_index = jnp.arange(rt, dtype=jnp.int32) * prows + p
    col_index = jnp.arange(ct, dtype=jnp.int32) * pcols + q
    trailing = (row_index >= PANELS)[:, None, None, None] & (col_index >= PANELS)[
        None, None, :, None
    ]
    out = jnp.where(trailing, update, 0.0)

    qc = jnp.minimum(q, PANELS - 1)
    pc = jnp.minimum(p, PANELS - 1)
    panel_vals = lax.dynamic_slice_in_dim(rows_solved, qc * tile, tile, axis=2)
    diag_tile = lax.dynamic_slice(factor, (pc * tile, qc * tile), (tile, tile))
    panel_vals = panel_vals.at[0].set(jnp.where(p < PANELS, diag_tile, panel_vals[0]))
    out = out.at[:, :, 0, :].set(jnp.where(q < PANELS, panel_vals, out[:, :, 0, :]))
    return out.reshape(1, rt, tile, 1, ct, tile)


def solution(mesh):
    return jax.shard_map(
        per_device,
        mesh=mesh,
        in_specs=(P("prow", None, None, "pcol", None, None),),
        out_specs=P("prow", None, None, "pcol", None, None),
        check_vma=False,
    )
```

time: 1020 us -> 336 us (0.33)
  waiting for transfers between devices: 802 us -> 38.9 us
  starting transfers between devices: 0.21 us -> 72.2 us
  other arithmetic: 123 us -> 144 us
  between operations: 16.6 us -> 3.49 us
    psum x6 -> x0, waiting for transfers between devices: 802 us -> none  [from_root(): return lax.psum(block, axis)]
    ppermute x0 -> x17, starting transfers between devices: none -> 72.2 us  [the longest x8 27 us: pcol_broadcast_pair(): got = lax.ppermute(buf, 'pcol', pairs)]
    ppermute x0 -> x17, waiting for transfers between devices: none -> 38.9 us  [the longest x8 19.8 us: pcol_broadcast_pair(): got = lax.ppermute(buf, 'pcol', pairs)]
    another operation x20 -> x19, other arithmetic: 109 us -> 122 us  [the longest x15 79.4 us: per_device(): factor = jnp.tril(jnp.linalg.cholesky(block))]
    reshape x3 -> x0, local copies, waits for them, and re-layouts: 11 us -> none  [the longest x1 7.19 us: per_device(): return tiles.reshape(1, rt_count, tile, 1, ct_count, tile)]
  transfers between devices with their start and end apart: 6 -> 17, of which waited for: 6 -> 6; matrix products, arithmetic and copies ran while one was open for 1% -> 55% of each run, Pallas kernels for 0% -> 0%
where the time goes in v1:
time: 336 us; the launch traced here: 329 us
  other arithmetic  144 us (43%)
  starting transfers between devices  72.2 us (21%)
  local copies, waits for them, and re-layouts  45.4 us (14%)
  waiting for transfers between devices  38.9 us (12%)
  matrix products  25.8 us (8%)
  between operations  3.49 us (1%)
    another operation x15, other arithmetic, per_device(): factor = jnp.tril(jnp.linalg.cholesky(block))  79.4 us
    another operation x3, other arithmetic, per_device(): jax.scipy.linalg.solve_triangular(factor, jnp.eye(nb, dtype=factor.dtype)...  41.7 us
    ppermute x8, starting transfers between devices, pcol_broadcast_pair(): got = lax.ppermute(buf, 'pcol', pairs)  27 us
    ppermute x2, starting transfers between devices, pcol_broadcast_pair(): other = lax.ppermute(buf, 'pcol', [(i, i ^ 1) for i in range(pcols)])  25.4 us
    ppermute x7, starting transfers between devices, prow_from_first_two(): got.append(lax.ppermute(x, 'prow', [(0, d), (1, (1 + d) % prows)]))  19.8 us
    ppermute x8, waiting for transfers between devices, pcol_broadcast_pair(): got = lax.ppermute(buf, 'pcol', pairs)  19.8 us
    ppermute x7, waiting for transfers between devices, prow_from_first_two(): got.append(lax.ppermute(x, 'prow', [(0, d), (1, (1 + d) % prows)]))  19.1 us
    unnamed x31, local copies, waits for them, and re-layouts  18.7 us
  transfers between devices with their start and end apart: 17, of which 6 were waited for; matrix products, arithmetic and copies ran while one was open for 55% of the time, Pallas kernels for 0%

profile of v1, /device:TPU:1, one launch (start us, length us, event | category | flops | bytes accessed | tf_op | source)
XLA Modules:
  0.0 329.4 jit_solution(12686673049741603659)
XLA Ops:
  1.2 7.9 %collective-permute-start.11 = (f32[256,2,256]{2,1,0:T(2,128)S(1)}, f32[256,2,256]{2,1,0:T(2,128)S(1)}, u32[]{:S(2)}, u32[]{:S(2)}) collective-permute-start(f32[256,2,256]{2,1,0:T(2,128)S(1)} %slice_bitcast_fusion.2), channel_id=1, source_target_pairs={{0,224},{32,0},{1,225},{33,1},{2,226},{34,2},{3,227},{35,3},{4,228... | collective-permute-start | bytes 1572872 | tf_op jit(solution)/shard_map/ppermute | solution.py:14
  9.2 2.1 collective-permute-start.10
  11.3 2.1 collective-permute-start.7
  13.4 2.1 collective-permute-start.6
  15.5 3.0 collective-permute-start.5
  18.4 2.7 copy.21
  21.1 1.9 copy-done.1
  23.2 2.0 bitcast_dynamic-update-slice_fusion.8
  25.2 17.0 %collective-permute-done.5 = f32[256,2,256]{2,1,0:T(2,128)} collective-permute-done((f32[256,2,256]{2,1,0:T(2,128)S(1)}, f32[256,2,256]{2,1,0:T(2,128)}, u32[]{:S(2)}, u32[]{:S(2)}) %collective-permute-start.5) | collective-permute-done | bytes 524320 | tf_op jit(solution)/shard_map/ppermute | solution.py:14
  43.6 2.0 bitcast_dynamic-update-slice_fusion.7
  45.6 2.1 collective-permute-done.6
  49.0 2.0 bitcast_dynamic-update-slice_fusion.6
  51.0 10.2 %collective-permute-start = (f32[8,256,256]{2,1,0:T(8,128)S(1)}, f32[8,256,256]{2,1,0:T(8,128)}, u32[]{:S(2)}, u32[]{:S(2)}) collective-permute-start(f32[8,256,256]{2,1,0:T(8,128)S(1)} %slice_bitcast_fusion.1), channel_id=1, source_target_pairs={{0,16},{1,9},{32,48},{33,41},{64,80},{65,73},{96,112},{97,105},{12... | collective-permute-start | bytes 6291464 | tf_op jit(solution)/shard_map/ppermute | solution.py:56
  61.2 2.0 bitcast_dynamic-update-slice_fusion.5
  65.2 2.0 bitcast_dynamic-update-slice_fusion.2
  73.0 4.7 %collective-permute-start.12 = (f32[2,256,256]{1,2,0:T(8,128)}, f32[2,256,256]{1,2,0:T(8,128)S(1)}, u32[]{:S(2)}, u32[]{:S(2)}) collective-permute-start(f32[2,256,256]{1,2,0:T(8,128)} %pad_maximum_fusion), channel_id=1, source_target_pairs={{0,16},{1,9},{32,48},{33,41},{64,80},{65,73},{96,112},{97,105},{12... | collective-permute-start | bytes 1572872 | tf_op jit(solution)/shard_map/ppermute | solution.py:56
  78.4 10.1 %collective-permute-done.12 = f32[2,256,256]{1,2,0:T(8,128)S(1)} collective-permute-done((f32[2,256,256]{1,2,0:T(8,128)}, f32[2,256,256]{1,2,0:T(8,128)S(1)}, u32[]{:S(2)}, u32[]{:S(2)}) %collective-permute-start.12) | collective-permute-done | bytes 524320 | tf_op jit(solution)/shard_map/ppermute | solution.py:56
  90.7 2.6 broadcast_select_fusion
  93.3 2.7 collective-permute-start.1
  100.2 5.3 %collective-permute-done.14 = f32[2,256,256]{1,2,0:T(8,128)S(1)} collective-permute-done((f32[2,256,256]{1,2,0:T(8,128)S(1)}, f32[2,256,256]{1,2,0:T(8,128)S(1)}, u32[]{:S(2)}, u32[]{:S(2)}) %collective-permute-start.14) | collective-permute-done | bytes 524320 | tf_op jit(solution)/shard_map/ppermute | solution.py:56
  109.4 4.2 %collective-permute-done.15 = f32[2,256,256]{1,2,0:T(8,128)S(1)} collective-permute-done((f32[2,256,256]{1,2,0:T(8,128)S(1)}, f32[2,256,256]{1,2,0:T(8,128)S(1)}, u32[]{:S(2)}, u32[]{:S(2)}) %collective-permute-start.15) | collective-permute-done | bytes 524320 | tf_op jit(solution)/shard_map/ppermute | solution.py:56
  114.3 21.3 %collective-permute-start.16 = (f32[2,256,256]{1,2,0:T(8,128)S(1)}, f32[2,256,256]{1,2,0:T(8,128)S(1)}, u32[]{:S(2)}, u32[]{:S(2)}) collective-permute-start(f32[2,256,256]{1,2,0:T(8,128)S(1)} %broadcast_select_fusion.9), channel_id=1, source_target_pairs={{0,1},{1,0},{2,3},{3,2},{4,5},{5,4},{6,7},{7,6},{8,9},{9,8},{10,11... | collective-permute-start | bytes 1572872 | tf_op jit(solution)/shard_map/ppermute | solution.py:60
  136.4 2.2 broadcast_select_fusion.1
  138.5 2.8 collective-permute-start.2
  142.2 11.7 %cholesky.104 = f32[128,128]{1,0:T(8,128)S(1)} custom-call(f32[128,128]{1,0:T(8,128)S(1)} %cholesky.266), custom_call_target="Cholesky" | custom-call | tf_op jit(solution)/shard_map/jit(cholesky)/cholesky | solution.py:88
  154.0 9.8 %custom-call.31 = f32[1,128,128]{1,2,0:T(8,128)S(1)} custom-call(f32[1,128,128]{2,1,0:T(8,128)S(1)} %get-tuple-element.68), custom_call_target="InvertDiagBlocksLowerTriangular" | custom-call | tf_op jit(solution)/shard_map/jit(cholesky)/cholesky | solution.py:88
  164.6 11.7 %cholesky.217 = f32[128,128]{1,0:T(8,128)S(1)} custom-call(f32[128,128]{1,0:T(8,128)S(1)} %cholesky.270), custom_call_target="Cholesky" | custom-call | tf_op jit(solution)/shard_map/jit(cholesky)/cholesky | solution.py:88
  176.4 10.2 %custom-call.32 = f32[1,128,128]{1,2,0:T(8,128)S(1)} custom-call(f32[1,128,128]{2,1,0:T(8,128)S(1)} %get-tuple-element.65), custom_call_target="InvertDiagBlocksLowerTriangular" | custom-call | tf_op jit(solution)/shard_map/jit(cholesky)/cholesky | solution.py:88
  186.6 2.6 broadcast_select_fusion.2
  189.2 2.7 collective-permute-start.3
  193.4 11.7 %cholesky.238 = f32[128,128]{1,0:T(8,128)S(1)} custom-call(f32[128,128]{1,0:T(8,128)S(1)} %cholesky.275), custom_call_target="Cholesky" | custom-call | tf_op jit(solution)/shard_map/jit(cholesky)/cholesky | solution.py:88
  205.2 9.8 %custom-call.33 = f32[1,128,128]{1,2,0:T(8,128)S(1)} custom-call(f32[1,128,128]{2,1,0:T(8,128)S(1)} %get-tuple-element.62), custom_call_target="InvertDiagBlocksLowerTriangular" | custom-call | tf_op jit(solution)/shard_map/jit(cholesky)/cholesky | solution.py:88
  216.4 11.7 %cholesky.255 = f32[128,128]{1,0:T(8,128)S(1)} custom-call(f32[128,128]{1,0:T(8,128)S(1)} %convolution_subtract_fusion.5), custom_call_target="Cholesky" | custom-call | tf_op jit(solution)/shard_map/jit(cholesky)/cholesky | solution.py:88
  233.5 1.6 fusion.15
  235.1 2.3 broadcast_select_fusion.3
  237.3 4.2 %collective-permute-start.4 = (f32[8,256,256]{2,1,0:T(8,128)}, f32[8,256,256]{2,1,0:T(8,128)S(1)}, u32[]{:S(2)}, u32[]{:S(2)}) collective-permute-start(f32[8,256,256]{2,1,0:T(8,128)} %broadcast_select_fusion.3), channel_id=1, source_target_pairs={{0,1},{1,0},{2,3},{3,2},{4,5},{5,4},{6,7},{7,6},{8,9},{9,8},{10,11... | collective-permute-start | bytes 6291464 | tf_op jit(solution)/shard_map/ppermute | solution.py:60
  241.5 14.2 %while.3 = (s32[]{:T(128)}, f32[512,512]{1,0:T(8,128)}, s32[4,2]{0,1:T(2,128)S(1)}, f32[4,128,128]{2,1,0:T(8,128)}, s32[]{:T(128)}) while((s32[]{:T(128)}, f32[512,512]{1,0:T(8,128)}, s32[4,2]{0,1:T(2,128)S(1)}, f32[4,128,128]{2,1,0:T(8,128)}, s32[]{:T(128)}) %tuple.41), condition=%wide.while_cond.2, body=%wide.while_body.2.sunk | while | flops 2 | bytes 132205 | solution.py:89
  242.2 2.9 bitcast_dynamic-update-slice_fusion.10
  245.7 2.9 bitcast_dynamic-update-slice_fusion.10
  249.3 2.9 bitcast_dynamic-update-slice_fusion.10
  252.8 2.8 bitcast_dynamic-update-slice_fusion.10
  255.7 40.1 %custom-call.34 = f32[4,128,128]{1,2,0:T(8,128)S(1)} custom-call(f32[4,128,128]{2,1,0:T(8,128)} %get-tuple-element.36), custom_call_target="InvertDiagBlocksLowerTriangular" | custom-call | tf_op jit(solution)/shard_map/jit(_solve_triangular)/triangular_solve | solution.py:89
  302.4 1.9 convolution_bitcast_fusion
  304.3 2.0 broadcast_select_fusion.5
  306.3 6.9 %fusion = f32[8,256,512]{2,1,0:T(8,128)S(1)} fusion(f32[8,256,256]{2,1,0:T(8,128)S(1)} %get-tuple-element.50, f32[8,256,256]{2,1,0:T(8,128)S(1)} %get-tuple-element.49, f32[128,512]{1,0:T(8,128)S(1)} %fusion.38, f32[128,512]{1,0:T(8,128)S(1)} %fusion.39, f32[128,512]{1,0:T(8,128)S(1)} %fusion.41, f32[128,512]{1,0:T(8,128)S(1)} %fusion.29), kind=kOutput, calls=%fused_computation.2 | convolution fusion | flops 6444285952 | bytes 9437184 | tf_op jit(solution)/shard_map/rak,bk->rab/dot_general | solution.py:97
  313.7 1.7 copy-done
  315.4 7.0 %subtract_select_fusion = f32[8,256,2,256]{3,1,0,2:T(8,128)S(1)} fusion(f32[2,256,512,1]{2,1,3,0:T(8,128)S(1)} %convolution_bitcast_fusion, f32[8,256,512]{2,1,0:T(8,128)S(1)} %fusion, pred[8,2]{0,1:T(4,128)(4,1)S(1)} %broadcast_and_fusion, f32[1,8,256,1,2,256]{5,4,3,2,1,0:T(2,128)S(1)} %copy-done), kind=kOutput, calls=%fused_computation.9 | convolution fusion | flops 6444548096 | bytes 13631504 | tf_op jit(solution)/shard_map/rak,cbk->racb/dot_general | solution.py:99
  323.9 5.2 %copy.15 = f32[1,8,256,1,2,256]{5,4,3,2,1,0:T(2,128)} copy(f32[1,8,256,1,2,256]{5,2,1,4,3,0:T(8,128)S(1)} %fusion.10) | data formatting | bytes 8388608 | tf_op jit(solution)/shard_map/scatter | solution.py:113
  (106 shorter events, 42.6 us)
Async XLA Ops:
  1.2 66.0 %collective-permute-start.11 = (f32[256,2,256]{2,1,0:T(2,128)S(1)}, f32[256,2,256]{2,1,0:T(2,128)S(1)}, u32[]{:S(2)}, u32[]{:S(2)}) collective-permute-start(f32[256,2,256]{2,1,0:T(2,128)S(1)} %slice_bitcast_fusion.2), channel_id=1, source_target_pairs={{0,224},{32,0},{1,225},{33,1},{2,226},{34,2},{3,227},{35,3},{4,228... | collective-permute-start | bytes 1572872 | tf_op jit(solution)/shard_map/ppermute | solution.py:14
  9.2 56.0 %collective-permute-start.10 = (f32[256,2,256]{2,1,0:T(2,128)S(1)}, f32[256,2,256]{2,1,0:T(2,128)}, u32[]{:S(2)}, u32[]{:S(2)}) collective-permute-start(f32[256,2,256]{2,1,0:T(2,128)S(1)} %slice_bitcast_fusion.2), channel_id=1, source_target_pairs={{0,192},{32,224},{1,193},{33,225},{2,194},{34,226},{3,195},{35,227... | collective-permute-start | bytes 1572872 | tf_op jit(solution)/shard_map/ppermute | solution.py:14
  11.3 39.7 %collective-permute-start.7 = (f32[256,2,256]{2,1,0:T(2,128)S(1)}, f32[256,2,256]{2,1,0:T(2,128)}, u32[]{:S(2)}, u32[]{:S(2)}) collective-permute-start(f32[256,2,256]{2,1,0:T(2,128)S(1)} %slice_bitcast_fusion.2), channel_id=1, source_target_pairs={{0,96},{32,128},{1,97},{33,129},{2,98},{34,130},{3,99},{35,131},{4... | collective-permute-start | bytes 1572872 | tf_op jit(solution)/shard_map/ppermute | solution.py:14
  13.4 34.3 %collective-permute-start.6 = (f32[256,2,256]{2,1,0:T(2,128)S(1)}, f32[256,2,256]{2,1,0:T(2,128)}, u32[]{:S(2)}, u32[]{:S(2)}) collective-permute-start(f32[256,2,256]{2,1,0:T(2,128)S(1)} %slice_bitcast_fusion.2), channel_id=1, source_target_pairs={{0,64},{32,96},{1,65},{33,97},{2,66},{34,98},{3,67},{35,99},{4,68}... | collective-permute-start | bytes 1572872 | tf_op jit(solution)/shard_map/ppermute | solution.py:14
  15.5 26.8 %collective-permute-start.5 = (f32[256,2,256]{2,1,0:T(2,128)S(1)}, f32[256,2,256]{2,1,0:T(2,128)}, u32[]{:S(2)}, u32[]{:S(2)}) collective-permute-start(f32[256,2,256]{2,1,0:T(2,128)S(1)} %slice_bitcast_fusion.2), channel_id=1, source_target_pairs={{0,32},{32,64},{1,33},{33,65},{2,34},{34,66},{3,35},{35,67},{4,36}... | collective-permute-start | bytes 1572872 | tf_op jit(solution)/shard_map/ppermute | solution.py:14
  21.1 1.9 copy-start.1
  42.2 21.0 %collective-permute-start.8 = (f32[256,2,256]{2,1,0:T(2,128)S(1)}, f32[256,2,256]{2,1,0:T(2,128)S(1)}, u32[]{:S(2)}, u32[]{:S(2)}) collective-permute-start(f32[256,2,256]{2,1,0:T(2,128)S(1)} %slice_bitcast_fusion.2), channel_id=1, source_target_pairs={{0,128},{32,160},{1,129},{33,161},{2,130},{34,162},{3,131},{35,163... | collective-permute-start | bytes 1572872 | tf_op jit(solution)/shard_map/ppermute | solution.py:14
  47.7 16.5 %collective-permute-start.9 = (f32[256,2,256]{2,1,0:T(2,128)S(1)}, f32[256,2,256]{2,1,0:T(2,128)S(1)}, u32[]{:S(2)}, u32[]{:S(2)}) collective-permute-start(f32[256,2,256]{2,1,0:T(2,128)S(1)} %slice_bitcast_fusion.2), channel_id=1, source_target_pairs={{0,160},{32,192},{1,161},{33,193},{2,162},{34,194},{3,163},{35,195... | collective-permute-start | bytes 1572872 | tf_op jit(solution)/shard_map/ppermute | solution.py:14
  51.0 39.7 %collective-permute-start = (f32[8,256,256]{2,1,0:T(8,128)S(1)}, f32[8,256,256]{2,1,0:T(8,128)}, u32[]{:S(2)}, u32[]{:S(2)}) collective-permute-start(f32[8,256,256]{2,1,0:T(8,128)S(1)} %slice_bitcast_fusion.1), channel_id=1, source_target_pairs={{0,16},{1,9},{32,48},{33,41},{64,80},{65,73},{96,112},{97,105},{12... | collective-permute-start | bytes 6291464 | tf_op jit(solution)/shard_map/ppermute | solution.py:56
  65.2 12.6 %copy-start.10 = (s32[2]{0:T(128)S(1)}, s32[2]{0:T(128)}, u32[]{:S(2)}) copy-start(s32[2]{0:T(128)} %constant.272.clone) | copy-start | bytes 28
  71.0 1.2 copy-start.5
  73.0 23.0 %copy-start.9 = (s32[4]{0:T(128)S(1)}, s32[4]{0:T(128)}, u32[]{:S(2)}) copy-start(s32[4]{0:T(128)} %constant.273.clone) | copy-start | bytes 52
  73.0 15.5 %collective-permute-start.12 = (f32[2,256,256]{1,2,0:T(8,128)}, f32[2,256,256]{1,2,0:T(8,128)S(1)}, u32[]{:S(2)}, u32[]{:S(2)}) collective-permute-start(f32[2,256,256]{1,2,0:T(8,128)} %pad_maximum_fusion), channel_id=1, source_target_pairs={{0,16},{1,9},{32,48},{33,41},{64,80},{65,73},{96,112},{97,105},{12... | collective-permute-start | bytes 1572872 | tf_op jit(solution)/shard_map/ppermute | solution.py:56
  89.3 10.1 %copy-start.8 = (s32[8]{0:T(128)S(1)}, s32[8]{0:T(128)}, u32[]{:S(2)}) copy-start(s32[8]{0:T(128)} %constant.274.clone) | copy-start | bytes 100
  89.3 18.3 %copy-start.7 = (s32[16]{0:T(128)S(1)}, s32[16]{0:T(128)}, u32[]{:S(2)}) copy-start(s32[16]{0:T(128)} %constant.275.clone) | copy-start | bytes 196
  89.3 7.4 %collective-permute-start.13 = (f32[2,256,256]{1,2,0:T(8,128)S(1)}, f32[2,256,256]{1,2,0:T(8,128)S(1)}, u32[]{:S(2)}, u32[]{:S(2)}) collective-permute-start(f32[2,256,256]{1,2,0:T(8,128)S(1)} %broadcast_select_fusion.6), channel_id=1, source_target_pairs={{0,8},{16,24},{1,17},{9,25},{32,40},{48,56},{33,49},{41,57},{64,72... | collective-permute-start | bytes 1572872 | tf_op jit(solution)/shard_map/ppermute | solution.py:56
  93.3 43.1 %collective-permute-start.1 = (f32[8,256,256]{2,1,0:T(8,128)S(1)}, f32[8,256,256]{2,1,0:T(8,128)}, u32[]{:S(2)}, u32[]{:S(2)}) collective-permute-start(f32[8,256,256]{2,1,0:T(8,128)S(1)} %broadcast_select_fusion), channel_id=1, source_target_pairs={{0,8},{16,24},{1,17},{9,25},{32,40},{48,56},{33,49},{41,57},{64,72... | collective-permute-start | bytes 6291464 | tf_op jit(solution)/shard_map/ppermute | solution.py:56
  98.1 7.4 %collective-permute-start.14 = (f32[2,256,256]{1,2,0:T(8,128)S(1)}, f32[2,256,256]{1,2,0:T(8,128)S(1)}, u32[]{:S(2)}, u32[]{:S(2)}) collective-permute-start(f32[2,256,256]{1,2,0:T(8,128)S(1)} %broadcast_select_fusion.7), channel_id=1, source_target_pairs={{0,4},{16,20},{8,12},{24,28},{1,13},{9,5},{17,29},{25,21},{32,36},... | collective-permute-start | bytes 1572872 | tf_op jit(solution)/shard_map/ppermute | solution.py:56
  106.3 7.4 %collective-permute-start.15 = (f32[2,256,256]{1,2,0:T(8,128)S(1)}, f32[2,256,256]{1,2,0:T(8,128)S(1)}, u32[]{:S(2)}, u32[]{:S(2)}) collective-permute-start(f32[2,256,256]{1,2,0:T(8,128)S(1)} %broadcast_select_fusion.8), channel_id=1, source_target_pairs={{0,2},{16,18},{8,10},{24,26},{4,6},{20,22},{12,14},{28,30},{1,15},... | collective-permute-start | bytes 1572872 | tf_op jit(solution)/shard_map/ppermute | solution.py:56
  114.3 27.0 %collective-permute-start.16 = (f32[2,256,256]{1,2,0:T(8,128)S(1)}, f32[2,256,256]{1,2,0:T(8,128)S(1)}, u32[]{:S(2)}, u32[]{:S(2)}) collective-permute-start(f32[2,256,256]{1,2,0:T(8,128)S(1)} %broadcast_select_fusion.9), channel_id=1, source_target_pairs={{0,1},{1,0},{2,3},{3,2},{4,5},{5,4},{6,7},{7,6},{8,9},{9,8},{10,11... | collective-permute-start | bytes 1572872 | tf_op jit(solution)/shard_map/ppermute | solution.py:60
  138.5 48.0 %collective-permute-start.2 = (f32[8,256,256]{2,1,0:T(8,128)}, f32[8,256,256]{2,1,0:T(8,128)}, u32[]{:S(2)}, u32[]{:S(2)}) collective-permute-start(f32[8,256,256]{2,1,0:T(8,128)} %broadcast_select_fusion.1), channel_id=1, source_target_pairs={{0,4},{16,20},{8,12},{24,28},{1,13},{9,5},{17,29},{25,21},{32,36},... | collective-permute-start | bytes 6291464 | tf_op jit(solution)/shard_map/ppermute | solution.py:56
  142.2 44.3 %copy-start.3 = (f32[512,512]{1,0:T(8,128)}, f32[512,512]{1,0:T(8,128)S(1)}, u32[]{:S(2)}) copy-start(f32[512,512]{1,0:T(8,128)S(1)} %fusion.14) | copy-start | bytes 3145732
  189.2 45.9 %collective-permute-start.3 = (f32[8,256,256]{2,1,0:T(8,128)S(1)}, f32[8,256,256]{2,1,0:T(8,128)}, u32[]{:S(2)}, u32[]{:S(2)}) collective-permute-start(f32[8,256,256]{2,1,0:T(8,128)S(1)} %broadcast_select_fusion.2), channel_id=1, source_target_pairs={{0,2},{16,18},{8,10},{24,26},{4,6},{20,22},{12,14},{28,30},{1,15},... | collective-permute-start | bytes 6291464 | tf_op jit(solution)/shard_map/ppermute | solution.py:56
  235.1 61.9 %copy-start.2 = (f32[512,512]{1,0:T(8,128)S(1)}, f32[512,512]{1,0:T(8,128)}, u32[]{:S(2)}) copy-start(f32[512,512]{1,0:T(8,128)} %fusion.24) | copy-start | bytes 3145732
  237.3 66.9 %collective-permute-start.4 = (f32[8,256,256]{2,1,0:T(8,128)}, f32[8,256,256]{2,1,0:T(8,128)S(1)}, u32[]{:S(2)}, u32[]{:S(2)}) collective-permute-start(f32[8,256,256]{2,1,0:T(8,128)} %broadcast_select_fusion.3), channel_id=1, source_target_pairs={{0,1},{1,0},{2,3},{3,2},{4,5},{5,4},{6,7},{7,6},{8,9},{9,8},{10,11... | collective-permute-start | bytes 6291464 | tf_op jit(solution)/shard_map/ppermute | solution.py:60
  295.8 6.6 %copy-start.4 = (f32[1,256,2,256]{1,3,2,0:T(8,128)S(1)}, f32[1,256,2,256]{1,3,2,0:T(8,128)}, u32[]{:S(2)}) copy-start(f32[1,256,2,256]{1,3,2,0:T(8,128)} %copy.11) | copy-start | bytes 1572868
  295.8 6.6 %copy-start.6 = (f32[1,256,2,256]{1,3,2,0:T(8,128)S(1)}, f32[1,256,2,256]{1,3,2,0:T(8,128)}, u32[]{:S(2)}) copy-start(f32[1,256,2,256]{1,3,2,0:T(8,128)} %copy-done.5) | copy-start | bytes 1572868
  313.2 2.2 copy-start

commit v2 on v1

--- a/solution.py
+++ b/solution.py
@@ -12,6 +12,19 @@
     got = [x]
     for d in range(1, prows):
         got.append(lax.ppermute(x, "prow", [(0, d), (1, (1 + d) % prows)]))
+    stack = jnp.stack(got)
+    return stack[me], stack[(me + prows - 1) % prows]
+
+
+def diag_to_first_pcols(tile0, prows, pcols):
+    me = lax.axis_index("prow")
+    got = [tile0]
+    for d in range(1, prows):
+        pairs = []
+        for q in range(PANELS):
+            pairs.append((q, d * pcols + q))
+            pairs.append((pcols + q, ((1 + d) % prows) * pcols + q))
+        got.append(lax.ppermute(tile0, ("prow", "pcol"), pairs))
     stack = jnp.stack(got)
     return stack[me], stack[(me + prows - 1) % prows]
 
@@ -73,11 +86,8 @@
     nb = PANELS * tile
     tiles = covariance.reshape(rt, tile, ct, tile)
 
-    t0, t1 = prow_from_first_two(tiles[0], prows)
-
-    col0, col1 = pcol_broadcast_pair(tiles[:, :, 0, :], pcols)
-
-    diag_a, diag_b = pcol_broadcast_pair(jnp.stack([t0[:, 0, :], t1[:, 0, :]]), pcols)
+    first, second = diag_to_first_pcols(tiles[0, :, 0, :], prows, pcols)
+    diag_a, diag_b = pcol_broadcast_pair(jnp.stack([first, second]), pcols)
     block = jnp.concatenate(
         [
             jnp.concatenate([diag_a[0], diag_b[0]], axis=1),
@@ -85,6 +95,13 @@
         ],
         axis=0,
     )
+
+    cols_src = lax.optimization_barrier((tiles[0], first, second))[0]
+    t0, t1 = prow_from_first_two(cols_src, prows)
+
+    rows_src = lax.optimization_barrier((tiles[:, :, 0, :], diag_a, diag_b))[0]
+    col0, col1 = pcol_broadcast_pair(rows_src, pcols)
+
     factor = jnp.tril(jnp.linalg.cholesky(block))
     inverse = jax.scipy.linalg.solve_triangular(
         factor, jnp.eye(nb, dtype=factor.dtype), lower=True

time: 336 us -> 393 us (1.17)
  waiting for transfers between devices: 38.9 us -> 91.1 us
  starting transfers between devices: 72.2 us -> 54.8 us
  local copies, waits for them, and re-layouts: 45.4 us -> 54.9 us
  matrix products: 25.8 us -> 34.7 us
    ppermute x2, starting transfers between devices: 25.4 us -> 3.99 us  [pcol_broadcast_pair(): other = lax.ppermute(buf, 'pcol', [(i, i ^ 1) for i in range(pcols)])]
    ppermute x7, waiting for transfers between devices: 19.1 us -> 39.8 us  [prow_from_first_two(): got.append(lax.ppermute(x, 'prow', [(0, d), (1, (1 + d) % prows)]))]
    ppermute x0 -> x7, waiting for transfers between devices: none -> 16.8 us  [diag_to_first_pcols(): got.append(lax.ppermute(tile0, ('prow', 'pcol'), pairs))]
    ppermute x0 -> x7, starting transfers between devices: none -> 15.3 us  [diag_to_first_pcols(): got.append(lax.ppermute(tile0, ('prow', 'pcol'), pairs))]
    ppermute x8, waiting for transfers between devices: 19.8 us -> 34.5 us  [pcol_broadcast_pair(): got = lax.ppermute(buf, 'pcol', pairs)]
    dot_general x1, matrix products: 6.88 us -> 13.4 us  [per_device(): rows_solved = jnp.einsum('rak,bk->rab', rows_panel, inverse, precision=HI)]
    ppermute x7, starting transfers between devices: 19.8 us -> 13.6 us  [prow_from_first_two(): got.append(lax.ppermute(x, 'prow', [(0, d), (1, (1 + d) % prows)]))]
    unnamed x31 -> x39, local copies, waits for them, and re-layouts: 18.7 us -> 24.4 us
  transfers between devices with their start and end apart: 17 -> 24, of which waited for: 6 -> 9; matrix products, arithmetic and copies ran while one was open for 55% -> 46% of each run, Pallas kernels for 0% -> 0%
where the time goes in v2:
time: 393 us; the launch traced here: 386 us
  other arithmetic  147 us (37%)
  waiting for transfers between devices  91.1 us (23%)
  local copies, waits for them, and re-layouts  54.9 us (14%)
  starting transfers between devices  54.8 us (14%)
  matrix products  34.7 us (9%)
    another operation x15, other arithmetic, per_device(): factor = jnp.tril(jnp.linalg.cholesky(block))  79 us
    another operation x3, other arithmetic, per_device(): jax.scipy.linalg.solve_triangular(factor, jnp.eye(nb, dtype=factor.dtype)...  41.9 us
    ppermute x7, waiting for transfers between devices, prow_from_first_two(): got.append(lax.ppermute(x, 'prow', [(0, d), (1, (1 + d) % prows)]))  39.8 us
    ppermute x8, waiting for transfers between devices, pcol_broadcast_pair(): got = lax.ppermute(buf, 'pcol', pairs)  34.5 us
    unnamed x39, local copies, waits for them, and re-layouts  24.4 us
    ppermute x8, starting transfers between devices, pcol_broadcast_pair(): got = lax.ppermute(buf, 'pcol', pairs)  21.9 us
    ppermute x7, waiting for transfers between devices, diag_to_first_pcols(): got.append(lax.ppermute(tile0, ('prow', 'pcol'), pairs))  16.8 us
    ppermute x7, starting transfers between devices, diag_to_first_pcols(): got.append(lax.ppermute(tile0, ('prow', 'pcol'), pairs))  15.3 us
  transfers between devices with their start and end apart: 24, of which 9 were waited for; matrix products, arithmetic and copies ran while one was open for 46% of the time, Pallas kernels for 0%

profile of v2, /device:TPU:1, one launch (start us, length us, event | category | flops | bytes accessed | tf_op | source)
XLA Modules:
  0.0 386.4 jit_solution(5583906429143846139)
XLA Ops:
  0.0 7.2 %copy.10 = f32[1,8,256,1,2,256]{2,5,4,1,3,0:T(8,128)} copy(f32[1,8,256,1,2,256]{5,4,3,2,1,0:T(2,128)} %param.13) | data formatting | bytes 8388608 | tf_op args[0]
  8.2 6.2 %collective-permute-start = (f32[256,256]{0,1:T(8,128)S(1)}, f32[256,256]{0,1:T(8,128)}, u32[]{:S(2)}, u32[]{:S(2)}) collective-permute-start(f32[256,256]{0,1:T(8,128)S(1)} %slice_bitcast_fusion.8), channel_id=1, source_target_pairs={{0,32},{32,64},{1,33},{33,65}} | collective-permute-start | bytes 786440 | tf_op jit(solution)/shard_map/ppermute | solution.py:27
  23.6 8.2 %collective-permute-done.1 = f32[256,256]{0,1:T(8,128)S(1)} collective-permute-done((f32[256,256]{0,1:T(8,128)S(1)}, f32[256,256]{0,1:T(8,128)S(1)}, u32[]{:S(2)}, u32[]{:S(2)}) %collective-permute-start.1) | collective-permute-done | bytes 262176 | tf_op jit(solution)/shard_map/ppermute | solution.py:27
  31.9 1.9 collective-permute-start.6
  33.9 3.6 collective-permute-done.3
  37.6 4.9 %collective-permute-done.6 = f32[256,256]{0,1:T(8,128)S(1)} collective-permute-done((f32[256,256]{0,1:T(8,128)S(1)}, f32[256,256]{0,1:T(8,128)S(1)}, u32[]{:S(2)}, u32[]{:S(2)}) %collective-permute-start.6) | collective-permute-done | bytes 262176 | tf_op jit(solution)/shard_map/ppermute | solution.py:27
  44.7 5.4 %collective-permute-done.7 = f32[2,256,256]{1,2,0:T(8,128)S(1)} collective-permute-done((f32[2,256,256]{1,2,0:T(8,128)S(1)}, f32[2,256,256]{1,2,0:T(8,128)S(1)}, u32[]{:S(2)}, u32[]{:S(2)}) %collective-permute-start.7) | collective-permute-done | bytes 524320 | tf_op jit(solution)/shard_map/ppermute | solution.py:69
  52.7 5.4 %collective-permute-done.8 = f32[2,256,256]{1,2,0:T(8,128)S(1)} collective-permute-done((f32[2,256,256]{1,2,0:T(8,128)S(1)}, f32[2,256,256]{1,2,0:T(8,128)S(1)}, u32[]{:S(2)}, u32[]{:S(2)}) %collective-permute-start.8) | collective-permute-done | bytes 524320 | tf_op jit(solution)/shard_map/ppermute | solution.py:69
  61.5 5.4 %collective-permute-done.9 = f32[2,256,256]{1,2,0:T(8,128)S(1)} collective-permute-done((f32[2,256,256]{1,2,0:T(8,128)S(1)}, f32[2,256,256]{1,2,0:T(8,128)S(1)}, u32[]{:S(2)}, u32[]{:S(2)}) %collective-permute-start.9) | collective-permute-done | bytes 524320 | tf_op jit(solution)/shard_map/ppermute | solution.py:69
  69.6 5.4 %collective-permute-done.10 = f32[2,256,256]{1,2,0:T(8,128)S(1)} collective-permute-done((f32[2,256,256]{1,2,0:T(8,128)S(1)}, f32[2,256,256]{1,2,0:T(8,128)S(1)}, u32[]{:S(2)}, u32[]{:S(2)}) %collective-permute-start.10) | collective-permute-done | bytes 524320 | tf_op jit(solution)/shard_map/ppermute | solution.py:69
  75.7 3.8 collective-permute-start.11
  82.5 8.1 %collective-permute-start.12 = (f32[8,256,256]{1,2,0:T(8,128)S(1)}, f32[8,256,256]{1,2,0:T(8,128)S(1)}, u32[]{:S(2)}, u32[]{:S(2)}) collective-permute-start(f32[8,256,256]{1,2,0:T(8,128)S(1)} %slice_bitcast_fusion.1), channel_id=1, source_target_pairs={{0,16},{1,9},{32,48},{33,41},{64,80},{65,73},{96,112},{97,105},{12... | collective-permute-start | bytes 6291464 | tf_op jit(solution)/shard_map/ppermute | solution.py:69
  91.9 2.1 collective-permute-start.17
  94.0 2.1 collective-permute-start.18
  96.0 2.1 collective-permute-start.19
  100.5 13.0 %collective-permute-done.12 = f32[8,256,256]{1,2,0:T(8,128)S(1)} collective-permute-done((f32[8,256,256]{1,2,0:T(8,128)S(1)}, f32[8,256,256]{1,2,0:T(8,128)S(1)}, u32[]{:S(2)}, u32[]{:S(2)}) %collective-permute-start.12) | collective-permute-done | bytes 2097184 | tf_op jit(solution)/shard_map/ppermute | solution.py:69
  114.4 2.6 collective-permute-start.13
  120.4 2.0 bitcast_dynamic-update-slice_fusion.7
  123.8 2.0 bitcast_dynamic-update-slice_fusion.6
  125.8 3.4 collective-permute-start.23
  129.2 2.0 bitcast_dynamic-update-slice_fusion.5
  132.1 39.7 %collective-permute-done.21 = f32[256,2,256]{2,1,0:T(2,128)S(1)} collective-permute-done((f32[256,2,256]{2,1,0:T(2,128)S(1)}, f32[256,2,256]{2,1,0:T(2,128)S(1)}, u32[]{:S(2)}, u32[]{:S(2)}) %collective-permute-start.21) | collective-permute-done | bytes 524320 | tf_op jit(solution)/shard_map/ppermute | solution.py:14
  173.8 2.2 broadcast_select_fusion.1
  176.0 2.8 collective-permute-start.14
  183.7 11.7 %cholesky.104 = f32[128,128]{1,0:T(8,128)S(1)} custom-call(f32[128,128]{1,0:T(8,128)S(1)} %cholesky.266), custom_call_target="Cholesky" | custom-call | tf_op jit(solution)/shard_map/jit(cholesky)/cholesky | solution.py:105
  195.5 9.8 %custom-call.31 = f32[1,128,128]{1,2,0:T(8,128)S(1)} custom-call(f32[1,128,128]{2,1,0:T(8,128)S(1)} %get-tuple-element.72), custom_call_target="InvertDiagBlocksLowerTriangular" | custom-call | tf_op jit(solution)/shard_map/jit(cholesky)/cholesky | solution.py:105
  206.2 11.7 %cholesky.217 = f32[128,128]{1,0:T(8,128)S(1)} custom-call(f32[128,128]{1,0:T(8,128)S(1)} %cholesky.270), custom_call_target="Cholesky" | custom-call | tf_op jit(solution)/shard_map/jit(cholesky)/cholesky | solution.py:105
  218.0 9.8 %custom-call.32 = f32[1,128,128]{1,2,0:T(8,128)S(1)} custom-call(f32[1,128,128]{2,1,0:T(8,128)S(1)} %get-tuple-element.70), custom_call_target="InvertDiagBlocksLowerTriangular" | custom-call | tf_op jit(solution)/shard_map/jit(cholesky)/cholesky | solution.py:105
  228.0 2.6 broadcast_select_fusion.2
  230.6 3.0 collective-permute-start.15
  235.4 11.7 %cholesky.238 = f32[128,128]{1,0:T(8,128)S(1)} custom-call(f32[128,128]{1,0:T(8,128)S(1)} %cholesky.275), custom_call_target="Cholesky" | custom-call | tf_op jit(solution)/shard_map/jit(cholesky)/cholesky | solution.py:105
  247.3 9.8 %custom-call.33 = f32[1,128,128]{1,2,0:T(8,128)S(1)} custom-call(f32[1,128,128]{2,1,0:T(8,128)S(1)} %get-tuple-element.68), custom_call_target="InvertDiagBlocksLowerTriangular" | custom-call | tf_op jit(solution)/shard_map/jit(cholesky)/cholesky | solution.py:105
  258.8 11.7 %cholesky.255 = f32[128,128]{1,0:T(8,128)S(1)} custom-call(f32[128,128]{1,0:T(8,128)S(1)} %convolution_subtract_fusion.5), custom_call_target="Cholesky" | custom-call | tf_op jit(solution)/shard_map/jit(cholesky)/cholesky | solution.py:105
  277.4 2.4 broadcast_select_fusion.3
  279.9 14.0 %while.3 = (s32[]{:T(128)}, f32[512,512]{0,1:T(8,128)}, s32[4,2]{0,1:T(2,128)S(1)}, f32[4,128,128]{2,1,0:T(8,128)}, s32[]{:T(128)}) while((s32[]{:T(128)}, f32[512,512]{0,1:T(8,128)}, s32[4,2]{0,1:T(2,128)S(1)}, f32[4,128,128]{2,1,0:T(8,128)}, s32[]{:T(128)}) %tuple.43), condition=%wide.while_cond.2, body=%wide.while_body.2.sunk | while | flops 2 | bytes 393329 | solution.py:106
  280.5 2.2 dynamic-slice.24
  284.0 2.2 dynamic-slice.24
  287.5 2.2 dynamic-slice.24
  291.0 2.1 dynamic-slice.24
  293.9 40.3 %custom-call.34 = f32[4,128,128]{1,2,0:T(8,128)S(1)} custom-call(f32[4,128,128]{2,1,0:T(8,128)} %get-tuple-element.38), custom_call_target="InvertDiagBlocksLowerTriangular" | custom-call | tf_op jit(solution)/shard_map/jit(_solve_triangular)/triangular_solve | solution.py:106
  340.9 3.5 convolution_bitcast_fusion
  344.4 2.7 broadcast_select_fusion.5
  347.1 13.4 %fusion = f32[8,256,512]{2,1,0:T(8,128)S(1)} fusion(f32[8,256,256]{1,2,0:T(8,128)S(1)} %get-tuple-element.56, f32[8,256,256]{1,2,0:T(8,128)S(1)} %get-tuple-element.55, f32[128,512]{1,0:T(8,128)S(1)} %fusion.36, f32[128,512]{1,0:T(8,128)S(1)} %fusion.37, f32[128,512]{1,0:T(8,128)S(1)} %fusion.39, f32[128,512]{1,0:T(8,128)S(1)} %fusion.27), kind=kOutput, calls=%fused_computation.2 | convolution fusion | flops 6444285952 | bytes 9437184 | tf_op jit(solution)/shard_map/rak,bk->rab/dot_general | solution.py:114
  360.5 7.2 %subtract_select_fusion = f32[8,256,2,256]{1,3,2,0:T(8,128)S(1)} fusion(f32[2,256,512,1]{2,1,0,3:T(8,128)S(1)} %convolution_bitcast_fusion, f32[8,256,512]{2,1,0:T(8,128)S(1)} %fusion, pred[8,2]{1,0:T(8,128)(4,1)S(1)} %broadcast_and_fusion, f32[1,8,256,1,2,256]{2,5,4,1,3,0:T(8,128)S(1)} %copy-done), kind=kOutput, calls=%fused_computation.8 | convolution fusion | flops 6444548096 | bytes 13631504 | tf_op jit(solution)/shard_map/rak,cbk->racb/dot_general | solution.py:116
  367.7 2.0 copy.65
  372.6 1.9 copy.32
  375.5 3.2 fusion.10
  378.7 7.2 %copy.24 = f32[1,8,256,1,2,256]{5,4,3,2,1,0:T(2,128)} copy(f32[1,8,256,1,2,256]{2,5,4,1,3,0:T(8,128)} %fusion.10) | data formatting | bytes 8388608 | tf_op jit(solution)/shard_map/scatter | solution.py:130
  (145 shorter events, 66.6 us)
Async XLA Ops:
  8.2 13.1 %collective-permute-start = (f32[256,256]{0,1:T(8,128)S(1)}, f32[256,256]{0,1:T(8,128)}, u32[]{:S(2)}, u32[]{:S(2)}) collective-permute-start(f32[256,256]{0,1:T(8,128)S(1)} %slice_bitcast_fusion.8), channel_id=1, source_target_pairs={{0,32},{32,64},{1,33},{33,65}} | collective-permute-start | bytes 786440 | tf_op jit(solution)/shard_map/ppermute | solution.py:27
  14.4 17.5 %collective-permute-start.1 = (f32[256,256]{0,1:T(8,128)S(1)}, f32[256,256]{0,1:T(8,128)S(1)}, u32[]{:S(2)}, u32[]{:S(2)}) collective-permute-start(f32[256,256]{0,1:T(8,128)S(1)} %slice_bitcast_fusion.8), channel_id=1, source_target_pairs={{0,64},{32,96},{1,65},{33,97}} | collective-permute-start | bytes 786440 | tf_op jit(solution)/shard_map/ppermute | solution.py:27
  15.7 18.1 %collective-permute-start.2 = (f32[256,256]{0,1:T(8,128)S(1)}, f32[256,256]{0,1:T(8,128)S(1)}, u32[]{:S(2)}, u32[]{:S(2)}) collective-permute-start(f32[256,256]{0,1:T(8,128)S(1)} %slice_bitcast_fusion.8), channel_id=1, source_target_pairs={{0,96},{32,128},{1,97},{33,129}} | collective-permute-start | bytes 786440 | tf_op jit(solution)/shard_map/ppermute | solution.py:27
  17.4 20.1 %collective-permute-start.3 = (f32[256,256]{0,1:T(8,128)S(1)}, f32[256,256]{0,1:T(8,128)S(1)}, u32[]{:S(2)}, u32[]{:S(2)}) collective-permute-start(f32[256,256]{0,1:T(8,128)S(1)} %slice_bitcast_fusion.8), channel_id=1, source_target_pairs={{0,128},{32,160},{1,129},{33,161}} | collective-permute-start | bytes 786440 | tf_op jit(solution)/shard_map/ppermute | solution.py:27
  18.7 18.8 %collective-permute-start.4 = (f32[256,256]{0,1:T(8,128)S(1)}, f32[256,256]{0,1:T(8,128)S(1)}, u32[]{:S(2)}, u32[]{:S(2)}) collective-permute-start(f32[256,256]{0,1:T(8,128)S(1)} %slice_bitcast_fusion.8), channel_id=1, source_target_pairs={{0,160},{32,192},{1,161},{33,193}} | collective-permute-start | bytes 786440 | tf_op jit(solution)/shard_map/ppermute | solution.py:27
  21.3 16.2 %collective-permute-start.5 = (f32[256,256]{0,1:T(8,128)S(1)}, f32[256,256]{0,1:T(8,128)S(1)}, u32[]{:S(2)}, u32[]{:S(2)}) collective-permute-start(f32[256,256]{0,1:T(8,128)S(1)} %slice_bitcast_fusion.8), channel_id=1, source_target_pairs={{0,192},{32,224},{1,193},{33,225}} | collective-permute-start | bytes 786440 | tf_op jit(solution)/shard_map/ppermute | solution.py:27
  31.9 10.7 %collective-permute-start.6 = (f32[256,256]{0,1:T(8,128)S(1)}, f32[256,256]{0,1:T(8,128)S(1)}, u32[]{:S(2)}, u32[]{:S(2)}) collective-permute-start(f32[256,256]{0,1:T(8,128)S(1)} %slice_bitcast_fusion.8), channel_id=1, source_target_pairs={{0,224},{32,0},{1,225},{33,1}} | collective-permute-start | bytes 786440 | tf_op jit(solution)/shard_map/ppermute | solution.py:27
  33.9 10.2 %copy-start.10 = (s32[2]{0:T(128)S(1)}, s32[2]{0:T(128)}, u32[]{:S(2)}) copy-start(s32[2]{0:T(128)} %constant.274.clone) | copy-start | bytes 28
  37.6 14.5 %copy-start.9 = (s32[4]{0:T(128)S(1)}, s32[4]{0:T(128)}, u32[]{:S(2)}) copy-start(s32[4]{0:T(128)} %constant.275.clone) | copy-start | bytes 52
  42.7 18.2 %copy-start.8 = (s32[8]{0:T(128)S(1)}, s32[8]{0:T(128)}, u32[]{:S(2)}) copy-start(s32[8]{0:T(128)} %constant.276.clone) | copy-start | bytes 100
  42.7 7.4 %collective-permute-start.7 = (f32[2,256,256]{1,2,0:T(8,128)S(1)}, f32[2,256,256]{1,2,0:T(8,128)S(1)}, u32[]{:S(2)}, u32[]{:S(2)}) collective-permute-start(f32[2,256,256]{1,2,0:T(8,128)S(1)} %pad_maximum_fusion.1), channel_id=1, source_target_pairs={{0,16},{1,9},{32,48},{33,41},{64,80},{65,73},{96,112},{97,105},{12... | collective-permute-start | bytes 1572872 | tf_op jit(solution)/shard_map/ppermute | solution.py:69
  50.8 18.1 %copy-start.7 = (s32[16]{0:T(128)S(1)}, s32[16]{0:T(128)}, u32[]{:S(2)}) copy-start(s32[16]{0:T(128)} %constant.277.clone) | copy-start | bytes 196
  50.8 7.4 %collective-permute-start.8 = (f32[2,256,256]{1,2,0:T(8,128)S(1)}, f32[2,256,256]{1,2,0:T(8,128)S(1)}, u32[]{:S(2)}, u32[]{:S(2)}) collective-permute-start(f32[2,256,256]{1,2,0:T(8,128)S(1)} %broadcast_select_fusion.6), channel_id=1, source_target_pairs={{0,8},{16,24},{1,17},{9,25},{32,40},{48,56},{33,49},{41,57},{64,72... | collective-permute-start | bytes 1572872 | tf_op jit(solution)/shard_map/ppermute | solution.py:69
  59.5 7.4 %collective-permute-start.9 = (f32[2,256,256]{1,2,0:T(8,128)S(1)}, f32[2,256,256]{1,2,0:T(8,128)S(1)}, u32[]{:S(2)}, u32[]{:S(2)}) collective-permute-start(f32[2,256,256]{1,2,0:T(8,128)S(1)} %broadcast_select_fusion.7), channel_id=1, source_target_pairs={{0,4},{16,20},{8,12},{24,28},{1,13},{9,5},{17,29},{25,21},{32,36},... | collective-permute-start | bytes 1572872 | tf_op jit(solution)/shard_map/ppermute | solution.py:69
  67.6 7.4 %collective-permute-start.10 = (f32[2,256,256]{1,2,0:T(8,128)S(1)}, f32[2,256,256]{1,2,0:T(8,128)S(1)}, u32[]{:S(2)}, u32[]{:S(2)}) collective-permute-start(f32[2,256,256]{1,2,0:T(8,128)S(1)} %broadcast_select_fusion.8), channel_id=1, source_target_pairs={{0,2},{16,18},{8,10},{24,26},{4,6},{20,22},{12,14},{28,30},{1,15},... | collective-permute-start | bytes 1572872 | tf_op jit(solution)/shard_map/ppermute | solution.py:69
  75.7 5.6 %collective-permute-start.11 = (f32[2,256,256]{1,2,0:T(8,128)S(1)}, f32[2,256,256]{1,2,0:T(8,128)S(1)}, u32[]{:S(2)}, u32[]{:S(2)}) collective-permute-start(f32[2,256,256]{1,2,0:T(8,128)S(1)} %broadcast_select_fusion.9), channel_id=1, source_target_pairs={{0,1},{1,0},{2,3},{3,2},{4,5},{5,4},{6,7},{7,6},{8,9},{9,8},{10,11... | collective-permute-start | bytes 1572872 | tf_op jit(solution)/shard_map/ppermute | solution.py:73
  82.5 31.0 %collective-permute-start.12 = (f32[8,256,256]{1,2,0:T(8,128)S(1)}, f32[8,256,256]{1,2,0:T(8,128)S(1)}, u32[]{:S(2)}, u32[]{:S(2)}) collective-permute-start(f32[8,256,256]{1,2,0:T(8,128)S(1)} %slice_bitcast_fusion.1), channel_id=1, source_target_pairs={{0,16},{1,9},{32,48},{33,41},{64,80},{65,73},{96,112},{97,105},{12... | collective-permute-start | bytes 6291464 | tf_op jit(solution)/shard_map/ppermute | solution.py:69
  91.9 27.2 %collective-permute-start.17 = (f32[256,2,256]{2,1,0:T(2,128)S(1)}, f32[256,2,256]{2,1,0:T(2,128)}, u32[]{:S(2)}, u32[]{:S(2)}) collective-permute-start(f32[256,2,256]{2,1,0:T(2,128)S(1)} %slice_bitcast_fusion.2), channel_id=1, source_target_pairs={{0,32},{32,64},{1,33},{33,65},{2,34},{34,66},{3,35},{35,67},{4,36}... | collective-permute-start | bytes 1572872 | tf_op jit(solution)/shard_map/ppermute | solution.py:14
  94.0 28.5 %collective-permute-start.18 = (f32[256,2,256]{2,1,0:T(2,128)S(1)}, f32[256,2,256]{2,1,0:T(2,128)}, u32[]{:S(2)}, u32[]{:S(2)}) collective-permute-start(f32[256,2,256]{2,1,0:T(2,128)S(1)} %slice_bitcast_fusion.2), channel_id=1, source_target_pairs={{0,64},{32,96},{1,65},{33,97},{2,66},{34,98},{3,67},{35,99},{4,68}... | collective-permute-start | bytes 1572872 | tf_op jit(solution)/shard_map/ppermute | solution.py:14
  96.0 29.7 %collective-permute-start.19 = (f32[256,2,256]{2,1,0:T(2,128)S(1)}, f32[256,2,256]{2,1,0:T(2,128)}, u32[]{:S(2)}, u32[]{:S(2)}) collective-permute-start(f32[256,2,256]{2,1,0:T(2,128)S(1)} %slice_bitcast_fusion.2), channel_id=1, source_target_pairs={{0,96},{32,128},{1,97},{33,129},{2,98},{34,130},{3,99},{35,131},{4... | collective-permute-start | bytes 1572872 | tf_op jit(solution)/shard_map/ppermute | solution.py:14
  98.1 33.0 %collective-permute-start.20 = (f32[256,2,256]{2,1,0:T(2,128)S(1)}, f32[256,2,256]{2,1,0:T(2,128)S(1)}, u32[]{:S(2)}, u32[]{:S(2)}) collective-permute-start(f32[256,2,256]{2,1,0:T(2,128)S(1)} %slice_bitcast_fusion.2), channel_id=1, source_target_pairs={{0,128},{32,160},{1,129},{33,161},{2,130},{34,162},{3,131},{35,163... | collective-permute-start | bytes 1572872 | tf_op jit(solution)/shard_map/ppermute | solution.py:14
  114.4 59.4 %collective-permute-start.13 = (f32[8,256,256]{1,2,0:T(8,128)S(1)}, f32[8,256,256]{1,2,0:T(8,128)}, u32[]{:S(2)}, u32[]{:S(2)}) collective-permute-start(f32[8,256,256]{1,2,0:T(8,128)S(1)} %broadcast_select_fusion), channel_id=1, source_target_pairs={{0,8},{16,24},{1,17},{9,25},{32,40},{48,56},{33,49},{41,57},{64,72... | collective-permute-start | bytes 6291464 | tf_op jit(solution)/shard_map/ppermute | solution.py:69
  119.1 52.8 %collective-permute-start.21 = (f32[256,2,256]{2,1,0:T(2,128)S(1)}, f32[256,2,256]{2,1,0:T(2,128)S(1)}, u32[]{:S(2)}, u32[]{:S(2)}) collective-permute-start(f32[256,2,256]{2,1,0:T(2,128)S(1)} %slice_bitcast_fusion.2), channel_id=1, source_target_pairs={{0,160},{32,192},{1,161},{33,193},{2,162},{34,194},{3,163},{35,195... | collective-permute-start | bytes 1572872 | tf_op jit(solution)/shard_map/ppermute | solution.py:14
  122.4 50.4 %collective-permute-start.22 = (f32[256,2,256]{2,1,0:T(2,128)S(1)}, f32[256,2,256]{2,1,0:T(2,128)S(1)}, u32[]{:S(2)}, u32[]{:S(2)}) collective-permute-start(f32[256,2,256]{2,1,0:T(2,128)S(1)} %slice_bitcast_fusion.2), channel_id=1, source_target_pairs={{0,192},{32,224},{1,193},{33,225},{2,194},{34,226},{3,195},{35,227... | collective-permute-start | bytes 1572872 | tf_op jit(solution)/shard_map/ppermute | solution.py:14
  125.8 53.1 %collective-permute-start.23 = (f32[256,2,256]{2,1,0:T(2,128)S(1)}, f32[256,2,256]{2,1,0:T(2,128)S(1)}, u32[]{:S(2)}, u32[]{:S(2)}) collective-permute-start(f32[256,2,256]{2,1,0:T(2,128)S(1)} %slice_bitcast_fusion.2), channel_id=1, source_target_pairs={{0,224},{32,0},{1,225},{33,1},{2,226},{34,2},{3,227},{35,3},{4,228... | collective-permute-start | bytes 1572872 | tf_op jit(solution)/shard_map/ppermute | solution.py:14
  176.0 52.0 %collective-permute-start.14 = (f32[8,256,256]{1,2,0:T(8,128)}, f32[8,256,256]{1,2,0:T(8,128)}, u32[]{:S(2)}, u32[]{:S(2)}) collective-permute-start(f32[8,256,256]{1,2,0:T(8,128)} %broadcast_select_fusion.1), channel_id=1, source_target_pairs={{0,4},{16,20},{8,12},{24,28},{1,13},{9,5},{17,29},{25,21},{32,36},... | collective-permute-start | bytes 6291464 | tf_op jit(solution)/shard_map/ppermute | solution.py:69
  179.8 3.1 copy-start.5
  179.8 3.1 copy-start.6
  183.7 44.3 %copy-start.4 = (f32[512,512]{1,0:T(8,128)}, f32[512,512]{1,0:T(8,128)S(1)}, u32[]{:S(2)}) copy-start(f32[512,512]{1,0:T(8,128)S(1)} %fusion.11) | copy-start | bytes 3145732
  230.6 46.8 %collective-permute-start.15 = (f32[8,256,256]{1,2,0:T(8,128)S(1)}, f32[8,256,256]{1,2,0:T(8,128)}, u32[]{:S(2)}, u32[]{:S(2)}) collective-permute-start(f32[8,256,256]{1,2,0:T(8,128)S(1)} %broadcast_select_fusion.2), channel_id=1, source_target_pairs={{0,2},{16,18},{8,10},{24,26},{4,6},{20,22},{12,14},{28,30},{1,15},... | collective-permute-start | bytes 6291464 | tf_op jit(solution)/shard_map/ppermute | solution.py:69
  277.4 58.0 %copy-start.3 = (f32[512,512]{1,0:T(8,128)S(1)}, f32[512,512]{1,0:T(8,128)}, u32[]{:S(2)}) copy-start(f32[512,512]{1,0:T(8,128)} %fusion.22) | copy-start | bytes 3145732
  279.7 64.6 %collective-permute-start.16 = (f32[8,256,256]{1,2,0:T(8,128)}, f32[8,256,256]{1,2,0:T(8,128)}, u32[]{:S(2)}, u32[]{:S(2)}) collective-permute-start(f32[8,256,256]{1,2,0:T(8,128)} %broadcast_select_fusion.3), channel_id=1, source_target_pairs={{0,1},{1,0},{2,3},{3,2},{4,5},{5,4},{6,7},{7,6},{8,9},{9,8},{10,11... | collective-permute-start | bytes 6291464 | tf_op jit(solution)/shard_map/ppermute | solution.py:73
  336.6 4.3 %copy-start.2 = (f32[2,256,512]{1,0,2:T(2,128)S(1)}, f32[2,256,512]{1,0,2:T(2,128)}, u32[]{:S(2)}) copy-start(f32[2,256,512]{1,0,2:T(2,128)} %pad_maximum_fusion) | copy-start | bytes 3145732
  347.1 13.5 %copy-start = (f32[1,8,256,1,2,256]{2,5,4,1,3,0:T(8,128)S(1)}, f32[1,8,256,1,2,256]{2,5,4,1,3,0:T(8,128)}, u32[]{:S(2)}) copy-start(f32[1,8,256,1,2,256]{2,5,4,1,3,0:T(8,128)} %copy.10) | copy-start | bytes 12582916
  367.7 3.3 copy-start.1

commit v3 on v2

--- a/solution.py
+++ b/solution.py
@@ -96,13 +96,14 @@
         axis=0,
     )
 
-    cols_src = lax.optimization_barrier((tiles[0], first, second))[0]
-    t0, t1 = prow_from_first_two(cols_src, prows)
-
     rows_src = lax.optimization_barrier((tiles[:, :, 0, :], diag_a, diag_b))[0]
     col0, col1 = pcol_broadcast_pair(rows_src, pcols)
 
     factor = jnp.tril(jnp.linalg.cholesky(block))
+
+    cols_src = lax.optimization_barrier((tiles[0], factor))[0]
+    t0, t1 = prow_from_first_two(cols_src, prows)
+
     inverse = jax.scipy.linalg.solve_triangular(
         factor, jnp.eye(nb, dtype=factor.dtype), lower=True
     )

time: 393 us -> 376 us (0.957)
  the two profiles are of different devices: /device:TPU:1 before, /device:TPU:28 now
where the time goes in v3:
time: 376 us; the launch traced here: 371 us
  other arithmetic  145 us (39%)
  waiting for transfers between devices  89.5 us (24%)
  local copies, waits for them, and re-layouts  57.9 us (15%)
  starting transfers between devices  37.8 us (10%)
  matrix products  36.6 us (10%)
  between operations  3.97 us (1%)
    another operation x15, other arithmetic, per_device(): factor = jnp.tril(jnp.linalg.cholesky(block))  80.2 us
    ppermute x8, waiting for transfers between devices, pcol_broadcast_pair(): got = lax.ppermute(buf, 'pcol', pairs)  45.5 us
    another operation x3, other arithmetic, per_device(): jax.scipy.linalg.solve_triangular(factor, jnp.eye(nb, dtype=factor.dtype)...  41.7 us
    unnamed x41, local copies, waits for them, and re-layouts  23 us
    ppermute x7, waiting for transfers between devices, diag_to_first_pcols(): got.append(lax.ppermute(tile0, ('prow', 'pcol'), pairs))  22.4 us
    ppermute x7, waiting for transfers between devices, prow_from_first_two(): got.append(lax.ppermute(x, 'prow', [(0, d), (1, (1 + d) % prows)]))  21.6 us
    ppermute x8, starting transfers between devices, pcol_broadcast_pair(): got = lax.ppermute(buf, 'pcol', pairs)  17.9 us
    another operation x20, local copies, waits for them, and re-layouts  14.3 us
  transfers between devices with their start and end apart: 24, of which 9 were waited for; matrix products, arithmetic and copies ran while one was open for 49% of the time, Pallas kernels for 0%

profile of v3, /device:TPU:28, one launch (start us, length us, event | category | flops | bytes accessed | tf_op | source)
XLA Modules:
  0.0 370.6 jit_solution(229162005276659727)
XLA Ops:
  0.0 7.2 %copy.10 = f32[1,8,256,1,2,256]{2,5,4,1,3,0:T(8,128)} copy(f32[1,8,256,1,2,256]{5,4,3,2,1,0:T(2,128)} %param.13) | data formatting | bytes 8388608 | tf_op args[0]
  17.0 9.7 %collective-permute-done.5 = f32[256,256]{0,1:T(8,128)S(1)} collective-permute-done((f32[256,256]{0,1:T(8,128)S(1)}, f32[256,256]{0,1:T(8,128)S(1)}, u32[]{:S(2)}, u32[]{:S(2)}) %collective-permute-start.5) | collective-permute-done | bytes 262176 | tf_op jit(solution)/shard_map/ppermute | solution.py:27
  26.7 12.7 %collective-permute-done.6 = f32[256,256]{0,1:T(8,128)S(1)} collective-permute-done((f32[256,256]{0,1:T(8,128)S(1)}, f32[256,256]{0,1:T(8,128)S(1)}, u32[]{:S(2)}, u32[]{:S(2)}) %collective-permute-start.6) | collective-permute-done | bytes 262176 | tf_op jit(solution)/shard_map/ppermute | solution.py:27
  41.5 6.0 %collective-permute-done.7 = f32[2,256,256]{1,2,0:T(8,128)S(1)} collective-permute-done((f32[2,256,256]{1,2,0:T(8,128)S(1)}, f32[2,256,256]{1,2,0:T(8,128)S(1)}, u32[]{:S(2)}, u32[]{:S(2)}) %collective-permute-start.7) | collective-permute-done | bytes 524320 | tf_op jit(solution)/shard_map/ppermute | solution.py:69
  50.2 5.9 %collective-permute-done.8 = f32[2,256,256]{1,2,0:T(8,128)S(1)} collective-permute-done((f32[2,256,256]{1,2,0:T(8,128)S(1)}, f32[2,256,256]{1,2,0:T(8,128)S(1)}, u32[]{:S(2)}, u32[]{:S(2)}) %collective-permute-start.8) | collective-permute-done | bytes 524320 | tf_op jit(solution)/shard_map/ppermute | solution.py:69
  59.4 6.0 %collective-permute-done.9 = f32[2,256,256]{1,2,0:T(8,128)S(1)} collective-permute-done((f32[2,256,256]{1,2,0:T(8,128)S(1)}, f32[2,256,256]{1,2,0:T(8,128)S(1)}, u32[]{:S(2)}, u32[]{:S(2)}) %collective-permute-start.9) | collective-permute-done | bytes 524320 | tf_op jit(solution)/shard_map/ppermute | solution.py:69
  68.0 6.0 %collective-permute-done.10 = f32[2,256,256]{1,2,0:T(8,128)S(1)} collective-permute-done((f32[2,256,256]{1,2,0:T(8,128)S(1)}, f32[2,256,256]{1,2,0:T(8,128)S(1)}, u32[]{:S(2)}, u32[]{:S(2)}) %collective-permute-start.10) | collective-permute-done | bytes 524320 | tf_op jit(solution)/shard_map/ppermute | solution.py:69
  74.8 1.8 slice_bitcast_fusion.1
  77.8 4.5 %collective-permute-start.12 = (f32[8,256,256]{1,2,0:T(8,128)S(1)}, f32[8,256,256]{1,2,0:T(8,128)S(1)}, u32[]{:S(2)}, u32[]{:S(2)}) collective-permute-start(f32[8,256,256]{1,2,0:T(8,128)S(1)} %slice_bitcast_fusion.1), channel_id=1, source_target_pairs={{0,16},{1,9},{32,48},{33,41},{64,80},{65,73},{96,112},{97,105},{12... | collective-permute-start | bytes 6291464 | tf_op jit(solution)/shard_map/ppermute | solution.py:69
  84.2 21.5 %collective-permute-done.12 = f32[8,256,256]{1,2,0:T(8,128)S(1)} collective-permute-done((f32[8,256,256]{1,2,0:T(8,128)S(1)}, f32[8,256,256]{1,2,0:T(8,128)S(1)}, u32[]{:S(2)}, u32[]{:S(2)}) %collective-permute-start.12) | collective-permute-done | bytes 2097184 | tf_op jit(solution)/shard_map/ppermute | solution.py:69
  106.6 2.8 collective-permute-start.13
  109.5 2.0 slice_bitcast_fusion.2
  114.8 1.6 copy.11
  118.7 11.7 %cholesky.104 = f32[128,128]{1,0:T(8,128)S(1)} custom-call(f32[128,128]{1,0:T(8,128)S(1)} %cholesky.266), custom_call_target="Cholesky" | custom-call | tf_op jit(solution)/shard_map/jit(cholesky)/cholesky | solution.py:102
  131.2 9.8 %custom-call.31 = f32[1,128,128]{1,2,0:T(8,128)S(1)} custom-call(f32[1,128,128]{2,1,0:T(8,128)S(1)} %get-tuple-element.74), custom_call_target="InvertDiagBlocksLowerTriangular" | custom-call | tf_op jit(solution)/shard_map/jit(cholesky)/cholesky | solution.py:102
  143.7 11.7 %cholesky.217 = f32[128,128]{1,0:T(8,128)S(1)} custom-call(f32[128,128]{1,0:T(8,128)S(1)} %cholesky.270), custom_call_target="Cholesky" | custom-call | tf_op jit(solution)/shard_map/jit(cholesky)/cholesky | solution.py:102
  156.1 10.8 %custom-call.32 = f32[1,128,128]{1,2,0:T(8,128)} custom-call(f32[1,128,128]{2,1,0:T(8,128)S(1)} %get-tuple-element.72), custom_call_target="InvertDiagBlocksLowerTriangular" | custom-call | tf_op jit(solution)/shard_map/jit(cholesky)/cholesky | solution.py:102
  168.8 2.3 broadcast_select_fusion.1
  171.1 2.6 collective-permute-start.14
  174.0 1.5 convolution_subtract_fusion.4
  175.5 11.7 %cholesky.238 = f32[128,128]{1,0:T(8,128)S(1)} custom-call(f32[128,128]{1,0:T(8,128)S(1)} %cholesky.275), custom_call_target="Cholesky" | custom-call | tf_op jit(solution)/shard_map/jit(cholesky)/cholesky | solution.py:102
  187.4 9.8 %custom-call.33 = f32[1,128,128]{1,2,0:T(8,128)S(1)} custom-call(f32[1,128,128]{2,1,0:T(8,128)S(1)} %get-tuple-element.70), custom_call_target="InvertDiagBlocksLowerTriangular" | custom-call | tf_op jit(solution)/shard_map/jit(cholesky)/cholesky | solution.py:102
  198.9 11.7 %cholesky.255 = f32[128,128]{1,0:T(8,128)S(1)} custom-call(f32[128,128]{1,0:T(8,128)S(1)} %convolution_subtract_fusion.5), custom_call_target="Cholesky" | custom-call | tf_op jit(solution)/shard_map/jit(cholesky)/cholesky | solution.py:102
  216.0 1.6 fusion.13
  217.6 1.5 collective-permute-start.17
  219.1 1.5 collective-permute-start.18
  220.6 1.5 collective-permute-start.19
  222.1 1.6 collective-permute-start.20
  223.8 2.6 broadcast_select_fusion.2
  226.4 2.6 collective-permute-start.15
  229.0 14.4 %while.3 = (s32[]{:T(128)}, f32[512,512]{0,1:T(8,128)}, s32[4,2]{0,1:T(2,128)S(1)}, f32[4,128,128]{2,1,0:T(8,128)}, s32[]{:T(128)}) while((s32[]{:T(128)}, f32[512,512]{0,1:T(8,128)}, s32[4,2]{0,1:T(2,128)S(1)}, f32[4,128,128]{2,1,0:T(8,128)}, s32[]{:T(128)}) %tuple.44), condition=%wide.while_cond.2, body=%wide.while_body.2.sunk | while | flops 2 | bytes 393329 | solution.py:107
  229.6 2.2 dynamic-slice.24
  233.3 2.2 dynamic-slice.24
  236.9 2.2 dynamic-slice.24
  240.5 2.2 dynamic-slice.24
  243.4 40.1 %custom-call.34 = f32[4,128,128]{1,2,0:T(8,128)S(1)} custom-call(f32[4,128,128]{2,1,0:T(8,128)} %get-tuple-element.40), custom_call_target="InvertDiagBlocksLowerTriangular" | custom-call | tf_op jit(solution)/shard_map/jit(_solve_triangular)/triangular_solve | solution.py:107
  288.1 1.6 convolution_subtract_fusion.2
  292.9 3.6 collective-permute-start.16
  300.3 1.5 collective-permute-start.23
  304.6 21.5 %collective-permute-done.22 = f32[256,2,256]{2,1,0:T(2,128)S(1)} collective-permute-done((f32[256,2,256]{2,1,0:T(2,128)}, f32[256,2,256]{2,1,0:T(2,128)S(1)}, u32[]{:S(2)}, u32[]{:S(2)}) %collective-permute-start.22) | collective-permute-done | bytes 524320 | tf_op jit(solution)/shard_map/ppermute | solution.py:14
  327.4 3.5 convolution_bitcast_fusion
  331.3 13.4 %fusion = f32[8,256,512]{2,1,0:T(8,128)S(1)} fusion(f32[8,256,256]{1,2,0:T(8,128)S(1)} %get-tuple-element.58, f32[8,256,256]{1,2,0:T(8,128)S(1)} %get-tuple-element.57, f32[128,512]{1,0:T(8,128)S(1)} %fusion.36, f32[128,512]{1,0:T(8,128)S(1)} %fusion.37, f32[128,512]{1,0:T(8,128)S(1)} %fusion.39, f32[128,512]{1,0:T(8,128)S(1)} %fusion.27), kind=kOutput, calls=%fused_computation.2 | convolution fusion | flops 6444285952 | bytes 9437184 | tf_op jit(solution)/shard_map/rak,bk->rab/dot_general | solution.py:115
  344.8 7.2 %subtract_select_fusion = f32[8,256,2,256]{1,3,2,0:T(8,128)S(1)} fusion(f32[2,256,512,1]{2,1,0,3:T(8,128)S(1)} %convolution_bitcast_fusion, f32[8,256,512]{2,1,0:T(8,128)S(1)} %fusion, pred[8,2]{1,0:T(8,128)(4,1)S(1)} %broadcast_and_fusion, f32[1,8,256,1,2,256]{2,5,4,1,3,0:T(8,128)S(1)} %copy-done), kind=kOutput, calls=%fused_computation.8 | convolution fusion | flops 6444548096 | bytes 13631504 | tf_op jit(solution)/shard_map/rak,cbk->racb/dot_general | solution.py:117
  352.0 2.0 copy.65
  355.2 1.6 constant_dynamic-slice_fusion.1
  356.8 1.9 copy.32
  359.8 3.1 fusion.10
  362.9 7.2 %copy.24 = f32[1,8,256,1,2,256]{5,4,3,2,1,0:T(2,128)} copy(f32[1,8,256,1,2,256]{2,5,4,1,3,0:T(8,128)} %fusion.10) | data formatting | bytes 8388608 | tf_op jit(solution)/shard_map/scatter | solution.py:131
  (147 shorter events, 65.2 us)
Async XLA Ops:
  8.2 5.1 %collective-permute-start = (f32[256,256]{0,1:T(8,128)S(1)}, f32[256,256]{0,1:T(8,128)}, u32[]{:S(2)}, u32[]{:S(2)}) collective-permute-start(f32[256,256]{0,1:T(8,128)S(1)} %slice_bitcast_fusion.8), channel_id=1, source_target_pairs={{0,32},{32,64},{1,33},{33,65}} | collective-permute-start | bytes 786440 | tf_op jit(solution)/shard_map/ppermute | solution.py:27
  9.5 6.0 %collective-permute-start.1 = (f32[256,256]{0,1:T(8,128)S(1)}, f32[256,256]{0,1:T(8,128)S(1)}, u32[]{:S(2)}, u32[]{:S(2)}) collective-permute-start(f32[256,256]{0,1:T(8,128)S(1)} %slice_bitcast_fusion.8), channel_id=1, source_target_pairs={{0,64},{32,96},{1,65},{33,97}} | collective-permute-start | bytes 786440 | tf_op jit(solution)/shard_map/ppermute | solution.py:27
  10.2 6.7 %collective-permute-start.2 = (f32[256,256]{0,1:T(8,128)S(1)}, f32[256,256]{0,1:T(8,128)S(1)}, u32[]{:S(2)}, u32[]{:S(2)}) collective-permute-start(f32[256,256]{0,1:T(8,128)S(1)} %slice_bitcast_fusion.8), channel_id=1, source_target_pairs={{0,96},{32,128},{1,97},{33,129}} | collective-permute-start | bytes 786440 | tf_op jit(solution)/shard_map/ppermute | solution.py:27
  10.9 6.0 %collective-permute-start.3 = (f32[256,256]{0,1:T(8,128)S(1)}, f32[256,256]{0,1:T(8,128)S(1)}, u32[]{:S(2)}, u32[]{:S(2)}) collective-permute-start(f32[256,256]{0,1:T(8,128)S(1)} %slice_bitcast_fusion.8), channel_id=1, source_target_pairs={{0,128},{32,160},{1,129},{33,161}} | collective-permute-start | bytes 786440 | tf_op jit(solution)/shard_map/ppermute | solution.py:27
  11.6 5.4 %collective-permute-start.4 = (f32[256,256]{0,1:T(8,128)S(1)}, f32[256,256]{0,1:T(8,128)S(1)}, u32[]{:S(2)}, u32[]{:S(2)}) collective-permute-start(f32[256,256]{0,1:T(8,128)S(1)} %slice_bitcast_fusion.8), channel_id=1, source_target_pairs={{0,160},{32,192},{1,161},{33,193}} | collective-permute-start | bytes 786440 | tf_op jit(solution)/shard_map/ppermute | solution.py:27
  13.3 13.4 %collective-permute-start.5 = (f32[256,256]{0,1:T(8,128)S(1)}, f32[256,256]{0,1:T(8,128)S(1)}, u32[]{:S(2)}, u32[]{:S(2)}) collective-permute-start(f32[256,256]{0,1:T(8,128)S(1)} %slice_bitcast_fusion.8), channel_id=1, source_target_pairs={{0,192},{32,224},{1,193},{33,225}} | collective-permute-start | bytes 786440 | tf_op jit(solution)/shard_map/ppermute | solution.py:27
  15.5 23.8 %collective-permute-start.6 = (f32[256,256]{0,1:T(8,128)S(1)}, f32[256,256]{0,1:T(8,128)S(1)}, u32[]{:S(2)}, u32[]{:S(2)}) collective-permute-start(f32[256,256]{0,1:T(8,128)S(1)} %slice_bitcast_fusion.8), channel_id=1, source_target_pairs={{0,224},{32,0},{1,225},{33,1}} | collective-permute-start | bytes 786440 | tf_op jit(solution)/shard_map/ppermute | solution.py:27
  16.9 23.9 %copy-start.11 = (s32[2]{0:T(128)S(1)}, s32[2]{0:T(128)}, u32[]{:S(2)}) copy-start(s32[2]{0:T(128)} %constant.274.clone) | copy-start | bytes 28
  26.7 22.8 %copy-start.10 = (s32[4]{0:T(128)S(1)}, s32[4]{0:T(128)}, u32[]{:S(2)}) copy-start(s32[4]{0:T(128)} %constant.275.clone) | copy-start | bytes 52
  39.5 19.3 %copy-start.9 = (s32[8]{0:T(128)S(1)}, s32[8]{0:T(128)}, u32[]{:S(2)}) copy-start(s32[8]{0:T(128)} %constant.276.clone) | copy-start | bytes 100
  39.5 8.0 %collective-permute-start.7 = (f32[2,256,256]{1,2,0:T(8,128)S(1)}, f32[2,256,256]{1,2,0:T(8,128)S(1)}, u32[]{:S(2)}, u32[]{:S(2)}) collective-permute-start(f32[2,256,256]{1,2,0:T(8,128)S(1)} %pad_maximum_fusion.1), channel_id=1, source_target_pairs={{0,16},{1,9},{32,48},{33,41},{64,80},{65,73},{96,112},{97,105},{12... | collective-permute-start | bytes 1572872 | tf_op jit(solution)/shard_map/ppermute | solution.py:69
  48.1 19.3 %copy-start.8 = (s32[16]{0:T(128)S(1)}, s32[16]{0:T(128)}, u32[]{:S(2)}) copy-start(s32[16]{0:T(128)} %constant.277.clone) | copy-start | bytes 196
  48.1 8.0 %collective-permute-start.8 = (f32[2,256,256]{1,2,0:T(8,128)S(1)}, f32[2,256,256]{1,2,0:T(8,128)S(1)}, u32[]{:S(2)}, u32[]{:S(2)}) collective-permute-start(f32[2,256,256]{1,2,0:T(8,128)S(1)} %broadcast_select_fusion.6), channel_id=1, source_target_pairs={{0,8},{16,24},{1,17},{9,25},{32,40},{48,56},{33,49},{41,57},{64,72... | collective-permute-start | bytes 1572872 | tf_op jit(solution)/shard_map/ppermute | solution.py:69
  57.5 8.0 %collective-permute-start.9 = (f32[2,256,256]{1,2,0:T(8,128)S(1)}, f32[2,256,256]{1,2,0:T(8,128)S(1)}, u32[]{:S(2)}, u32[]{:S(2)}) collective-permute-start(f32[2,256,256]{1,2,0:T(8,128)S(1)} %broadcast_select_fusion.7), channel_id=1, source_target_pairs={{0,4},{16,20},{8,12},{24,28},{1,13},{9,5},{17,29},{25,21},{32,36},... | collective-permute-start | bytes 1572872 | tf_op jit(solution)/shard_map/ppermute | solution.py:69
  66.1 8.0 %collective-permute-start.10 = (f32[2,256,256]{1,2,0:T(8,128)S(1)}, f32[2,256,256]{1,2,0:T(8,128)S(1)}, u32[]{:S(2)}, u32[]{:S(2)}) collective-permute-start(f32[2,256,256]{1,2,0:T(8,128)S(1)} %broadcast_select_fusion.8), channel_id=1, source_target_pairs={{0,2},{16,18},{8,10},{24,26},{4,6},{20,22},{12,14},{28,30},{1,15},... | collective-permute-start | bytes 1572872 | tf_op jit(solution)/shard_map/ppermute | solution.py:69
  74.7 2.0 collective-permute-start.11
  77.8 27.9 %collective-permute-start.12 = (f32[8,256,256]{1,2,0:T(8,128)S(1)}, f32[8,256,256]{1,2,0:T(8,128)S(1)}, u32[]{:S(2)}, u32[]{:S(2)}) collective-permute-start(f32[8,256,256]{1,2,0:T(8,128)S(1)} %slice_bitcast_fusion.1), channel_id=1, source_target_pairs={{0,16},{1,9},{32,48},{33,41},{64,80},{65,73},{96,112},{97,105},{12... | collective-permute-start | bytes 6291464 | tf_op jit(solution)/shard_map/ppermute | solution.py:69
  106.6 62.2 %collective-permute-start.13 = (f32[8,256,256]{1,2,0:T(8,128)S(1)}, f32[8,256,256]{1,2,0:T(8,128)}, u32[]{:S(2)}, u32[]{:S(2)}) collective-permute-start(f32[8,256,256]{1,2,0:T(8,128)S(1)} %broadcast_select_fusion), channel_id=1, source_target_pairs={{0,8},{16,24},{1,17},{9,25},{32,40},{48,56},{33,49},{41,57},{64,72... | collective-permute-start | bytes 6291464 | tf_op jit(solution)/shard_map/ppermute | solution.py:69
  112.8 0.7 copy-start.4
  112.8 0.8 copy-start.5
  112.8 0.9 copy-start.6
  117.7 1.0 copy-start.3
  168.8 4.9 %copy-start.7 = (f32[1,128,128]{1,2,0:T(8,128)S(1)}, f32[1,128,128]{1,2,0:T(8,128)}, u32[]{:S(2)}) copy-start(f32[1,128,128]{1,2,0:T(8,128)} %custom-call.32) | copy-start | bytes 196612
  171.1 52.6 %collective-permute-start.14 = (f32[8,256,256]{1,2,0:T(8,128)}, f32[8,256,256]{1,2,0:T(8,128)}, u32[]{:S(2)}, u32[]{:S(2)}) collective-permute-start(f32[8,256,256]{1,2,0:T(8,128)} %broadcast_select_fusion.1), channel_id=1, source_target_pairs={{0,4},{16,20},{8,12},{24,28},{1,13},{9,5},{17,29},{25,21},{32,36},... | collective-permute-start | bytes 6291464 | tf_op jit(solution)/shard_map/ppermute | solution.py:69
  217.6 75.2 %collective-permute-start.17 = (f32[256,2,256]{2,1,0:T(2,128)}, f32[256,2,256]{2,1,0:T(2,128)}, u32[]{:S(2)}, u32[]{:S(2)}) collective-permute-start(f32[256,2,256]{2,1,0:T(2,128)} %slice_bitcast_fusion.2), channel_id=1, source_target_pairs={{0,32},{32,64},{1,33},{33,65},{2,34},{34,66},{3,35},{35,67},{4,36}... | collective-permute-start | bytes 1572872 | tf_op jit(solution)/shard_map/ppermute | solution.py:14
  219.1 78.6 %collective-permute-start.18 = (f32[256,2,256]{2,1,0:T(2,128)}, f32[256,2,256]{2,1,0:T(2,128)}, u32[]{:S(2)}, u32[]{:S(2)}) collective-permute-start(f32[256,2,256]{2,1,0:T(2,128)} %slice_bitcast_fusion.2), channel_id=1, source_target_pairs={{0,64},{32,96},{1,65},{33,97},{2,66},{34,98},{3,67},{35,99},{4,68}... | collective-permute-start | bytes 1572872 | tf_op jit(solution)/shard_map/ppermute | solution.py:14
  220.6 79.7 %collective-permute-start.19 = (f32[256,2,256]{2,1,0:T(2,128)}, f32[256,2,256]{2,1,0:T(2,128)}, u32[]{:S(2)}, u32[]{:S(2)}) collective-permute-start(f32[256,2,256]{2,1,0:T(2,128)} %slice_bitcast_fusion.2), channel_id=1, source_target_pairs={{0,96},{32,128},{1,97},{33,129},{2,98},{34,130},{3,99},{35,131},{4... | collective-permute-start | bytes 1572872 | tf_op jit(solution)/shard_map/ppermute | solution.py:14
  222.1 81.0 %collective-permute-start.20 = (f32[256,2,256]{2,1,0:T(2,128)}, f32[256,2,256]{2,1,0:T(2,128)}, u32[]{:S(2)}, u32[]{:S(2)}) collective-permute-start(f32[256,2,256]{2,1,0:T(2,128)} %slice_bitcast_fusion.2), channel_id=1, source_target_pairs={{0,128},{32,160},{1,129},{33,161},{2,130},{34,162},{3,131},{35,163... | collective-permute-start | bytes 1572872 | tf_op jit(solution)/shard_map/ppermute | solution.py:14
  223.7 60.8 %copy-start.2 = (f32[512,512]{1,0:T(8,128)S(1)}, f32[512,512]{1,0:T(8,128)}, u32[]{:S(2)}) copy-start(f32[512,512]{1,0:T(8,128)} %fusion.22) | copy-start | bytes 3145732
  226.4 65.0 %collective-permute-start.15 = (f32[8,256,256]{1,2,0:T(8,128)S(1)}, f32[8,256,256]{1,2,0:T(8,128)}, u32[]{:S(2)}, u32[]{:S(2)}) collective-permute-start(f32[8,256,256]{1,2,0:T(8,128)S(1)} %broadcast_select_fusion.2), channel_id=1, source_target_pairs={{0,2},{16,18},{8,10},{24,26},{4,6},{20,22},{12,14},{28,30},{1,15},... | collective-permute-start | bytes 6291464 | tf_op jit(solution)/shard_map/ppermute | solution.py:69
  291.3 13.0 %collective-permute-start.21 = (f32[256,2,256]{2,1,0:T(2,128)}, f32[256,2,256]{2,1,0:T(2,128)S(1)}, u32[]{:S(2)}, u32[]{:S(2)}) collective-permute-start(f32[256,2,256]{2,1,0:T(2,128)} %slice_bitcast_fusion.2), channel_id=1, source_target_pairs={{0,160},{32,192},{1,161},{33,193},{2,162},{34,194},{3,163},{35,195... | collective-permute-start | bytes 1572872 | tf_op jit(solution)/shard_map/ppermute | solution.py:14
  292.9 38.0 %collective-permute-start.16 = (f32[8,256,256]{1,2,0:T(8,128)S(1)}, f32[8,256,256]{1,2,0:T(8,128)S(1)}, u32[]{:S(2)}, u32[]{:S(2)}) collective-permute-start(f32[8,256,256]{1,2,0:T(8,128)S(1)} %broadcast_select_fusion.3), channel_id=1, source_target_pairs={{0,1},{1,0},{2,3},{3,2},{4,5},{5,4},{6,7},{7,6},{8,9},{9,8},{10,11... | collective-permute-start | bytes 6291464 | tf_op jit(solution)/shard_map/ppermute | solution.py:73
  297.7 28.4 %collective-permute-start.22 = (f32[256,2,256]{2,1,0:T(2,128)}, f32[256,2,256]{2,1,0:T(2,128)S(1)}, u32[]{:S(2)}, u32[]{:S(2)}) collective-permute-start(f32[256,2,256]{2,1,0:T(2,128)} %slice_bitcast_fusion.2), channel_id=1, source_target_pairs={{0,192},{32,224},{1,193},{33,225},{2,194},{34,226},{3,195},{35,227... | collective-permute-start | bytes 1572872 | tf_op jit(solution)/shard_map/ppermute | solution.py:14
  300.3 26.0 %collective-permute-start.23 = (f32[256,2,256]{2,1,0:T(2,128)}, f32[256,2,256]{2,1,0:T(2,128)S(1)}, u32[]{:S(2)}, u32[]{:S(2)}) collective-permute-start(f32[256,2,256]{2,1,0:T(2,128)} %slice_bitcast_fusion.2), channel_id=1, source_target_pairs={{0,224},{32,0},{1,225},{33,1},{2,226},{34,2},{3,227},{35,3},{4,228... | collective-permute-start | bytes 1572872 | tf_op jit(solution)/shard_map/ppermute | solution.py:14
  331.3 13.5 %copy-start = (f32[1,8,256,1,2,256]{2,5,4,1,3,0:T(8,128)S(1)}, f32[1,8,256,1,2,256]{2,5,4,1,3,0:T(8,128)}, u32[]{:S(2)}) copy-start(f32[1,8,256,1,2,256]{2,5,4,1,3,0:T(8,128)} %copy.10) | copy-start | bytes 12582916
  352.0 3.3 copy-start.1

commit v4 on v3

--- a/solution.py
+++ b/solution.py
@@ -9,11 +9,18 @@
 
 def prow_from_first_two(x, prows):
     me = lax.axis_index("prow")
-    got = [x]
-    for d in range(1, prows):
-        got.append(lax.ppermute(x, "prow", [(0, d), (1, (1 + d) % prows)]))
-    stack = jnp.stack(got)
-    return stack[me], stack[(me + prows - 1) % prows]
+    other = lax.ppermute(x, "prow", [(0, 1), (1, 0)])
+    pair = jnp.where(me == 0, jnp.stack([x, other]), jnp.stack([other, x]))
+    have = 2
+    while have < prows:
+        step = prows // 2 if have == 2 else have // 2
+        span = 2 * step
+        pairs = [(i, i + step) for i in range(prows) if i % span < 2 and i + step < prows]
+        got = lax.ppermute(pair, "prow", pairs)
+        targets = jnp.array([t for _, t in pairs], jnp.int32)
+        pair = jnp.where(jnp.any(targets == me), got, pair)
+        have *= 2
+    return pair[0], pair[1]
 
 
 def diag_to_first_pcols(tile0, prows, pcols):
@@ -83,29 +90,35 @@
     rt = covariance.shape[1]
     tile = covariance.shape[2]
     ct = covariance.shape[4]
-    nb = PANELS * tile
     tiles = covariance.reshape(rt, tile, ct, tile)
 
     first, second = diag_to_first_pcols(tiles[0, :, 0, :], prows, pcols)
     diag_a, diag_b = pcol_broadcast_pair(jnp.stack([first, second]), pcols)
-    block = jnp.concatenate(
-        [
-            jnp.concatenate([diag_a[0], diag_b[0]], axis=1),
-            jnp.concatenate([diag_a[1], diag_b[1]], axis=1),
-        ],
-        axis=0,
-    )
 
     rows_src = lax.optimization_barrier((tiles[:, :, 0, :], diag_a, diag_b))[0]
     col0, col1 = pcol_broadcast_pair(rows_src, pcols)
 
-    factor = jnp.tril(jnp.linalg.cholesky(block))
+    a00, a10 = diag_a[0], diag_a[1]
+    a11 = diag_b[1]
+    eye = jnp.eye(tile, dtype=a00.dtype)
+    l00 = jnp.tril(jnp.linalg.cholesky(a00))
 
-    cols_src = lax.optimization_barrier((tiles[0], factor))[0]
+    cols_src = lax.optimization_barrier((tiles[0], l00))[0]
     t0, t1 = prow_from_first_two(cols_src, prows)
 
-    inverse = jax.scipy.linalg.solve_triangular(
-        factor, jnp.eye(nb, dtype=factor.dtype), lower=True
+    l00_inv = jax.scipy.linalg.solve_triangular(l00, eye, lower=True)
+    l10 = jnp.dot(a10, l00_inv.T, precision=HI)
+    schur = a11 - jnp.dot(l10, l10.T, precision=HI)
+    l11 = jnp.tril(jnp.linalg.cholesky(schur))
+    l11_inv = jax.scipy.linalg.solve_triangular(l11, eye, lower=True)
+    low_inv = -jnp.dot(l11_inv, jnp.dot(l10, l00_inv, precision=HI), precision=HI)
+    zero = jnp.zeros_like(eye)
+    factor = jnp.concatenate(
+        [jnp.concatenate([l00, zero], axis=1), jnp.concatenate([l10, l11], axis=1)], axis=0
+    )
+    inverse = jnp.concatenate(
+        [jnp.concatenate([l00_inv, zero], axis=1), jnp.concatenate([low_inv, l11_inv], axis=1)],
+        axis=0,
     )
 
     rows_panel = jnp.concatenate([col0, col1], axis=-1)

time: 376 us -> 370 us (0.984)
  the two profiles are of different devices: /device:TPU:28 before, /device:TPU:1 now
where the time goes in v4:
time: 370 us; the launch traced here: 365 us
  other arithmetic  139 us (38%)
  waiting for transfers between devices  85.7 us (23%)
  local copies, waits for them, and re-layouts  48.6 us (13%)
  starting transfers between devices  48.2 us (13%)
  matrix products  39 us (11%)
  between operations  3.86 us (1%)
    ppermute x8, waiting for transfers between devices, pcol_broadcast_pair(): got = lax.ppermute(buf, 'pcol', pairs)  41.1 us
    another operation x7, other arithmetic, per_device(): l11 = jnp.tril(jnp.linalg.cholesky(schur))  34.7 us
    another operation x6, other arithmetic, per_device(): l00 = jnp.tril(jnp.linalg.cholesky(a00))  34 us
    ppermute x8, starting transfers between devices, pcol_broadcast_pair(): got = lax.ppermute(buf, 'pcol', pairs)  23.2 us
    another operation x2, other arithmetic, per_device(): l11_inv = jax.scipy.linalg.solve_triangular(l11, eye, lower=True)  22.3 us
    another operation x4, other arithmetic, per_device(): l00_inv = jax.scipy.linalg.solve_triangular(l00, eye, lower=True)  21.2 us
    ppermute x2, waiting for transfers between devices, prow_from_first_two(): got = lax.ppermute(pair, 'prow', pairs)  20.4 us
    unnamed x66, local copies, waits for them, and re-layouts  20.3 us
  transfers between devices with their start and end apart: 20, of which 10 were waited for; matrix products, arithmetic and copies ran while one was open for 44% of the time, Pallas kernels for 0%

profile of v4, /device:TPU:1, one launch (start us, length us, event | category | flops | bytes accessed | tf_op | source)
XLA Modules:
  0.0 364.8 jit_solution(2680654949747715145)
XLA Ops:
  0.0 7.2 %copy.12 = f32[1,8,256,1,2,256]{2,5,4,1,3,0:T(8,128)} copy(f32[1,8,256,1,2,256]{5,4,3,2,1,0:T(2,128)} %param.18) | data formatting | bytes 8388608 | tf_op args[0]
  8.2 6.2 %collective-permute-start = (f32[256,256]{0,1:T(8,128)S(1)}, f32[256,256]{0,1:T(8,128)}, u32[]{:S(2)}, u32[]{:S(2)}) collective-permute-start(f32[256,256]{0,1:T(8,128)S(1)} %slice_bitcast_fusion.10), channel_id=1, source_target_pairs={{0,32},{32,64},{1,33},{33,65}} | collective-permute-start | bytes 786440 | tf_op jit(solution)/shard_map/ppermute | solution.py:34
  15.6 1.7 collective-permute-start.2
  18.6 1.7 collective-permute-start.4
  23.6 8.2 %collective-permute-done.1 = f32[256,256]{0,1:T(8,128)S(1)} collective-permute-done((f32[256,256]{0,1:T(8,128)S(1)}, f32[256,256]{0,1:T(8,128)S(1)}, u32[]{:S(2)}, u32[]{:S(2)}) %collective-permute-start.1) | collective-permute-done | bytes 262176 | tf_op jit(solution)/shard_map/ppermute | solution.py:34
  31.8 1.9 collective-permute-start.6
  33.8 3.6 collective-permute-done.3
  37.6 4.9 %collective-permute-done.6 = f32[256,256]{0,1:T(8,128)S(1)} collective-permute-done((f32[256,256]{0,1:T(8,128)S(1)}, f32[256,256]{0,1:T(8,128)S(1)}, u32[]{:S(2)}, u32[]{:S(2)}) %collective-permute-start.6) | collective-permute-done | bytes 262176 | tf_op jit(solution)/shard_map/ppermute | solution.py:34
  44.7 5.3 %collective-permute-done.7 = f32[2,256,256]{1,2,0:T(8,128)S(1)} collective-permute-done((f32[2,256,256]{1,2,0:T(8,128)S(1)}, f32[2,256,256]{1,2,0:T(8,128)S(1)}, u32[]{:S(2)}, u32[]{:S(2)}) %collective-permute-start.7) | collective-permute-done | bytes 524320 | tf_op jit(solution)/shard_map/ppermute | solution.py:76
  52.8 5.4 %collective-permute-done.8 = f32[2,256,256]{1,2,0:T(8,128)S(1)} collective-permute-done((f32[2,256,256]{1,2,0:T(8,128)S(1)}, f32[2,256,256]{1,2,0:T(8,128)S(1)}, u32[]{:S(2)}, u32[]{:S(2)}) %collective-permute-start.8) | collective-permute-done | bytes 524320 | tf_op jit(solution)/shard_map/ppermute | solution.py:76
  61.6 5.4 %collective-permute-done.9 = f32[2,256,256]{1,2,0:T(8,128)S(1)} collective-permute-done((f32[2,256,256]{1,2,0:T(8,128)S(1)}, f32[2,256,256]{1,2,0:T(8,128)S(1)}, u32[]{:S(2)}, u32[]{:S(2)}) %collective-permute-start.9) | collective-permute-done | bytes 524320 | tf_op jit(solution)/shard_map/ppermute | solution.py:76
  69.7 5.4 %collective-permute-done.10 = f32[2,256,256]{1,2,0:T(8,128)S(1)} collective-permute-done((f32[2,256,256]{1,2,0:T(8,128)S(1)}, f32[2,256,256]{1,2,0:T(8,128)S(1)}, u32[]{:S(2)}, u32[]{:S(2)}) %collective-permute-start.10) | collective-permute-done | bytes 524320 | tf_op jit(solution)/shard_map/ppermute | solution.py:76
  75.8 3.8 %collective-permute-start.11 = (f32[2,256,256]{1,2,0:T(8,128)S(1)}, f32[2,256,256]{1,2,0:T(8,128)}, u32[]{:S(2)}, u32[]{:S(2)}) collective-permute-start(f32[2,256,256]{1,2,0:T(8,128)S(1)} %broadcast_select_fusion.11), channel_id=1, source_target_pairs={{0,1},{1,0},{2,3},{3,2},{4,5},{5,4},{6,7},{7,6},{8,9},{9,8},{10,11... | collective-permute-start | bytes 1572872 | tf_op jit(solution)/shard_map/ppermute | solution.py:80
  79.6 1.8 slice_bitcast_fusion.1
  81.5 2.4 broadcast_select_fusion.12
  83.9 9.3 %collective-permute-start.12 = (f32[8,256,256]{1,2,0:T(8,128)S(1)}, f32[8,256,256]{1,2,0:T(8,128)}, u32[]{:S(2)}, u32[]{:S(2)}) collective-permute-start(f32[8,256,256]{1,2,0:T(8,128)S(1)} %slice_bitcast_fusion.1), channel_id=1, source_target_pairs={{0,16},{1,9},{32,48},{33,41},{64,80},{65,73},{96,112},{97,105},{12... | collective-permute-start | bytes 6291464 | tf_op jit(solution)/shard_map/ppermute | solution.py:76
  95.3 19.5 %collective-permute-done.12 = f32[8,256,256]{1,2,0:T(8,128)} collective-permute-done((f32[8,256,256]{1,2,0:T(8,128)S(1)}, f32[8,256,256]{1,2,0:T(8,128)}, u32[]{:S(2)}, u32[]{:S(2)}) %collective-permute-start.12) | collective-permute-done | bytes 2097184 | tf_op jit(solution)/shard_map/ppermute | solution.py:76
  114.8 2.6 broadcast_select_fusion.2
  117.5 2.8 collective-permute-start.13
  124.1 11.7 %cholesky.130 = f32[128,128]{1,0:T(8,128)S(1)} custom-call(f32[128,128]{1,0:T(8,128)S(1)} %cholesky.194), custom_call_target="Cholesky" | custom-call | tf_op jit(solution)/shard_map/jit(cholesky)/cholesky | solution.py:104
  135.9 9.8 %custom-call.13 = f32[1,128,128]{1,2,0:T(8,128)S(1)} custom-call(f32[1,128,128]{2,1,0:T(8,128)S(1)} %get-tuple-element.94), custom_call_target="InvertDiagBlocksLowerTriangular" | custom-call | tf_op jit(solution)/shard_map/jit(cholesky)/cholesky | solution.py:104
  148.0 11.7 %cholesky.147 = f32[128,128]{1,0:T(8,128)S(1)} custom-call(f32[128,128]{1,0:T(8,128)S(1)} %convolution_subtract_fusion.3), custom_call_target="Cholesky" | custom-call | tf_op jit(solution)/shard_map/jit(cholesky)/cholesky | solution.py:104
  162.6 2.5 broadcast_select_fusion.3
  165.2 2.8 collective-permute-start.14
  168.7 5.4 %while.6 = (s32[]{:T(128)}, f32[256,256]{0,1:T(8,128)S(1)}, s32[2,2]{1,0:T(2,128)S(1)}, f32[2,128,128]{2,1,0:T(8,128)}, s32[]{:T(128)}) while((s32[]{:T(128)}, f32[256,256]{0,1:T(8,128)S(1)}, s32[2,2]{1,0:T(2,128)S(1)}, f32[2,128,128]{2,1,0:T(8,128)}, s32[]{:T(128)}) %tuple.60), condition=%wide.while_cond.2, body=%wide.while_body.2.sunk | while | flops 2 | bytes 393829 | solution.py:109
  174.8 20.5 %custom-call.14 = f32[2,128,128]{1,2,0:T(8,128)S(1)} custom-call(f32[2,128,128]{2,1,0:T(8,128)} %get-tuple-element.49), custom_call_target="InvertDiagBlocksLowerTriangular" | custom-call | tf_op jit(solution)/shard_map/jit(_solve_triangular)/triangular_solve | solution.py:109
  202.8 11.7 %cholesky.164 = f32[128,128]{1,0:T(8,128)S(1)} custom-call(f32[128,128]{1,0:T(8,128)S(1)} %cholesky.197), custom_call_target="Cholesky" | custom-call | tf_op jit(solution)/shard_map/jit(cholesky)/cholesky | solution.py:112
  214.6 9.8 %custom-call.15 = f32[1,128,128]{1,2,0:T(8,128)S(1)} custom-call(f32[1,128,128]{2,1,0:T(8,128)S(1)} %get-tuple-element.92), custom_call_target="InvertDiagBlocksLowerTriangular" | custom-call | tf_op jit(solution)/shard_map/jit(cholesky)/cholesky | solution.py:112
  226.3 2.6 broadcast_select_fusion.4
  228.9 3.0 collective-permute-start.15
  233.1 11.7 %cholesky.181 = f32[128,128]{1,0:T(8,128)S(1)} custom-call(f32[128,128]{1,0:T(8,128)S(1)} %convolution_subtract_fusion.2), custom_call_target="Cholesky" | custom-call | tf_op jit(solution)/shard_map/jit(cholesky)/cholesky | solution.py:112
  244.8 1.9 collective-permute-start.17
  250.2 1.8 fusion.32
  252.0 7.4 %collective-permute-done.17 = f32[256,2,256]{2,1,0:T(2,128)S(1)} collective-permute-done((f32[256,2,256]{2,1,0:T(2,128)S(1)}, f32[256,2,256]{2,1,0:T(2,128)S(1)}, u32[]{:S(2)}, u32[]{:S(2)}) %collective-permute-start.17) | collective-permute-done | bytes 524320 | tf_op jit(solution)/shard_map/ppermute | solution.py:12
  260.2 2.9 maximum_select_fusion
  263.1 2.3 collective-permute-start.18
  266.0 5.3 %while.7 = (s32[]{:T(128)}, f32[256,256]{0,1:T(8,128)S(1)}, s32[2,2]{1,0:T(2,128)S(1)}, f32[2,128,128]{2,1,0:T(8,128)}, s32[]{:T(128)}) while((s32[]{:T(128)}, f32[256,256]{0,1:T(8,128)S(1)}, s32[2,2]{1,0:T(2,128)S(1)}, f32[2,128,128]{2,1,0:T(8,128)}, s32[]{:T(128)}) %tuple.67), condition=%wide.while_cond.2.clone, body=%wide.while_body.2.clone.sunk | while | flops 2 | bytes 393829 | solution.py:113
  271.3 20.5 %custom-call.16 = f32[2,128,128]{1,2,0:T(8,128)S(1)} custom-call(f32[2,128,128]{2,1,0:T(8,128)} %get-tuple-element.50), custom_call_target="InvertDiagBlocksLowerTriangular" | custom-call | tf_op jit(solution)/shard_map/jit(_solve_triangular)/triangular_solve | solution.py:113
  298.1 20.4 %collective-permute-done.19 = f32[2,256,2,256]{3,2,1,0:T(2,128)S(1)} collective-permute-done((f32[2,256,2,256]{3,2,1,0:T(2,128)S(1)}, f32[2,256,2,256]{3,2,1,0:T(2,128)S(1)}, u32[]{:S(2)}, u32[]{:S(2)}) %collective-permute-start.19) | collective-permute-done | bytes 1048608 | tf_op jit(solution)/shard_map/ppermute | solution.py:19
  320.0 4.5 %convolution_bitcast_fusion = f32[2,256,512,1]{2,1,0,3:T(8,128)} fusion(f32[2,256,512]{1,0,2:T(2,128)S(1)} %pad_maximum_fusion, f32[256,256]{1,0:T(8,128)S(1)} %pad_maximum_fusion.2, f32[128,256]{1,0:T(8,128)S(1)} %fusion.40, f32[128,256]{1,0:T(8,128)S(1)} %fusion.35, f32[256,256]{1,0:T(8,128)S(1)} %convolution_negate_fusion), kind=kOutput, calls=%fused_computation.16 | convolution fusion | flops 1611923456 | bytes 2883584 | tf_op jit(solution)/shard_map/cak,bk->cab/dot_general | solution.py:129
  324.9 13.4 %fusion = f32[8,256,512]{2,1,0:T(8,128)S(1)} fusion(f32[8,256,256]{1,2,0:T(8,128)S(1)} %get-tuple-element.84, f32[8,256,256]{1,2,0:T(8,128)S(1)} %get-tuple-element.83, f32[256,256]{1,0:T(8,128)S(1)} %pad_maximum_fusion.2, f32[128,256]{1,0:T(8,128)S(1)} %fusion.40, f32[128,256]{1,0:T(8,128)S(1)} %fusion.35, f32[256,256]{1,0:T(8,128)S(1)} %convolution_negate_fusion), kind=kOutput, calls=%fused_computation.4 | convolution fusion | flops 6444810240 | bytes 9175040 | tf_op jit(solution)/shard_map/rak,bk->rab/dot_general | solution.py:128
  338.3 1.9 copy-done
  340.2 1.6 constant_dynamic-slice_fusion.2
  341.8 2.2 copy.37
  344.1 9.3 %subtract_select_fusion = f32[8,256,2,256]{1,3,2,0:T(8,128)S(1)} fusion(f32[2,256,512,1]{2,1,0,3:T(8,128)S(1)} %copy-done.16, f32[8,256,512]{2,1,0:T(8,128)} %copy-done, pred[8,2]{1,0:T(8,128)(4,1)S(1)} %broadcast_and_fusion, f32[1,8,256,1,2,256]{2,5,4,1,3,0:T(8,128)} %copy.12), kind=kOutput, calls=%fused_computation.10 | convolution fusion | flops 6444548096 | bytes 13631504 | tf_op jit(solution)/shard_map/rak,cbk->racb/dot_general | solution.py:130
  353.4 1.9 copy.70
  355.7 1.7 fusion.10
  357.3 7.2 %copy.28 = f32[1,8,256,1,2,256]{5,4,3,2,1,0:T(2,128)} copy(f32[1,8,256,1,2,256]{2,5,4,1,3,0:T(8,128)} %fusion.10) | data formatting | bytes 8388608 | tf_op jit(solution)/shard_map/scatter | solution.py:144
  (172 shorter events, 62.8 us)
Async XLA Ops:
  8.2 13.1 %collective-permute-start = (f32[256,256]{0,1:T(8,128)S(1)}, f32[256,256]{0,1:T(8,128)}, u32[]{:S(2)}, u32[]{:S(2)}) collective-permute-start(f32[256,256]{0,1:T(8,128)S(1)} %slice_bitcast_fusion.10), channel_id=1, source_target_pairs={{0,32},{32,64},{1,33},{33,65}} | collective-permute-start | bytes 786440 | tf_op jit(solution)/shard_map/ppermute | solution.py:34
  14.3 17.5 %collective-permute-start.1 = (f32[256,256]{0,1:T(8,128)S(1)}, f32[256,256]{0,1:T(8,128)S(1)}, u32[]{:S(2)}, u32[]{:S(2)}) collective-permute-start(f32[256,256]{0,1:T(8,128)S(1)} %slice_bitcast_fusion.10), channel_id=1, source_target_pairs={{0,64},{32,96},{1,65},{33,97}} | collective-permute-start | bytes 786440 | tf_op jit(solution)/shard_map/ppermute | solution.py:34
  15.6 18.1 %collective-permute-start.2 = (f32[256,256]{0,1:T(8,128)S(1)}, f32[256,256]{0,1:T(8,128)S(1)}, u32[]{:S(2)}, u32[]{:S(2)}) collective-permute-start(f32[256,256]{0,1:T(8,128)S(1)} %slice_bitcast_fusion.10), channel_id=1, source_target_pairs={{0,96},{32,128},{1,97},{33,129}} | collective-permute-start | bytes 786440 | tf_op jit(solution)/shard_map/ppermute | solution.py:34
  17.3 20.1 %collective-permute-start.3 = (f32[256,256]{0,1:T(8,128)S(1)}, f32[256,256]{0,1:T(8,128)S(1)}, u32[]{:S(2)}, u32[]{:S(2)}) collective-permute-start(f32[256,256]{0,1:T(8,128)S(1)} %slice_bitcast_fusion.10), channel_id=1, source_target_pairs={{0,128},{32,160},{1,129},{33,161}} | collective-permute-start | bytes 786440 | tf_op jit(solution)/shard_map/ppermute | solution.py:34
  18.6 18.8 %collective-permute-start.4 = (f32[256,256]{0,1:T(8,128)S(1)}, f32[256,256]{0,1:T(8,128)S(1)}, u32[]{:S(2)}, u32[]{:S(2)}) collective-permute-start(f32[256,256]{0,1:T(8,128)S(1)} %slice_bitcast_fusion.10), channel_id=1, source_target_pairs={{0,160},{32,192},{1,161},{33,193}} | collective-permute-start | bytes 786440 | tf_op jit(solution)/shard_map/ppermute | solution.py:34
  21.3 16.2 %collective-permute-start.5 = (f32[256,256]{0,1:T(8,128)S(1)}, f32[256,256]{0,1:T(8,128)S(1)}, u32[]{:S(2)}, u32[]{:S(2)}) collective-permute-start(f32[256,256]{0,1:T(8,128)S(1)} %slice_bitcast_fusion.10), channel_id=1, source_target_pairs={{0,192},{32,224},{1,193},{33,225}} | collective-permute-start | bytes 786440 | tf_op jit(solution)/shard_map/ppermute | solution.py:34
  31.8 10.7 %collective-permute-start.6 = (f32[256,256]{0,1:T(8,128)S(1)}, f32[256,256]{0,1:T(8,128)S(1)}, u32[]{:S(2)}, u32[]{:S(2)}) collective-permute-start(f32[256,256]{0,1:T(8,128)S(1)} %slice_bitcast_fusion.10), channel_id=1, source_target_pairs={{0,224},{32,0},{1,225},{33,1}} | collective-permute-start | bytes 786440 | tf_op jit(solution)/shard_map/ppermute | solution.py:34
  33.8 10.2 %copy-start.27 = (s32[2]{0:T(128)S(1)}, s32[2]{0:T(128)}, u32[]{:S(2)}) copy-start(s32[2]{0:T(128)} %constant.194.clone) | copy-start | bytes 28
  37.5 14.6 %copy-start.26 = (s32[4]{0:T(128)S(1)}, s32[4]{0:T(128)}, u32[]{:S(2)}) copy-start(s32[4]{0:T(128)} %constant.195.clone) | copy-start | bytes 52
  42.6 18.3 %copy-start.25 = (s32[8]{0:T(128)S(1)}, s32[8]{0:T(128)}, u32[]{:S(2)}) copy-start(s32[8]{0:T(128)} %constant.196.clone) | copy-start | bytes 100
  42.6 7.4 %collective-permute-start.7 = (f32[2,256,256]{1,2,0:T(8,128)S(1)}, f32[2,256,256]{1,2,0:T(8,128)S(1)}, u32[]{:S(2)}, u32[]{:S(2)}) collective-permute-start(f32[2,256,256]{1,2,0:T(8,128)S(1)} %pad_maximum_fusion.1), channel_id=1, source_target_pairs={{0,16},{1,9},{32,48},{33,41},{64,80},{65,73},{96,112},{97,105},{12... | collective-permute-start | bytes 1572872 | tf_op jit(solution)/shard_map/ppermute | solution.py:76
  50.8 18.2 %copy-start.24 = (s32[16]{0:T(128)S(1)}, s32[16]{0:T(128)}, u32[]{:S(2)}) copy-start(s32[16]{0:T(128)} %constant.197.clone) | copy-start | bytes 196
  50.8 7.4 %collective-permute-start.8 = (f32[2,256,256]{1,2,0:T(8,128)S(1)}, f32[2,256,256]{1,2,0:T(8,128)S(1)}, u32[]{:S(2)}, u32[]{:S(2)}) collective-permute-start(f32[2,256,256]{1,2,0:T(8,128)S(1)} %broadcast_select_fusion.8), channel_id=1, source_target_pairs={{0,8},{16,24},{1,17},{9,25},{32,40},{48,56},{33,49},{41,57},{64,72... | collective-permute-start | bytes 1572872 | tf_op jit(solution)/shard_map/ppermute | solution.py:76
  59.6 7.4 %collective-permute-start.9 = (f32[2,256,256]{1,2,0:T(8,128)S(1)}, f32[2,256,256]{1,2,0:T(8,128)S(1)}, u32[]{:S(2)}, u32[]{:S(2)}) collective-permute-start(f32[2,256,256]{1,2,0:T(8,128)S(1)} %broadcast_select_fusion.9), channel_id=1, source_target_pairs={{0,4},{16,20},{8,12},{24,28},{1,13},{9,5},{17,29},{25,21},{32,36},... | collective-permute-start | bytes 1572872 | tf_op jit(solution)/shard_map/ppermute | solution.py:76
  67.7 7.4 %collective-permute-start.10 = (f32[2,256,256]{1,2,0:T(8,128)S(1)}, f32[2,256,256]{1,2,0:T(8,128)S(1)}, u32[]{:S(2)}, u32[]{:S(2)}) collective-permute-start(f32[2,256,256]{1,2,0:T(8,128)S(1)} %broadcast_select_fusion.10), channel_id=1, source_target_pairs={{0,2},{16,18},{8,10},{24,26},{4,6},{20,22},{12,14},{28,30},{1,15},... | collective-permute-start | bytes 1572872 | tf_op jit(solution)/shard_map/ppermute | solution.py:76
  75.8 5.7 %collective-permute-start.11 = (f32[2,256,256]{1,2,0:T(8,128)S(1)}, f32[2,256,256]{1,2,0:T(8,128)}, u32[]{:S(2)}, u32[]{:S(2)}) collective-permute-start(f32[2,256,256]{1,2,0:T(8,128)S(1)} %broadcast_select_fusion.11), channel_id=1, source_target_pairs={{0,1},{1,0},{2,3},{3,2},{4,5},{5,4},{6,7},{7,6},{8,9},{9,8},{10,11... | collective-permute-start | bytes 1572872 | tf_op jit(solution)/shard_map/ppermute | solution.py:80
  81.4 13.9 %copy-start.3 = (f32[8,256,256]{1,2,0:T(8,128)}, f32[8,256,256]{1,2,0:T(8,128)S(1)}, u32[]{:S(2)}) copy-start(f32[8,256,256]{1,2,0:T(8,128)S(1)} %slice_bitcast_fusion.1) | copy-start | bytes 6291460
  81.4 11.8 %copy-start.23 = (s32[2]{0:T(128)S(1)}, s32[2]{0:T(128)}, u32[]{:S(2)}) copy-start(s32[2]{0:T(128)} %constant.198.clone) | copy-start | bytes 28
  81.5 12.4 %copy-start.22 = (s32[4]{0:T(128)S(1)}, s32[4]{0:T(128)}, u32[]{:S(2)}) copy-start(s32[4]{0:T(128)} %constant.199.clone) | copy-start | bytes 52
  83.9 31.0 %collective-permute-start.12 = (f32[8,256,256]{1,2,0:T(8,128)S(1)}, f32[8,256,256]{1,2,0:T(8,128)}, u32[]{:S(2)}, u32[]{:S(2)}) collective-permute-start(f32[8,256,256]{1,2,0:T(8,128)S(1)} %slice_bitcast_fusion.1), channel_id=1, source_target_pairs={{0,16},{1,9},{32,48},{33,41},{64,80},{65,73},{96,112},{97,105},{12... | collective-permute-start | bytes 6291464 | tf_op jit(solution)/shard_map/ppermute | solution.py:76
  117.5 44.4 %copy-start.2 = (f32[8,256,256]{1,2,0:T(8,128)}, f32[8,256,256]{1,2,0:T(8,128)S(1)}, u32[]{:S(2)}) copy-start(f32[8,256,256]{1,2,0:T(8,128)S(1)} %broadcast_select_fusion.2) | copy-start | bytes 6291460
  117.5 45.1 %collective-permute-start.13 = (f32[8,256,256]{1,2,0:T(8,128)S(1)}, f32[8,256,256]{1,2,0:T(8,128)}, u32[]{:S(2)}, u32[]{:S(2)}) collective-permute-start(f32[8,256,256]{1,2,0:T(8,128)S(1)} %broadcast_select_fusion.2), channel_id=1, source_target_pairs={{0,8},{16,24},{1,17},{9,25},{32,40},{48,56},{33,49},{41,57},{64,72... | collective-permute-start | bytes 6291464 | tf_op jit(solution)/shard_map/ppermute | solution.py:76
  123.4 0.7 copy-start.17
  165.2 36.7 %copy-start.1 = (f32[8,256,256]{1,2,0:T(8,128)}, f32[8,256,256]{1,2,0:T(8,128)S(1)}, u32[]{:S(2)}) copy-start(f32[8,256,256]{1,2,0:T(8,128)S(1)} %broadcast_select_fusion.3) | copy-start | bytes 6291460
  165.2 61.2 %collective-permute-start.14 = (f32[8,256,256]{1,2,0:T(8,128)S(1)}, f32[8,256,256]{1,2,0:T(8,128)}, u32[]{:S(2)}, u32[]{:S(2)}) collective-permute-start(f32[8,256,256]{1,2,0:T(8,128)S(1)} %broadcast_select_fusion.3), channel_id=1, source_target_pairs={{0,4},{16,20},{8,12},{24,28},{1,13},{9,5},{17,29},{25,21},{32,36},... | collective-permute-start | bytes 6291464 | tf_op jit(solution)/shard_map/ppermute | solution.py:76
  174.1 0.7 copy-start.12
  195.3 0.7 copy-start.21
  197.2 17.4 %copy-start.4 = (f32[128,256]{1,0:T(8,128)}, f32[128,256]{1,0:T(8,128)S(1)}, u32[]{:S(2)}) copy-start(f32[128,256]{1,0:T(8,128)S(1)} %fusion.37) | copy-start | bytes 393220
  199.6 0.7 copy-start.9
  202.0 0.7 copy-start.18
  225.6 0.7 copy-start.15
  228.9 63.2 %collective-permute-start.15 = (f32[8,256,256]{1,2,0:T(8,128)S(1)}, f32[8,256,256]{1,2,0:T(8,128)}, u32[]{:S(2)}, u32[]{:S(2)}) collective-permute-start(f32[8,256,256]{1,2,0:T(8,128)S(1)} %broadcast_select_fusion.4), channel_id=1, source_target_pairs={{0,2},{16,18},{8,10},{24,26},{4,6},{20,22},{12,14},{28,30},{1,15},... | collective-permute-start | bytes 6291464 | tf_op jit(solution)/shard_map/ppermute | solution.py:76
  244.8 14.6 %collective-permute-start.17 = (f32[256,2,256]{2,1,0:T(2,128)S(1)}, f32[256,2,256]{2,1,0:T(2,128)S(1)}, u32[]{:S(2)}, u32[]{:S(2)}) collective-permute-start(f32[256,2,256]{2,1,0:T(2,128)S(1)} %slice_bitcast_fusion.4), channel_id=1, source_target_pairs={{0,32},{32,0},{1,33},{33,1},{2,34},{34,2},{3,35},{35,3},{4,36},{36... | collective-permute-start | bytes 1572872 | tf_op jit(solution)/shard_map/ppermute | solution.py:12
  259.4 0.8 copy-start.7
  260.2 5.9 %copy-start.11 = (f32[256,256]{0,1:T(8,128)S(1)}, f32[256,256]{0,1:T(8,128)}, u32[]{:S(2)}) copy-start(f32[256,256]{0,1:T(8,128)} %get-tuple-element.173) | copy-start | bytes 786436
  260.2 31.6 %copy-start.6 = (f32[256,256]{1,0:T(8,128)S(1)}, f32[256,256]{1,0:T(8,128)}, u32[]{:S(2)}) copy-start(f32[256,256]{1,0:T(8,128)} %fusion.34) | copy-start | bytes 786436
  263.1 30.4 %collective-permute-start.18 = (f32[2,256,2,256]{3,2,1,0:T(2,128)}, f32[2,256,2,256]{3,2,1,0:T(2,128)}, u32[]{:S(2)}, u32[]{:S(2)}) collective-permute-start(f32[2,256,2,256]{3,2,1,0:T(2,128)} %maximum_select_fusion), channel_id=1, source_target_pairs={{0,128},{32,160},{1,129},{33,161},{2,130},{34,162},{3,131},{35,163... | collective-permute-start | bytes 3145736 | tf_op jit(solution)/shard_map/ppermute | solution.py:19
  291.8 0.7 copy-start.19
  292.1 1.4 copy-start.8
  293.4 3.0 copy-start.5
  293.4 3.0 copy-start.10
  293.4 3.4 copy-start.20
  293.4 31.1 %collective-permute-start.16 = (f32[8,256,256]{1,2,0:T(8,128)S(1)}, f32[8,256,256]{1,2,0:T(8,128)S(1)}, u32[]{:S(2)}, u32[]{:S(2)}) collective-permute-start(f32[8,256,256]{1,2,0:T(8,128)S(1)} %broadcast_select_fusion.5), channel_id=1, source_target_pairs={{0,1},{1,0},{2,3},{3,2},{4,5},{5,4},{6,7},{7,6},{8,9},{9,8},{10,11... | collective-permute-start | bytes 6291464 | tf_op jit(solution)/shard_map/ppermute | solution.py:80
  294.9 23.6 %collective-permute-start.19 = (f32[2,256,2,256]{3,2,1,0:T(2,128)S(1)}, f32[2,256,2,256]{3,2,1,0:T(2,128)S(1)}, u32[]{:S(2)}, u32[]{:S(2)}) collective-permute-start(f32[2,256,2,256]{3,2,1,0:T(2,128)S(1)} %broadcast_select_fusion), channel_id=1, source_target_pairs={{0,64},{32,96},{128,192},{160,224},{1,65},{33,97},{129,193},{161,2... | collective-permute-start | bytes 3145736 | tf_op jit(solution)/shard_map/ppermute | solution.py:19
  338.3 1.9 copy-start
  341.8 2.3 copy-start.16
  353.4 2.0 copy-start.13
  353.4 2.0 copy-start.14

commit v5 on v4

--- a/solution.py
+++ b/solution.py
@@ -95,16 +95,16 @@
     first, second = diag_to_first_pcols(tiles[0, :, 0, :], prows, pcols)
     diag_a, diag_b = pcol_broadcast_pair(jnp.stack([first, second]), pcols)
 
-    rows_src = lax.optimization_barrier((tiles[:, :, 0, :], diag_a, diag_b))[0]
-    col0, col1 = pcol_broadcast_pair(rows_src, pcols)
+    cols_src = lax.optimization_barrier((tiles[0], first, second))[0]
+    t0, t1 = prow_from_first_two(cols_src, prows)
 
     a00, a10 = diag_a[0], diag_a[1]
     a11 = diag_b[1]
     eye = jnp.eye(tile, dtype=a00.dtype)
     l00 = jnp.tril(jnp.linalg.cholesky(a00))
 
-    cols_src = lax.optimization_barrier((tiles[0], l00))[0]
-    t0, t1 = prow_from_first_two(cols_src, prows)
+    rows_src = lax.optimization_barrier((tiles[:, :, 0, :], l00))[0]
+    col0, col1 = pcol_broadcast_pair(rows_src, pcols)
 
     l00_inv = jax.scipy.linalg.solve_triangular(l00, eye, lower=True)
     l10 = jnp.dot(a10, l00_inv.T, precision=HI)

time: 370 us -> 382 us (1.032)
  starting transfers between devices: 48.2 us -> 64.2 us
  waiting for transfers between devices: 85.7 us -> 92.5 us
  local copies, waits for them, and re-layouts: 48.6 us -> 42.6 us
    ppermute x2, waiting for transfers between devices: 20.4 us -> 35.7 us  [prow_from_first_two(): got = lax.ppermute(pair, 'prow', pairs)]
    ppermute x8, starting transfers between devices: 23.2 us -> 36.1 us  [pcol_broadcast_pair(): got = lax.ppermute(buf, 'pcol', pairs)]
    ppermute x1, waiting for transfers between devices: 7.36 us -> 0.01 us  [prow_from_first_two(): other = lax.ppermute(x, 'prow', [(0, 1), (1, 0)])]
    unnamed x66 -> x46, local copies, waits for them, and re-layouts: 20.3 us -> 16.9 us
  transfers between devices with their start and end apart: 20 -> 20, of which waited for: 10 -> 10; matrix products, arithmetic and copies ran while one was open for 44% -> 31% of each run, Pallas kernels for 0% -> 0%
where the time goes in v5:
time: 382 us; the launch traced here: 377 us
  other arithmetic  138 us (36%)
  waiting for transfers between devices  92.5 us (24%)
  starting transfers between devices  64.2 us (17%)
  local copies, waits for them, and re-layouts  42.6 us (11%)
  matrix products  35.5 us (9%)
    ppermute x8, waiting for transfers between devices, pcol_broadcast_pair(): got = lax.ppermute(buf, 'pcol', pairs)  40 us
    ppermute x8, starting transfers between devices, pcol_broadcast_pair(): got = lax.ppermute(buf, 'pcol', pairs)  36.1 us
    ppermute x2, waiting for transfers between devices, prow_from_first_two(): got = lax.ppermute(pair, 'prow', pairs)  35.7 us
    another operation x7, other arithmetic, per_device(): l11 = jnp.tril(jnp.linalg.cholesky(schur))  34.6 us
    another operation x6, other arithmetic, per_device(): l00 = jnp.tril(jnp.linalg.cholesky(a00))  34 us
    another operation x2, other arithmetic, per_device(): l11_inv = jax.scipy.linalg.solve_triangular(l11, eye, lower=True)  20.8 us
    another operation x4, other arithmetic, per_device(): l00_inv = jax.scipy.linalg.solve_triangular(l00, eye, lower=True)  20.5 us
    unnamed x46, local copies, waits for them, and re-layouts  16.9 us
  transfers between devices with their start and end apart: 20, of which 10 were waited for; matrix products, arithmetic and copies ran while one was open for 31% of the time, Pallas kernels for 0%

profile of v5, /device:TPU:1, one launch (start us, length us, event | category | flops | bytes accessed | tf_op | source)
XLA Modules:
  0.0 376.7 jit_solution(12324594422823493977)
XLA Ops:
  0.0 7.2 %copy.12 = f32[1,8,256,1,2,256]{2,5,4,1,3,0:T(8,128)} copy(f32[1,8,256,1,2,256]{5,4,3,2,1,0:T(2,128)} %param.18) | data formatting | bytes 8388608 | tf_op args[0]
  8.2 6.2 %collective-permute-start = (f32[256,256]{0,1:T(8,128)S(1)}, f32[256,256]{0,1:T(8,128)}, u32[]{:S(2)}, u32[]{:S(2)}) collective-permute-start(f32[256,256]{0,1:T(8,128)S(1)} %slice_bitcast_fusion.9), channel_id=1, source_target_pairs={{0,32},{32,64},{1,33},{33,65}} | collective-permute-start | bytes 786440 | tf_op jit(solution)/shard_map/ppermute | solution.py:34
  15.6 1.7 collective-permute-start.2
  23.6 8.2 %collective-permute-done.1 = f32[256,256]{0,1:T(8,128)S(1)} collective-permute-done((f32[256,256]{0,1:T(8,128)S(1)}, f32[256,256]{0,1:T(8,128)S(1)}, u32[]{:S(2)}, u32[]{:S(2)}) %collective-permute-start.1) | collective-permute-done | bytes 262176 | tf_op jit(solution)/shard_map/ppermute | solution.py:34
  31.8 1.9 collective-permute-start.6
  33.8 3.6 collective-permute-done.3
  37.6 4.9 %collective-permute-done.6 = f32[256,256]{0,1:T(8,128)S(1)} collective-permute-done((f32[256,256]{0,1:T(8,128)S(1)}, f32[256,256]{0,1:T(8,128)S(1)}, u32[]{:S(2)}, u32[]{:S(2)}) %collective-permute-start.6) | collective-permute-done | bytes 262176 | tf_op jit(solution)/shard_map/ppermute | solution.py:34
  44.6 5.4 %collective-permute-done.7 = f32[2,256,256]{1,2,0:T(8,128)S(1)} collective-permute-done((f32[2,256,256]{1,2,0:T(8,128)S(1)}, f32[2,256,256]{1,2,0:T(8,128)S(1)}, u32[]{:S(2)}, u32[]{:S(2)}) %collective-permute-start.7) | collective-permute-done | bytes 524320 | tf_op jit(solution)/shard_map/ppermute | solution.py:76
  52.7 5.4 %collective-permute-done.8 = f32[2,256,256]{1,2,0:T(8,128)S(1)} collective-permute-done((f32[2,256,256]{1,2,0:T(8,128)S(1)}, f32[2,256,256]{1,2,0:T(8,128)S(1)}, u32[]{:S(2)}, u32[]{:S(2)}) %collective-permute-start.8) | collective-permute-done | bytes 524320 | tf_op jit(solution)/shard_map/ppermute | solution.py:76
  61.5 5.4 %collective-permute-done.9 = f32[2,256,256]{1,2,0:T(8,128)S(1)} collective-permute-done((f32[2,256,256]{1,2,0:T(8,128)S(1)}, f32[2,256,256]{1,2,0:T(8,128)S(1)}, u32[]{:S(2)}, u32[]{:S(2)}) %collective-permute-start.9) | collective-permute-done | bytes 524320 | tf_op jit(solution)/shard_map/ppermute | solution.py:76
  69.6 5.4 %collective-permute-done.10 = f32[2,256,256]{1,2,0:T(8,128)S(1)} collective-permute-done((f32[2,256,256]{1,2,0:T(8,128)S(1)}, f32[2,256,256]{1,2,0:T(8,128)S(1)}, u32[]{:S(2)}, u32[]{:S(2)}) %collective-permute-start.10) | collective-permute-done | bytes 524320 | tf_op jit(solution)/shard_map/ppermute | solution.py:76
  75.7 4.2 %collective-permute-start.11 = (f32[2,256,256]{1,2,0:T(8,128)S(1)}, f32[2,256,256]{1,2,0:T(8,128)}, u32[]{:S(2)}, u32[]{:S(2)}) collective-permute-start(f32[2,256,256]{1,2,0:T(8,128)S(1)} %broadcast_select_fusion.11), channel_id=1, source_target_pairs={{0,1},{1,0},{2,3},{3,2},{4,5},{5,4},{6,7},{7,6},{8,9},{9,8},{10,11... | collective-permute-start | bytes 1572872 | tf_op jit(solution)/shard_map/ppermute | solution.py:80
  79.9 1.8 slice_bitcast_fusion.1
  85.4 11.7 %cholesky.130 = f32[128,128]{1,0:T(8,128)S(1)} custom-call(f32[128,128]{1,0:T(8,128)S(1)} %cholesky.194), custom_call_target="Cholesky" | custom-call | tf_op jit(solution)/shard_map/jit(cholesky)/cholesky | solution.py:104
  97.2 9.8 %custom-call.13 = f32[1,128,128]{1,2,0:T(8,128)S(1)} custom-call(f32[1,128,128]{2,1,0:T(8,128)S(1)} %get-tuple-element.90), custom_call_target="InvertDiagBlocksLowerTriangular" | custom-call | tf_op jit(solution)/shard_map/jit(cholesky)/cholesky | solution.py:104
  109.2 11.7 %cholesky.147 = f32[128,128]{1,0:T(8,128)S(1)} custom-call(f32[128,128]{1,0:T(8,128)S(1)} %convolution_subtract_fusion.3), custom_call_target="Cholesky" | custom-call | tf_op jit(solution)/shard_map/jit(cholesky)/cholesky | solution.py:104
  124.1 9.3 %collective-permute-start.12 = (f32[8,256,256]{1,2,0:T(8,128)S(1)}, f32[8,256,256]{1,2,0:T(8,128)}, u32[]{:S(2)}, u32[]{:S(2)}) collective-permute-start(f32[8,256,256]{1,2,0:T(8,128)S(1)} %slice_bitcast_fusion.1), channel_id=1, source_target_pairs={{0,16},{1,9},{32,48},{33,41},{64,80},{65,73},{96,112},{97,105},{12... | collective-permute-start | bytes 6291464 | tf_op jit(solution)/shard_map/ppermute | solution.py:76
  134.7 1.9 collective-permute-start.17
  136.6 18.5 %collective-permute-done.12 = f32[8,256,256]{1,2,0:T(8,128)} collective-permute-done((f32[8,256,256]{1,2,0:T(8,128)S(1)}, f32[8,256,256]{1,2,0:T(8,128)}, u32[]{:S(2)}, u32[]{:S(2)}) %collective-permute-start.12) | collective-permute-done | bytes 2097184 | tf_op jit(solution)/shard_map/ppermute | solution.py:76
  156.0 16.2 %collective-permute-start.13 = (f32[8,256,256]{1,2,0:T(8,128)S(1)}, f32[8,256,256]{1,2,0:T(8,128)S(1)}, u32[]{:S(2)}, u32[]{:S(2)}) collective-permute-start(f32[8,256,256]{1,2,0:T(8,128)S(1)} %broadcast_select_fusion.2), channel_id=1, source_target_pairs={{0,8},{16,24},{1,17},{9,25},{32,40},{48,56},{33,49},{41,57},{64,72... | collective-permute-start | bytes 6291464 | tf_op jit(solution)/shard_map/ppermute | solution.py:76
  172.2 1.9 maximum_select_fusion
  176.1 20.3 %collective-permute-done.18 = f32[2,256,2,256]{3,2,1,0:T(2,128)S(1)} collective-permute-done((f32[2,256,2,256]{3,2,1,0:T(2,128)S(1)}, f32[2,256,2,256]{3,2,1,0:T(2,128)S(1)}, u32[]{:S(2)}, u32[]{:S(2)}) %collective-permute-start.18) | collective-permute-done | bytes 1048608 | tf_op jit(solution)/shard_map/ppermute | solution.py:19
  196.5 3.6 broadcast_select_fusion
  200.0 2.3 collective-permute-start.19
  204.1 2.6 collective-permute-start.14
  206.7 15.4 %collective-permute-done.19 = f32[2,256,2,256]{3,2,1,0:T(2,128)} collective-permute-done((f32[2,256,2,256]{3,2,1,0:T(2,128)}, f32[2,256,2,256]{3,2,1,0:T(2,128)}, u32[]{:S(2)}, u32[]{:S(2)}) %collective-permute-start.19) | collective-permute-done | bytes 1048608 | tf_op jit(solution)/shard_map/ppermute | solution.py:19
  222.1 1.9 broadcast_select_fusion.1
  225.9 6.1 %while.6 = (s32[]{:T(128)}, f32[256,256]{0,1:T(8,128)}, s32[2,2]{1,0:T(2,128)S(1)}, f32[2,128,128]{2,1,0:T(8,128)S(1)}, s32[]{:T(128)}) while((s32[]{:T(128)}, f32[256,256]{0,1:T(8,128)}, s32[2,2]{1,0:T(2,128)S(1)}, f32[2,128,128]{2,1,0:T(8,128)S(1)}, s32[]{:T(128)}) %tuple.58), condition=%wide.while_cond.2, body=%wide.while_body.2.sunk | while | flops 2 | bytes 393321 | solution.py:109
  226.6 2.3 dynamic-slice.29
  229.7 2.2 dynamic-slice.29
  232.0 19.7 %custom-call.14 = f32[2,128,128]{1,2,0:T(8,128)S(1)} custom-call(f32[2,128,128]{2,1,0:T(8,128)S(1)} %get-tuple-element.47), custom_call_target="InvertDiagBlocksLowerTriangular" | custom-call | tf_op jit(solution)/shard_map/jit(_solve_triangular)/triangular_solve | solution.py:109
  253.5 2.3 broadcast_select_fusion.4
  255.8 2.6 collective-permute-start.15
  261.6 11.7 %cholesky.164 = f32[128,128]{1,0:T(8,128)S(1)} custom-call(f32[128,128]{1,0:T(8,128)S(1)} %cholesky.197), custom_call_target="Cholesky" | custom-call | tf_op jit(solution)/shard_map/jit(cholesky)/cholesky | solution.py:112
  273.4 9.8 %custom-call.15 = f32[1,128,128]{1,2,0:T(8,128)S(1)} custom-call(f32[1,128,128]{2,1,0:T(8,128)S(1)} %get-tuple-element.88), custom_call_target="InvertDiagBlocksLowerTriangular" | custom-call | tf_op jit(solution)/shard_map/jit(cholesky)/cholesky | solution.py:112
  283.9 11.7 %cholesky.181 = f32[128,128]{1,0:T(8,128)S(1)} custom-call(f32[128,128]{1,0:T(8,128)S(1)} %convolution_subtract_fusion.2), custom_call_target="Cholesky" | custom-call | tf_op jit(solution)/shard_map/jit(cholesky)/cholesky | solution.py:112
  299.0 2.6 broadcast_select_fusion.5
  301.5 3.0 collective-permute-start.16
  304.5 4.1 %while.7 = (s32[]{:T(128)}, f32[256,256]{0,1:T(8,128)S(1)}, s32[2,2]{1,0:T(2,128)S(1)}, f32[2,128,128]{2,1,0:T(8,128)S(1)}, s32[]{:T(128)}) while((s32[]{:T(128)}, f32[256,256]{0,1:T(8,128)S(1)}, s32[2,2]{1,0:T(2,128)S(1)}, f32[2,128,128]{2,1,0:T(8,128)S(1)}, s32[]{:T(128)}) %tuple.64), condition=%wide.while_cond.2.clone, body=%wide.while_body.2.clone.sunk | while | flops 2 | bytes 393321 | solution.py:113
  308.6 20.1 %custom-call.16 = f32[2,128,128]{1,2,0:T(8,128)S(1)} custom-call(f32[2,128,128]{2,1,0:T(8,128)S(1)} %get-tuple-element.48), custom_call_target="InvertDiagBlocksLowerTriangular" | custom-call | tf_op jit(solution)/shard_map/jit(_solve_triangular)/triangular_solve | solution.py:113
  330.7 4.5 %convolution_bitcast_fusion = f32[2,256,512,1]{2,1,0,3:T(8,128)} fusion(f32[2,256,512]{1,0,2:T(2,128)S(1)} %copy-done.5, f32[256,256]{1,0:T(8,128)S(1)} %pad_maximum_fusion.2, f32[128,256]{1,0:T(8,128)S(1)} %fusion.41, f32[128,256]{1,0:T(8,128)S(1)} %fusion.36, f32[256,256]{1,0:T(8,128)S(1)} %convolution_negate_fusion), kind=kOutput, calls=%fused_computation.16 | convolution fusion | flops 1611923456 | bytes 2883584 | tf_op jit(solution)/shard_map/cak,bk->cab/dot_general | solution.py:129
  335.2 2.0 broadcast_select_fusion.7
  337.1 13.4 %fusion = f32[8,256,512]{2,1,0:T(8,128)S(1)} fusion(f32[8,256,256]{1,2,0:T(8,128)S(1)} %get-tuple-element.82, f32[8,256,256]{1,2,0:T(8,128)S(1)} %get-tuple-element.81, f32[256,256]{1,0:T(8,128)S(1)} %pad_maximum_fusion.2, f32[128,256]{1,0:T(8,128)S(1)} %fusion.41, f32[128,256]{1,0:T(8,128)S(1)} %fusion.36, f32[256,256]{1,0:T(8,128)S(1)} %convolution_negate_fusion), kind=kOutput, calls=%fused_computation.4 | convolution fusion | flops 6444810240 | bytes 9175040 | tf_op jit(solution)/shard_map/rak,bk->rab/dot_general | solution.py:128
  350.5 1.9 copy-done
  354.0 2.0 copy.37
  356.1 9.3 %subtract_select_fusion = f32[8,256,2,256]{1,3,2,0:T(8,128)S(1)} fusion(f32[2,256,512,1]{2,1,0,3:T(8,128)S(1)} %copy-done.8, f32[8,256,512]{2,1,0:T(8,128)} %copy-done, pred[8,2]{1,0:T(8,128)(4,1)S(1)} %broadcast_and_fusion, f32[1,8,256,1,2,256]{2,5,4,1,3,0:T(8,128)} %copy.12), kind=kOutput, calls=%fused_computation.10 | convolution fusion | flops 6444548096 | bytes 13631504 | tf_op jit(solution)/shard_map/rak,cbk->racb/dot_general | solution.py:130
  365.4 1.9 copy.70
  369.3 7.2 %copy.28 = f32[1,8,256,1,2,256]{5,4,3,2,1,0:T(2,128)} copy(f32[1,8,256,1,2,256]{2,5,4,1,3,0:T(8,128)} %fusion.10) | data formatting | bytes 8388608 | tf_op jit(solution)/shard_map/scatter | solution.py:144
  (152 shorter events, 54.3 us)
Async XLA Ops:
  8.2 13.1 %collective-permute-start = (f32[256,256]{0,1:T(8,128)S(1)}, f32[256,256]{0,1:T(8,128)}, u32[]{:S(2)}, u32[]{:S(2)}) collective-permute-start(f32[256,256]{0,1:T(8,128)S(1)} %slice_bitcast_fusion.9), channel_id=1, source_target_pairs={{0,32},{32,64},{1,33},{33,65}} | collective-permute-start | bytes 786440 | tf_op jit(solution)/shard_map/ppermute | solution.py:34
  14.3 17.5 %collective-permute-start.1 = (f32[256,256]{0,1:T(8,128)S(1)}, f32[256,256]{0,1:T(8,128)S(1)}, u32[]{:S(2)}, u32[]{:S(2)}) collective-permute-start(f32[256,256]{0,1:T(8,128)S(1)} %slice_bitcast_fusion.9), channel_id=1, source_target_pairs={{0,64},{32,96},{1,65},{33,97}} | collective-permute-start | bytes 786440 | tf_op jit(solution)/shard_map/ppermute | solution.py:34
  15.6 18.1 %collective-permute-start.2 = (f32[256,256]{0,1:T(8,128)S(1)}, f32[256,256]{0,1:T(8,128)S(1)}, u32[]{:S(2)}, u32[]{:S(2)}) collective-permute-start(f32[256,256]{0,1:T(8,128)S(1)} %slice_bitcast_fusion.9), channel_id=1, source_target_pairs={{0,96},{32,128},{1,97},{33,129}} | collective-permute-start | bytes 786440 | tf_op jit(solution)/shard_map/ppermute | solution.py:34
  17.3 20.1 %collective-permute-start.3 = (f32[256,256]{0,1:T(8,128)S(1)}, f32[256,256]{0,1:T(8,128)S(1)}, u32[]{:S(2)}, u32[]{:S(2)}) collective-permute-start(f32[256,256]{0,1:T(8,128)S(1)} %slice_bitcast_fusion.9), channel_id=1, source_target_pairs={{0,128},{32,160},{1,129},{33,161}} | collective-permute-start | bytes 786440 | tf_op jit(solution)/shard_map/ppermute | solution.py:34
  18.6 18.8 %collective-permute-start.4 = (f32[256,256]{0,1:T(8,128)S(1)}, f32[256,256]{0,1:T(8,128)S(1)}, u32[]{:S(2)}, u32[]{:S(2)}) collective-permute-start(f32[256,256]{0,1:T(8,128)S(1)} %slice_bitcast_fusion.9), channel_id=1, source_target_pairs={{0,160},{32,192},{1,161},{33,193}} | collective-permute-start | bytes 786440 | tf_op jit(solution)/shard_map/ppermute | solution.py:34
  21.3 16.2 %collective-permute-start.5 = (f32[256,256]{0,1:T(8,128)S(1)}, f32[256,256]{0,1:T(8,128)S(1)}, u32[]{:S(2)}, u32[]{:S(2)}) collective-permute-start(f32[256,256]{0,1:T(8,128)S(1)} %slice_bitcast_fusion.9), channel_id=1, source_target_pairs={{0,192},{32,224},{1,193},{33,225}} | collective-permute-start | bytes 786440 | tf_op jit(solution)/shard_map/ppermute | solution.py:34
  31.8 10.7 %collective-permute-start.6 = (f32[256,256]{0,1:T(8,128)S(1)}, f32[256,256]{0,1:T(8,128)S(1)}, u32[]{:S(2)}, u32[]{:S(2)}) collective-permute-start(f32[256,256]{0,1:T(8,128)S(1)} %slice_bitcast_fusion.9), channel_id=1, source_target_pairs={{0,224},{32,0},{1,225},{33,1}} | collective-permute-start | bytes 786440 | tf_op jit(solution)/shard_map/ppermute | solution.py:34
  33.8 10.2 %copy-start.17 = (s32[2]{0:T(128)S(1)}, s32[2]{0:T(128)}, u32[]{:S(2)}) copy-start(s32[2]{0:T(128)} %constant.194.clone) | copy-start | bytes 28
  37.5 14.5 %copy-start.16 = (s32[4]{0:T(128)S(1)}, s32[4]{0:T(128)}, u32[]{:S(2)}) copy-start(s32[4]{0:T(128)} %constant.195.clone) | copy-start | bytes 52
  42.6 18.2 %copy-start.15 = (s32[8]{0:T(128)S(1)}, s32[8]{0:T(128)}, u32[]{:S(2)}) copy-start(s32[8]{0:T(128)} %constant.196.clone) | copy-start | bytes 100
  42.6 7.4 %collective-permute-start.7 = (f32[2,256,256]{1,2,0:T(8,128)S(1)}, f32[2,256,256]{1,2,0:T(8,128)S(1)}, u32[]{:S(2)}, u32[]{:S(2)}) collective-permute-start(f32[2,256,256]{1,2,0:T(8,128)S(1)} %pad_maximum_fusion.1), channel_id=1, source_target_pairs={{0,16},{1,9},{32,48},{33,41},{64,80},{65,73},{96,112},{97,105},{12... | collective-permute-start | bytes 1572872 | tf_op jit(solution)/shard_map/ppermute | solution.py:76
  50.7 18.2 %copy-start.14 = (s32[16]{0:T(128)S(1)}, s32[16]{0:T(128)}, u32[]{:S(2)}) copy-start(s32[16]{0:T(128)} %constant.197.clone) | copy-start | bytes 196
  50.7 7.4 %collective-permute-start.8 = (f32[2,256,256]{1,2,0:T(8,128)S(1)}, f32[2,256,256]{1,2,0:T(8,128)S(1)}, u32[]{:S(2)}, u32[]{:S(2)}) collective-permute-start(f32[2,256,256]{1,2,0:T(8,128)S(1)} %broadcast_select_fusion.8), channel_id=1, source_target_pairs={{0,8},{16,24},{1,17},{9,25},{32,40},{48,56},{33,49},{41,57},{64,72... | collective-permute-start | bytes 1572872 | tf_op jit(solution)/shard_map/ppermute | solution.py:76
  59.5 7.4 %collective-permute-start.9 = (f32[2,256,256]{1,2,0:T(8,128)S(1)}, f32[2,256,256]{1,2,0:T(8,128)S(1)}, u32[]{:S(2)}, u32[]{:S(2)}) collective-permute-start(f32[2,256,256]{1,2,0:T(8,128)S(1)} %broadcast_select_fusion.9), channel_id=1, source_target_pairs={{0,4},{16,20},{8,12},{24,28},{1,13},{9,5},{17,29},{25,21},{32,36},... | collective-permute-start | bytes 1572872 | tf_op jit(solution)/shard_map/ppermute | solution.py:76
  67.6 7.4 %collective-permute-start.10 = (f32[2,256,256]{1,2,0:T(8,128)S(1)}, f32[2,256,256]{1,2,0:T(8,128)S(1)}, u32[]{:S(2)}, u32[]{:S(2)}) collective-permute-start(f32[2,256,256]{1,2,0:T(8,128)S(1)} %broadcast_select_fusion.10), channel_id=1, source_target_pairs={{0,2},{16,18},{8,10},{24,26},{4,6},{20,22},{12,14},{28,30},{1,15},... | collective-permute-start | bytes 1572872 | tf_op jit(solution)/shard_map/ppermute | solution.py:76
  75.7 6.0 %collective-permute-start.11 = (f32[2,256,256]{1,2,0:T(8,128)S(1)}, f32[2,256,256]{1,2,0:T(8,128)}, u32[]{:S(2)}, u32[]{:S(2)}) collective-permute-start(f32[2,256,256]{1,2,0:T(8,128)S(1)} %broadcast_select_fusion.11), channel_id=1, source_target_pairs={{0,1},{1,0},{2,3},{3,2},{4,5},{5,4},{6,7},{7,6},{8,9},{9,8},{10,11... | collective-permute-start | bytes 1572872 | tf_op jit(solution)/shard_map/ppermute | solution.py:80
  82.8 41.3 %copy-start.1 = (f32[2,256,256]{1,2,0:T(8,128)}, f32[2,256,256]{1,2,0:T(8,128)S(1)}, u32[]{:S(2)}) copy-start(f32[2,256,256]{1,2,0:T(8,128)S(1)} %broadcast_select_fusion.12) | copy-start | bytes 1572868
  84.7 0.7 copy-start.9
  124.1 31.0 %collective-permute-start.12 = (f32[8,256,256]{1,2,0:T(8,128)S(1)}, f32[8,256,256]{1,2,0:T(8,128)}, u32[]{:S(2)}, u32[]{:S(2)}) collective-permute-start(f32[8,256,256]{1,2,0:T(8,128)S(1)} %slice_bitcast_fusion.1), channel_id=1, source_target_pairs={{0,16},{1,9},{32,48},{33,41},{64,80},{65,73},{96,112},{97,105},{12... | collective-permute-start | bytes 6291464 | tf_op jit(solution)/shard_map/ppermute | solution.py:76
  134.7 37.5 %collective-permute-start.17 = (f32[256,2,256]{2,1,0:T(2,128)S(1)}, f32[256,2,256]{2,1,0:T(2,128)}, u32[]{:S(2)}, u32[]{:S(2)}) collective-permute-start(f32[256,2,256]{2,1,0:T(2,128)S(1)} %slice_bitcast_fusion.4), channel_id=1, source_target_pairs={{0,32},{32,0},{1,33},{33,1},{2,34},{34,2},{3,35},{35,3},{4,36},{36... | collective-permute-start | bytes 1572872 | tf_op jit(solution)/shard_map/ppermute | solution.py:12
  155.9 19.5 %copy-start.13 = (s32[2]{0:T(128)S(1)}, s32[2]{0:T(128)}, u32[]{:S(2)}) copy-start(s32[2]{0:T(128)} %constant.198.clone) | copy-start | bytes 28
  156.0 47.1 %collective-permute-start.13 = (f32[8,256,256]{1,2,0:T(8,128)S(1)}, f32[8,256,256]{1,2,0:T(8,128)S(1)}, u32[]{:S(2)}, u32[]{:S(2)}) collective-permute-start(f32[8,256,256]{1,2,0:T(8,128)S(1)} %broadcast_select_fusion.2), channel_id=1, source_target_pairs={{0,8},{16,24},{1,17},{9,25},{32,40},{48,56},{33,49},{41,57},{64,72... | collective-permute-start | bytes 6291464 | tf_op jit(solution)/shard_map/ppermute | solution.py:76
  174.1 28.2 %copy-start.12 = (s32[4]{0:T(128)S(1)}, s32[4]{0:T(128)}, u32[]{:S(2)}) copy-start(s32[4]{0:T(128)} %constant.199.clone) | copy-start | bytes 52
  174.1 22.3 %collective-permute-start.18 = (f32[2,256,2,256]{3,2,1,0:T(2,128)S(1)}, f32[2,256,2,256]{3,2,1,0:T(2,128)S(1)}, u32[]{:S(2)}, u32[]{:S(2)}) collective-permute-start(f32[2,256,2,256]{3,2,1,0:T(2,128)S(1)} %maximum_select_fusion), channel_id=1, source_target_pairs={{0,128},{32,160},{1,129},{33,161},{2,130},{34,162},{3,131},{35,163... | collective-permute-start | bytes 3145736 | tf_op jit(solution)/shard_map/ppermute | solution.py:19
  200.0 22.1 %collective-permute-start.19 = (f32[2,256,2,256]{3,2,1,0:T(2,128)}, f32[2,256,2,256]{3,2,1,0:T(2,128)}, u32[]{:S(2)}, u32[]{:S(2)}) collective-permute-start(f32[2,256,2,256]{3,2,1,0:T(2,128)} %broadcast_select_fusion), channel_id=1, source_target_pairs={{0,64},{32,96},{128,192},{160,224},{1,65},{33,97},{129,193},{161,2... | collective-permute-start | bytes 3145736 | tf_op jit(solution)/shard_map/ppermute | solution.py:19
  204.1 49.4 %collective-permute-start.14 = (f32[8,256,256]{1,2,0:T(8,128)S(1)}, f32[8,256,256]{1,2,0:T(8,128)}, u32[]{:S(2)}, u32[]{:S(2)}) collective-permute-start(f32[8,256,256]{1,2,0:T(8,128)S(1)} %broadcast_select_fusion.3), channel_id=1, source_target_pairs={{0,4},{16,20},{8,12},{24,28},{1,13},{9,5},{17,29},{25,21},{32,36},... | collective-permute-start | bytes 6291464 | tf_op jit(solution)/shard_map/ppermute | solution.py:76
  251.7 0.7 copy-start.10
  253.5 4.9 %copy-start.11 = (f32[2,128,128]{1,2,0:T(8,128)S(1)}, f32[2,128,128]{1,2,0:T(8,128)}, u32[]{:S(2)}) copy-start(f32[2,128,128]{1,2,0:T(8,128)} %copy-done.10) | copy-start | bytes 393220
  253.5 5.9 %copy-start.2 = (f32[2,256,256]{1,2,0:T(8,128)S(1)}, f32[2,256,256]{1,2,0:T(8,128)}, u32[]{:S(2)}) copy-start(f32[2,256,256]{1,2,0:T(8,128)} %copy-done.1) | copy-start | bytes 1572868
  255.8 43.2 %collective-permute-start.15 = (f32[8,256,256]{1,2,0:T(8,128)}, f32[8,256,256]{1,2,0:T(8,128)}, u32[]{:S(2)}, u32[]{:S(2)}) collective-permute-start(f32[8,256,256]{1,2,0:T(8,128)} %broadcast_select_fusion.4), channel_id=1, source_target_pairs={{0,2},{16,18},{8,10},{24,26},{4,6},{20,22},{12,14},{28,30},{1,15},... | collective-permute-start | bytes 6291464 | tf_op jit(solution)/shard_map/ppermute | solution.py:76
  258.7 0.7 copy-start.3
  301.5 27.2 %copy-start.4 = (f32[128,256]{1,0:T(8,128)S(1)}, f32[128,256]{1,0:T(8,128)}, u32[]{:S(2)}) copy-start(f32[128,256]{1,0:T(8,128)} %copy-done.3) | copy-start | bytes 393220
  301.5 33.6 %collective-permute-start.16 = (f32[8,256,256]{1,2,0:T(8,128)S(1)}, f32[8,256,256]{1,2,0:T(8,128)}, u32[]{:S(2)}, u32[]{:S(2)}) collective-permute-start(f32[8,256,256]{1,2,0:T(8,128)S(1)} %broadcast_select_fusion.5), channel_id=1, source_target_pairs={{0,1},{1,0},{2,3},{3,2},{4,5},{5,4},{6,7},{7,6},{8,9},{9,8},{10,11... | collective-permute-start | bytes 6291464 | tf_op jit(solution)/shard_map/ppermute | solution.py:80
  328.7 2.0 copy-start.5
  350.5 1.9 copy-start
  354.0 2.0 copy-start.8
  365.4 2.0 copy-start.6
  365.4 2.0 copy-start.7

commit v6 on v5

--- a/solution.py
+++ b/solution.py
@@ -95,16 +95,14 @@
     first, second = diag_to_first_pcols(tiles[0, :, 0, :], prows, pcols)
     diag_a, diag_b = pcol_broadcast_pair(jnp.stack([first, second]), pcols)
 
-    cols_src = lax.optimization_barrier((tiles[0], first, second))[0]
-    t0, t1 = prow_from_first_two(cols_src, prows)
+    t0, t1 = prow_from_first_two(tiles[0], prows)
 
     a00, a10 = diag_a[0], diag_a[1]
     a11 = diag_b[1]
     eye = jnp.eye(tile, dtype=a00.dtype)
     l00 = jnp.tril(jnp.linalg.cholesky(a00))
 
-    rows_src = lax.optimization_barrier((tiles[:, :, 0, :], l00))[0]
-    col0, col1 = pcol_broadcast_pair(rows_src, pcols)
+    col0, col1 = pcol_broadcast_pair(tiles[:, :, 0, :], pcols)
 
     l00_inv = jax.scipy.linalg.solve_triangular(l00, eye, lower=True)
     l10 = jnp.dot(a10, l00_inv.T, precision=HI)

time: 382 us -> 327 us (0.86)
  waiting for transfers between devices: 92.5 us -> 31.1 us
  local copies, waits for them, and re-layouts: 42.6 us -> 47.7 us
    ppermute x2, waiting for transfers between devices: 35.7 us -> 0.01 us  [prow_from_first_two(): got = lax.ppermute(pair, 'prow', pairs)]
    ppermute x8, waiting for transfers between devices: 40 us -> 19.9 us  [pcol_broadcast_pair(): got = lax.ppermute(buf, 'pcol', pairs)]
    ppermute x2, starting transfers between devices: 7.18 us -> 26.6 us  [pcol_broadcast_pair(): other = lax.ppermute(buf, 'pcol', [(i, i ^ 1) for i in range(pcols)])]
    ppermute x8, starting transfers between devices: 36.1 us -> 18.4 us  [pcol_broadcast_pair(): got = lax.ppermute(buf, 'pcol', pairs)]
    ppermute x7, waiting for transfers between devices: 16.8 us -> 4.96 us  [diag_to_first_pcols(): got.append(lax.ppermute(tile0, ('prow', 'pcol'), pairs))]
    ppermute x1, waiting for transfers between devices: 0.01 us -> 6.28 us  [prow_from_first_two(): other = lax.ppermute(x, 'prow', [(0, 1), (1, 0)])]
    unnamed x46, local copies, waits for them, and re-layouts: 16.9 us -> 20.9 us
  transfers between devices with their start and end apart: 20 -> 20, of which waited for: 10 -> 6; matrix products, arithmetic and copies ran while one was open for 31% -> 50% of each run, Pallas kernels for 0% -> 0%
where the time goes in v6:
time: 327 us; the launch traced here: 321 us
  other arithmetic  136 us (42%)
  starting transfers between devices  67.4 us (21%)
  local copies, waits for them, and re-layouts  47.7 us (15%)
  matrix products  35.2 us (11%)
  waiting for transfers between devices  31.1 us (10%)
  between operations  3.44 us (1%)
    another operation x7, other arithmetic, per_device(): l11 = jnp.tril(jnp.linalg.cholesky(schur))  34.7 us
    another operation x6, other arithmetic, per_device(): l00 = jnp.tril(jnp.linalg.cholesky(a00))  34 us
    ppermute x2, starting transfers between devices, pcol_broadcast_pair(): other = lax.ppermute(buf, 'pcol', [(i, i ^ 1) for i in range(pcols)])  26.6 us
    another operation x2, other arithmetic, per_device(): l11_inv = jax.scipy.linalg.solve_triangular(l11, eye, lower=True)  21.5 us
    unnamed x46, local copies, waits for them, and re-layouts  20.9 us
    another operation x4, other arithmetic, per_device(): l00_inv = jax.scipy.linalg.solve_triangular(l00, eye, lower=True)  20.4 us
    ppermute x8, waiting for transfers between devices, pcol_broadcast_pair(): got = lax.ppermute(buf, 'pcol', pairs)  19.9 us
    ppermute x8, starting transfers between devices, pcol_broadcast_pair(): got = lax.ppermute(buf, 'pcol', pairs)  18.4 us
  transfers between devices with their start and end apart: 20, of which 6 were waited for; matrix products, arithmetic and copies ran while one was open for 50% of the time, Pallas kernels for 0%

profile of v6, /device:TPU:1, one launch (start us, length us, event | category | flops | bytes accessed | tf_op | source)
XLA Modules:
  0.0 321.4 jit_solution(405704207755001047)
XLA Ops:
  0.0 7.2 %copy.12 = f32[1,8,256,1,2,256]{2,5,4,1,3,0:T(8,128)} copy(f32[1,8,256,1,2,256]{5,4,3,2,1,0:T(2,128)} %param.18) | data formatting | bytes 8388608 | tf_op args[0]
  8.2 5.5 %collective-permute-start.5 = (f32[256,256]{0,1:T(8,128)S(1)}, f32[256,256]{0,1:T(8,128)S(1)}, u32[]{:S(2)}, u32[]{:S(2)}) collective-permute-start(f32[256,256]{0,1:T(8,128)S(1)} %slice_bitcast_fusion.10), channel_id=1, source_target_pairs={{0,32},{32,64},{1,33},{33,65}} | collective-permute-start | bytes 786440 | tf_op jit(solution)/shard_map/ppermute | solution.py:34
  15.0 1.7 collective-permute-start.7
  18.0 1.7 collective-permute-start.9
  19.6 3.1 slice_bitcast_fusion.1
  24.0 1.7 bitcast_dynamic-update-slice_fusion.9
  27.7 4.1 %collective-permute-done.6 = f32[256,256]{0,1:T(8,128)S(1)} collective-permute-done((f32[256,256]{0,1:T(8,128)S(1)}, f32[256,256]{0,1:T(8,128)S(1)}, u32[]{:S(2)}, u32[]{:S(2)}) %collective-permute-start.6) | collective-permute-done | bytes 262176 | tf_op jit(solution)/shard_map/ppermute | solution.py:34
  31.8 1.9 collective-permute-start.11
  37.5 4.2 %collective-permute-start.17 = (f32[256,2,256]{2,1,0:T(2,128)S(1)}, f32[256,2,256]{2,1,0:T(2,128)S(1)}, u32[]{:S(2)}, u32[]{:S(2)}) collective-permute-start(f32[256,2,256]{2,1,0:T(2,128)S(1)} %get-tuple-element.82), channel_id=1, source_target_pairs={{0,32},{32,0},{1,33},{33,1},{2,34},{34,2},{3,35},{35,3},{4,36},{36... | collective-permute-start | bytes 1572872 | tf_op jit(solution)/shard_map/ppermute | solution.py:12
  48.3 6.3 %collective-permute-done.17 = f32[256,2,256]{2,1,0:T(2,128)S(1)} collective-permute-done((f32[256,2,256]{2,1,0:T(2,128)S(1)}, f32[256,2,256]{2,1,0:T(2,128)S(1)}, u32[]{:S(2)}, u32[]{:S(2)}) %collective-permute-start.17) | collective-permute-done | bytes 524320 | tf_op jit(solution)/shard_map/ppermute | solution.py:12
  56.4 8.1 %collective-permute-done.12 = f32[2,256,256]{1,2,0:T(8,128)S(1)} collective-permute-done((f32[2,256,256]{1,2,0:T(8,128)S(1)}, f32[2,256,256]{1,2,0:T(8,128)S(1)}, u32[]{:S(2)}, u32[]{:S(2)}) %collective-permute-start.12) | collective-permute-done | bytes 524320 | tf_op jit(solution)/shard_map/ppermute | solution.py:76
  68.0 10.2 %collective-permute-done.13 = f32[2,256,256]{1,2,0:T(8,128)S(1)} collective-permute-done((f32[2,256,256]{1,2,0:T(8,128)S(1)}, f32[2,256,256]{1,2,0:T(8,128)S(1)}, u32[]{:S(2)}, u32[]{:S(2)}) %collective-permute-start.13) | collective-permute-done | bytes 524320 | tf_op jit(solution)/shard_map/ppermute | solution.py:76
  81.7 1.5 broadcast_select_fusion
  83.2 2.3 collective-permute-start.19
  85.4 1.5 collective-permute-done.14
  87.0 1.6 broadcast_select_fusion.10
  88.6 2.1 collective-permute-start.15
  92.3 5.1 %collective-permute-start.1 = (f32[8,256,256]{1,2,0:T(8,128)S(1)}, f32[8,256,256]{1,2,0:T(8,128)}, u32[]{:S(2)}, u32[]{:S(2)}) collective-permute-start(f32[8,256,256]{1,2,0:T(8,128)S(1)} %broadcast_select_fusion.2), channel_id=1, source_target_pairs={{0,8},{16,24},{1,17},{9,25},{32,40},{48,56},{33,49},{41,57},{64,72... | collective-permute-start | bytes 6291464 | tf_op jit(solution)/shard_map/ppermute | solution.py:76
  97.5 1.7 broadcast_select_fusion.11
  99.2 24.1 %collective-permute-start.16 = (f32[2,256,256]{1,2,0:T(8,128)S(1)}, f32[2,256,256]{1,2,0:T(8,128)S(1)}, u32[]{:S(2)}, u32[]{:S(2)}) collective-permute-start(f32[2,256,256]{1,2,0:T(8,128)S(1)} %broadcast_select_fusion.11), channel_id=1, source_target_pairs={{0,1},{1,0},{2,3},{3,2},{4,5},{5,4},{6,7},{7,6},{8,9},{9,8},{10,11... | collective-permute-start | bytes 1572872 | tf_op jit(solution)/shard_map/ppermute | solution.py:80
  126.9 11.7 %cholesky.130 = f32[128,128]{1,0:T(8,128)S(1)} custom-call(f32[128,128]{1,0:T(8,128)S(1)} %cholesky.194), custom_call_target="Cholesky" | custom-call | tf_op jit(solution)/shard_map/jit(cholesky)/cholesky | solution.py:103
  138.7 9.8 %custom-call.13 = f32[1,128,128]{1,2,0:T(8,128)S(1)} custom-call(f32[1,128,128]{2,1,0:T(8,128)S(1)} %get-tuple-element.90), custom_call_target="InvertDiagBlocksLowerTriangular" | custom-call | tf_op jit(solution)/shard_map/jit(cholesky)/cholesky | solution.py:103
  148.7 2.2 broadcast_select_fusion.3
  150.9 2.8 collective-permute-start.2
  154.2 11.7 %cholesky.147 = f32[128,128]{1,0:T(8,128)S(1)} custom-call(f32[128,128]{1,0:T(8,128)S(1)} %convolution_subtract_fusion.3), custom_call_target="Cholesky" | custom-call | tf_op jit(solution)/shard_map/jit(cholesky)/cholesky | solution.py:103
  168.8 4.0 %while.6 = (s32[]{:T(128)}, f32[256,256]{0,1:T(8,128)S(1)}, s32[2,2]{1,0:T(2,128)S(1)}, f32[2,128,128]{2,1,0:T(8,128)S(1)}, s32[]{:T(128)}) while((s32[]{:T(128)}, f32[256,256]{0,1:T(8,128)S(1)}, s32[2,2]{1,0:T(2,128)S(1)}, f32[2,128,128]{2,1,0:T(8,128)S(1)}, s32[]{:T(128)}) %tuple.56), condition=%wide.while_cond.2, body=%wide.while_body.2.sunk | while | flops 2 | bytes 393321 | solution.py:107
  172.8 19.7 %custom-call.14 = f32[2,128,128]{1,2,0:T(8,128)S(1)} custom-call(f32[2,128,128]{2,1,0:T(8,128)S(1)} %get-tuple-element.45), custom_call_target="InvertDiagBlocksLowerTriangular" | custom-call | tf_op jit(solution)/shard_map/jit(_solve_triangular)/triangular_solve | solution.py:107
  193.1 2.7 broadcast_select_fusion.4
  195.9 3.0 collective-permute-start.3
  201.1 11.7 %cholesky.164 = f32[128,128]{1,0:T(8,128)S(1)} custom-call(f32[128,128]{1,0:T(8,128)S(1)} %cholesky.197), custom_call_target="Cholesky" | custom-call | tf_op jit(solution)/shard_map/jit(cholesky)/cholesky | solution.py:110
  213.0 9.8 %custom-call.15 = f32[1,128,128]{1,2,0:T(8,128)S(1)} custom-call(f32[1,128,128]{2,1,0:T(8,128)S(1)} %get-tuple-element.88), custom_call_target="InvertDiagBlocksLowerTriangular" | custom-call | tf_op jit(solution)/shard_map/jit(cholesky)/cholesky | solution.py:110
  223.5 1.8 constant_dynamic-update-slice_fusion
  226.4 11.7 %cholesky.181 = f32[128,128]{1,0:T(8,128)S(1)} custom-call(f32[128,128]{1,0:T(8,128)S(1)} %convolution_subtract_fusion.2), custom_call_target="Cholesky" | custom-call | tf_op jit(solution)/shard_map/jit(cholesky)/cholesky | solution.py:110
  241.5 1.7 fusion.33
  243.2 2.2 broadcast_select_fusion.5
  245.4 2.5 collective-permute-start.4
  247.9 4.4 %while.7 = (s32[]{:T(128)}, f32[256,256]{0,1:T(8,128)S(1)}, s32[2,2]{1,0:T(2,128)S(1)}, f32[2,128,128]{2,1,0:T(8,128)S(1)}, s32[]{:T(128)}) while((s32[]{:T(128)}, f32[256,256]{0,1:T(8,128)S(1)}, s32[2,2]{1,0:T(2,128)S(1)}, f32[2,128,128]{2,1,0:T(8,128)S(1)}, s32[]{:T(128)}) %tuple.62), condition=%wide.while_cond.2.clone, body=%wide.while_body.2.clone.sunk | while | flops 2 | bytes 393321 | solution.py:111
  252.4 19.8 %custom-call.16 = f32[2,128,128]{1,2,0:T(8,128)S(1)} custom-call(f32[2,128,128]{2,1,0:T(8,128)S(1)} %get-tuple-element.46), custom_call_target="InvertDiagBlocksLowerTriangular" | custom-call | tf_op jit(solution)/shard_map/jit(_solve_triangular)/triangular_solve | solution.py:111
  275.3 4.5 %convolution_bitcast_fusion = f32[2,256,512,1]{2,1,0,3:T(8,128)} fusion(f32[2,256,512]{1,0,2:T(2,128)S(1)} %copy-done.6, f32[256,256]{1,0:T(8,128)S(1)} %pad_maximum_fusion.2, f32[128,256]{1,0:T(8,128)S(1)} %fusion.41, f32[128,256]{1,0:T(8,128)S(1)} %fusion.36, f32[256,256]{1,0:T(8,128)S(1)} %convolution_negate_fusion), kind=kOutput, calls=%fused_computation.16 | convolution fusion | flops 1611923456 | bytes 2883584 | tf_op jit(solution)/shard_map/cak,bk->cab/dot_general | solution.py:127
  279.8 2.0 broadcast_select_fusion.7
  281.8 13.4 %fusion = f32[8,256,512]{2,1,0:T(8,128)S(1)} fusion(f32[8,256,256]{1,2,0:T(8,128)S(1)} %get-tuple-element.80, f32[8,256,256]{1,2,0:T(8,128)S(1)} %get-tuple-element.79, f32[256,256]{1,0:T(8,128)S(1)} %pad_maximum_fusion.2, f32[128,256]{1,0:T(8,128)S(1)} %fusion.41, f32[128,256]{1,0:T(8,128)S(1)} %fusion.36, f32[256,256]{1,0:T(8,128)S(1)} %convolution_negate_fusion), kind=kOutput, calls=%fused_computation.4 | convolution fusion | flops 6444810240 | bytes 9175040 | tf_op jit(solution)/shard_map/rak,bk->rab/dot_general | solution.py:126
  295.2 1.9 copy-done.1
  297.2 1.6 constant_dynamic-slice_fusion.2
  298.8 2.0 copy.37
  300.8 9.3 %subtract_select_fusion = f32[8,256,2,256]{1,3,2,0:T(8,128)S(1)} fusion(f32[2,256,512,1]{2,1,0,3:T(8,128)S(1)} %copy-done.9, f32[8,256,512]{2,1,0:T(8,128)} %copy-done.1, pred[8,2]{1,0:T(8,128)(4,1)S(1)} %broadcast_and_fusion, f32[1,8,256,1,2,256]{2,5,4,1,3,0:T(8,128)} %copy.12), kind=kOutput, calls=%fused_computation.10 | convolution fusion | flops 6444548096 | bytes 13631504 | tf_op jit(solution)/shard_map/rak,cbk->racb/dot_general | solution.py:128
  310.1 1.9 copy.70
  312.4 1.7 fusion.10
  314.0 7.2 %copy.28 = f32[1,8,256,1,2,256]{5,4,3,2,1,0:T(2,128)} copy(f32[1,8,256,1,2,256]{2,5,4,1,3,0:T(8,128)} %fusion.10) | data formatting | bytes 8388608 | tf_op jit(solution)/shard_map/scatter | solution.py:142
  (152 shorter events, 52.0 us)
Async XLA Ops:
  8.2 17.5 %collective-permute-start.5 = (f32[256,256]{0,1:T(8,128)S(1)}, f32[256,256]{0,1:T(8,128)S(1)}, u32[]{:S(2)}, u32[]{:S(2)}) collective-permute-start(f32[256,256]{0,1:T(8,128)S(1)} %slice_bitcast_fusion.10), channel_id=1, source_target_pairs={{0,32},{32,64},{1,33},{33,65}} | collective-permute-start | bytes 786440 | tf_op jit(solution)/shard_map/ppermute | solution.py:34
  13.6 18.2 %collective-permute-start.6 = (f32[256,256]{0,1:T(8,128)S(1)}, f32[256,256]{0,1:T(8,128)S(1)}, u32[]{:S(2)}, u32[]{:S(2)}) collective-permute-start(f32[256,256]{0,1:T(8,128)S(1)} %slice_bitcast_fusion.10), channel_id=1, source_target_pairs={{0,64},{32,96},{1,65},{33,97}} | collective-permute-start | bytes 786440 | tf_op jit(solution)/shard_map/ppermute | solution.py:34
  15.0 19.5 %collective-permute-start.7 = (f32[256,256]{0,1:T(8,128)S(1)}, f32[256,256]{0,1:T(8,128)S(1)}, u32[]{:S(2)}, u32[]{:S(2)}) collective-permute-start(f32[256,256]{0,1:T(8,128)S(1)} %slice_bitcast_fusion.10), channel_id=1, source_target_pairs={{0,96},{32,128},{1,97},{33,129}} | collective-permute-start | bytes 786440 | tf_op jit(solution)/shard_map/ppermute | solution.py:34
  16.6 20.8 %collective-permute-start.8 = (f32[256,256]{0,1:T(8,128)S(1)}, f32[256,256]{0,1:T(8,128)S(1)}, u32[]{:S(2)}, u32[]{:S(2)}) collective-permute-start(f32[256,256]{0,1:T(8,128)S(1)} %slice_bitcast_fusion.10), channel_id=1, source_target_pairs={{0,128},{32,160},{1,129},{33,161}} | collective-permute-start | bytes 786440 | tf_op jit(solution)/shard_map/ppermute | solution.py:34
  18.0 24.4 %collective-permute-start.9 = (f32[256,256]{0,1:T(8,128)S(1)}, f32[256,256]{0,1:T(8,128)S(1)}, u32[]{:S(2)}, u32[]{:S(2)}) collective-permute-start(f32[256,256]{0,1:T(8,128)S(1)} %slice_bitcast_fusion.10), channel_id=1, source_target_pairs={{0,160},{32,192},{1,161},{33,193}} | collective-permute-start | bytes 786440 | tf_op jit(solution)/shard_map/ppermute | solution.py:34
  25.7 17.4 %collective-permute-start.10 = (f32[256,256]{0,1:T(8,128)S(1)}, f32[256,256]{0,1:T(8,128)S(1)}, u32[]{:S(2)}, u32[]{:S(2)}) collective-permute-start(f32[256,256]{0,1:T(8,128)S(1)} %slice_bitcast_fusion.10), channel_id=1, source_target_pairs={{0,192},{32,224},{1,193},{33,225}} | collective-permute-start | bytes 786440 | tf_op jit(solution)/shard_map/ppermute | solution.py:34
  31.8 12.0 %collective-permute-start.11 = (f32[256,256]{0,1:T(8,128)S(1)}, f32[256,256]{0,1:T(8,128)S(1)}, u32[]{:S(2)}, u32[]{:S(2)}) collective-permute-start(f32[256,256]{0,1:T(8,128)S(1)} %slice_bitcast_fusion.10), channel_id=1, source_target_pairs={{0,224},{32,0},{1,225},{33,1}} | collective-permute-start | bytes 786440 | tf_op jit(solution)/shard_map/ppermute | solution.py:34
  34.5 56.9 %collective-permute-start = (f32[8,256,256]{1,2,0:T(8,128)}, f32[8,256,256]{1,2,0:T(8,128)S(1)}, u32[]{:S(2)}, u32[]{:S(2)}) collective-permute-start(f32[8,256,256]{1,2,0:T(8,128)} %slice_bitcast_fusion.1), channel_id=1, source_target_pairs={{0,16},{1,9},{32,48},{33,41},{64,80},{65,73},{96,112},{97,105},{12... | collective-permute-start | bytes 6291464 | tf_op jit(solution)/shard_map/ppermute | solution.py:76
  37.4 9.6 %copy-start.17 = (s32[2]{0:T(128)S(1)}, s32[2]{0:T(128)}, u32[]{:S(2)}) copy-start(s32[2]{0:T(128)} %constant.194.clone) | copy-start | bytes 28
  37.5 10.3 %copy-start.16 = (s32[4]{0:T(128)S(1)}, s32[4]{0:T(128)}, u32[]{:S(2)}) copy-start(s32[4]{0:T(128)} %constant.195.clone) | copy-start | bytes 52
  37.5 17.2 %collective-permute-start.17 = (f32[256,2,256]{2,1,0:T(2,128)S(1)}, f32[256,2,256]{2,1,0:T(2,128)S(1)}, u32[]{:S(2)}, u32[]{:S(2)}) collective-permute-start(f32[256,2,256]{2,1,0:T(2,128)S(1)} %get-tuple-element.82), channel_id=1, source_target_pairs={{0,32},{32,0},{1,33},{33,1},{2,34},{34,2},{3,35},{35,3},{4,36},{36... | collective-permute-start | bytes 1572872 | tf_op jit(solution)/shard_map/ppermute | solution.py:12
  45.6 21.0 %copy-start.15 = (s32[8]{0:T(128)S(1)}, s32[8]{0:T(128)}, u32[]{:S(2)}) copy-start(s32[8]{0:T(128)} %constant.196.clone) | copy-start | bytes 100
  45.6 21.7 %copy-start.14 = (s32[16]{0:T(128)S(1)}, s32[16]{0:T(128)}, u32[]{:S(2)}) copy-start(s32[16]{0:T(128)} %constant.197.clone) | copy-start | bytes 196
  45.7 18.9 %collective-permute-start.12 = (f32[2,256,256]{1,2,0:T(8,128)S(1)}, f32[2,256,256]{1,2,0:T(8,128)S(1)}, u32[]{:S(2)}, u32[]{:S(2)}) collective-permute-start(f32[2,256,256]{1,2,0:T(8,128)S(1)} %pad_maximum_fusion.1), channel_id=1, source_target_pairs={{0,16},{1,9},{32,48},{33,41},{64,80},{65,73},{96,112},{97,105},{12... | collective-permute-start | bytes 1572872 | tf_op jit(solution)/shard_map/ppermute | solution.py:76
  55.1 25.8 %copy-start.13 = (s32[2]{0:T(128)S(1)}, s32[2]{0:T(128)}, u32[]{:S(2)}) copy-start(s32[2]{0:T(128)} %constant.198.clone) | copy-start | bytes 28
  55.1 26.6 %collective-permute-start.18 = (f32[2,256,2,256]{3,2,1,0:T(2,128)S(1)}, f32[2,256,2,256]{3,2,1,0:T(2,128)S(1)}, u32[]{:S(2)}, u32[]{:S(2)}) collective-permute-start(f32[2,256,2,256]{3,2,1,0:T(2,128)S(1)} %maximum_select_fusion), channel_id=1, source_target_pairs={{0,128},{32,160},{1,129},{33,161},{2,130},{34,162},{3,131},{35,163... | collective-permute-start | bytes 3145736 | tf_op jit(solution)/shard_map/ppermute | solution.py:19
  65.3 13.0 %collective-permute-start.13 = (f32[2,256,256]{1,2,0:T(8,128)S(1)}, f32[2,256,256]{1,2,0:T(8,128)S(1)}, u32[]{:S(2)}, u32[]{:S(2)}) collective-permute-start(f32[2,256,256]{1,2,0:T(8,128)S(1)} %broadcast_select_fusion.8), channel_id=1, source_target_pairs={{0,8},{16,24},{1,17},{9,25},{32,40},{48,56},{33,49},{41,57},{64,72... | collective-permute-start | bytes 1572872 | tf_op jit(solution)/shard_map/ppermute | solution.py:76
  79.6 7.4 %collective-permute-start.14 = (f32[2,256,256]{1,2,0:T(8,128)S(1)}, f32[2,256,256]{1,2,0:T(8,128)S(1)}, u32[]{:S(2)}, u32[]{:S(2)}) collective-permute-start(f32[2,256,256]{1,2,0:T(8,128)S(1)} %broadcast_select_fusion.9), channel_id=1, source_target_pairs={{0,4},{16,20},{8,12},{24,28},{1,13},{9,5},{17,29},{25,21},{32,36},... | collective-permute-start | bytes 1572872 | tf_op jit(solution)/shard_map/ppermute | solution.py:76
  81.6 9.0 %copy-start.12 = (s32[4]{0:T(128)S(1)}, s32[4]{0:T(128)}, u32[]{:S(2)}) copy-start(s32[4]{0:T(128)} %constant.199.clone) | copy-start | bytes 52
  81.6 9.7 %copy-start = (f32[1,8,256,1,2,256]{2,5,4,1,3,0:T(8,128)S(1)}, f32[1,8,256,1,2,256]{2,5,4,1,3,0:T(8,128)}, u32[]{:S(2)}) copy-start(f32[1,8,256,1,2,256]{2,5,4,1,3,0:T(8,128)} %copy.12) | copy-start | bytes 12582916
  83.2 40.2 %collective-permute-start.19 = (f32[2,256,2,256]{3,2,1,0:T(2,128)S(1)}, f32[2,256,2,256]{3,2,1,0:T(2,128)}, u32[]{:S(2)}, u32[]{:S(2)}) collective-permute-start(f32[2,256,2,256]{3,2,1,0:T(2,128)S(1)} %broadcast_select_fusion), channel_id=1, source_target_pairs={{0,64},{32,96},{128,192},{160,224},{1,65},{33,97},{129,193},{161,2... | collective-permute-start | bytes 3145736 | tf_op jit(solution)/shard_map/ppermute | solution.py:19
  88.6 8.9 %collective-permute-start.15 = (f32[2,256,256]{1,2,0:T(8,128)}, f32[2,256,256]{1,2,0:T(8,128)}, u32[]{:S(2)}, u32[]{:S(2)}) collective-permute-start(f32[2,256,256]{1,2,0:T(8,128)} %broadcast_select_fusion.10), channel_id=1, source_target_pairs={{0,2},{16,18},{8,10},{24,26},{4,6},{20,22},{12,14},{28,30},{1,15},... | collective-permute-start | bytes 1572872 | tf_op jit(solution)/shard_map/ppermute | solution.py:76
  92.3 56.4 %collective-permute-start.1 = (f32[8,256,256]{1,2,0:T(8,128)S(1)}, f32[8,256,256]{1,2,0:T(8,128)}, u32[]{:S(2)}, u32[]{:S(2)}) collective-permute-start(f32[8,256,256]{1,2,0:T(8,128)S(1)} %broadcast_select_fusion.2), channel_id=1, source_target_pairs={{0,8},{16,24},{1,17},{9,25},{32,40},{48,56},{33,49},{41,57},{64,72... | collective-permute-start | bytes 6291464 | tf_op jit(solution)/shard_map/ppermute | solution.py:76
  99.2 26.7 %copy-start.2 = (f32[2,256,256]{1,2,0:T(8,128)}, f32[2,256,256]{1,2,0:T(8,128)S(1)}, u32[]{:S(2)}) copy-start(f32[2,256,256]{1,2,0:T(8,128)S(1)} %broadcast_select_fusion.11) | copy-start | bytes 1572868
  99.2 26.7 %collective-permute-start.16 = (f32[2,256,256]{1,2,0:T(8,128)S(1)}, f32[2,256,256]{1,2,0:T(8,128)S(1)}, u32[]{:S(2)}, u32[]{:S(2)}) collective-permute-start(f32[2,256,256]{1,2,0:T(8,128)S(1)} %broadcast_select_fusion.11), channel_id=1, source_target_pairs={{0,1},{1,0},{2,3},{3,2},{4,5},{5,4},{6,7},{7,6},{8,9},{9,8},{10,11... | collective-permute-start | bytes 1572872 | tf_op jit(solution)/shard_map/ppermute | solution.py:80
  125.9 0.8 copy-start.4
  150.9 42.2 %collective-permute-start.2 = (f32[8,256,256]{1,2,0:T(8,128)}, f32[8,256,256]{1,2,0:T(8,128)}, u32[]{:S(2)}, u32[]{:S(2)}) collective-permute-start(f32[8,256,256]{1,2,0:T(8,128)} %broadcast_select_fusion.3), channel_id=1, source_target_pairs={{0,4},{16,20},{8,12},{24,28},{1,13},{9,5},{17,29},{25,21},{32,36},... | collective-permute-start | bytes 6291464 | tf_op jit(solution)/shard_map/ppermute | solution.py:76
  193.1 6.5 %copy-start.3 = (f32[2,256,256]{1,2,0:T(8,128)S(1)}, f32[2,256,256]{1,2,0:T(8,128)}, u32[]{:S(2)}) copy-start(f32[2,256,256]{1,2,0:T(8,128)} %copy-done.2) | copy-start | bytes 1572868
  193.1 6.5 %copy-start.5 = (f32[2,256,256]{1,2,0:T(8,128)S(1)}, f32[2,256,256]{1,2,0:T(8,128)}, u32[]{:S(2)}) copy-start(f32[2,256,256]{1,2,0:T(8,128)} %copy-done.4) | copy-start | bytes 1572868
  195.9 47.3 %collective-permute-start.3 = (f32[8,256,256]{1,2,0:T(8,128)S(1)}, f32[8,256,256]{1,2,0:T(8,128)}, u32[]{:S(2)}, u32[]{:S(2)}) collective-permute-start(f32[8,256,256]{1,2,0:T(8,128)S(1)} %broadcast_select_fusion.4), channel_id=1, source_target_pairs={{0,2},{16,18},{8,10},{24,26},{4,6},{20,22},{12,14},{28,30},{1,15},... | collective-permute-start | bytes 6291464 | tf_op jit(solution)/shard_map/ppermute | solution.py:76
  200.4 0.7 copy-start.10
  245.4 34.4 %collective-permute-start.4 = (f32[8,256,256]{1,2,0:T(8,128)}, f32[8,256,256]{1,2,0:T(8,128)S(1)}, u32[]{:S(2)}, u32[]{:S(2)}) collective-permute-start(f32[8,256,256]{1,2,0:T(8,128)} %broadcast_select_fusion.5), channel_id=1, source_target_pairs={{0,1},{1,0},{2,3},{3,2},{4,5},{5,4},{6,7},{7,6},{8,9},{9,8},{10,11... | collective-permute-start | bytes 6291464 | tf_op jit(solution)/shard_map/ppermute | solution.py:80
  272.2 0.7 copy-start.11
  272.2 3.1 copy-start.6
  295.2 1.9 copy-start.1
  298.8 2.0 copy-start.9
  310.1 2.0 copy-start.7
  310.1 2.0 copy-start.8

commit v7 on v6

--- a/solution.py
+++ b/solution.py
@@ -123,9 +123,9 @@
     cols_panel = jnp.concatenate(
         [jnp.transpose(t0, (1, 2, 0)), jnp.transpose(t1, (1, 2, 0))], axis=-1
     )
-    rows_solved = jnp.einsum("rak,bk->rab", rows_panel, inverse, precision=HI)
     cols_solved = jnp.einsum("cak,bk->cab", cols_panel, inverse, precision=HI)
-    update = tiles - jnp.einsum("rak,cbk->racb", rows_solved, cols_solved, precision=HI)
+    folded = jnp.einsum("mk,cbm->ckb", inverse, cols_solved, precision=HI)
+    update = tiles - jnp.einsum("rak,ckb->racb", rows_panel, folded, precision=HI)
 
     row_index = jnp.arange(rt, dtype=jnp.int32) * prows + p
     col_index = jnp.arange(ct, dtype=jnp.int32) * pcols + q
@@ -136,7 +136,8 @@
 
     qc = jnp.minimum(q, PANELS - 1)
     pc = jnp.minimum(p, PANELS - 1)
-    panel_vals = lax.dynamic_slice_in_dim(rows_solved, qc * tile, tile, axis=2)
+    inverse_rows = lax.dynamic_slice_in_dim(inverse, qc * tile, tile, axis=0)
+    panel_vals = jnp.einsum("rak,bk->rab", rows_panel, inverse_rows, precision=HI)
     diag_tile = lax.dynamic_slice(factor, (pc * tile, qc * tile), (tile, tile))
     panel_vals = panel_vals.at[0].set(jnp.where(p < PANELS, diag_tile, panel_vals[0]))
     out = out.at[:, :, 0, :].set(jnp.where(q < PANELS, panel_vals, out[:, :, 0, :]))

time: 327 us -> 313 us (0.957)
  matrix products: 35.2 us -> 24.7 us
  local copies, waits for them, and re-layouts: 47.7 us -> 42.3 us
    ppermute x2, starting transfers between devices: 26.6 us -> 13.8 us  [pcol_broadcast_pair(): other = lax.ppermute(buf, 'pcol', [(i, i ^ 1) for i in range(pcols)])]
    dot_general x2 -> x3, matrix products: 22.7 us -> 13.2 us  [the longest x1 7.45 us: per_device(): jnp.einsum('rak,ckb->racb', rows_panel, folded, precision=HI)]
    ppermute x8, waiting for transfers between devices: 19.9 us -> 27.1 us  [pcol_broadcast_pair(): got = lax.ppermute(buf, 'pcol', pairs)]
    ppermute x1, waiting for transfers between devices: 6.28 us -> 0.01 us  [prow_from_first_two(): other = lax.ppermute(x, 'prow', [(0, 1), (1, 0)])]
    unnamed x46 -> x41, local copies, waits for them, and re-layouts: 20.9 us -> 16.2 us
    ppermute x2, starting transfers between devices: 3.61 us -> 7.94 us  [prow_from_first_two(): got = lax.ppermute(pair, 'prow', pairs)]
  transfers between devices with their start and end apart: 20 -> 20, of which waited for: 6 -> 6; matrix products, arithmetic and copies ran while one was open for 50% -> 53% of each run, Pallas kernels for 0% -> 0%
where the time goes in v7:
time: 313 us; the launch traced here: 308 us
  other arithmetic  137 us (44%)
  starting transfers between devices  65.5 us (21%)
  local copies, waits for them, and re-layouts  42.3 us (14%)
  waiting for transfers between devices  34.3 us (11%)
  matrix products  24.7 us (8%)
  between operations  3.72 us (1%)
    another operation x7, other arithmetic, per_device(): l11 = jnp.tril(jnp.linalg.cholesky(schur))  34.7 us
    another operation x6, other arithmetic, per_device(): l00 = jnp.tril(jnp.linalg.cholesky(a00))  34 us
    ppermute x8, waiting for transfers between devices, pcol_broadcast_pair(): got = lax.ppermute(buf, 'pcol', pairs)  27.1 us
    another operation x2, other arithmetic, per_device(): l11_inv = jax.scipy.linalg.solve_triangular(l11, eye, lower=True)  21.6 us
    ppermute x8, starting transfers between devices, pcol_broadcast_pair(): got = lax.ppermute(buf, 'pcol', pairs)  21.5 us
    another operation x4, other arithmetic, per_device(): l00_inv = jax.scipy.linalg.solve_triangular(l00, eye, lower=True)  20.4 us
    ppermute x7, starting transfers between devices, diag_to_first_pcols(): got.append(lax.ppermute(tile0, ('prow', 'pcol'), pairs))  16.6 us
    unnamed x41, local copies, waits for them, and re-layouts  16.2 us
  transfers between devices with their start and end apart: 20, of which 6 were waited for; matrix products, arithmetic and copies ran while one was open for 53% of the time, Pallas kernels for 0%

profile of v7, /device:TPU:1, one launch (start us, length us, event | category | flops | bytes accessed | tf_op | source)
XLA Modules:
  0.0 307.6 jit_solution(18103203601905459973)
XLA Ops:
  0.0 7.2 %copy.12 = f32[1,8,256,1,2,256]{2,5,4,1,3,0:T(8,128)} copy(f32[1,8,256,1,2,256]{5,4,3,2,1,0:T(2,128)} %param.18) | data formatting | bytes 8388608 | tf_op args[0]
  8.2 7.9 %collective-permute-start.14 = (f32[256,256]{0,1:T(8,128)S(1)}, f32[256,256]{0,1:T(8,128)S(1)}, u32[]{:S(2)}, u32[]{:S(2)}) collective-permute-start(f32[256,256]{0,1:T(8,128)S(1)} %slice_bitcast_fusion.10), channel_id=1, source_target_pairs={{0,224},{32,0},{1,225},{33,1}} | collective-permute-start | bytes 786440 | tf_op jit(solution)/shard_map/ppermute | solution.py:34
  20.0 2.2 collective-permute-start.8
  22.2 3.1 %slice_bitcast_fusion.1 = f32[8,256,256]{1,2,0:T(8,128)} fusion(f32[8,256,2,256]{1,3,2,0:T(8,128)} %bitcast.157), kind=kLoop, calls=%fused_computation.13 | loop fusion | bytes 4194304 | tf_op jit(solution)/shard_map/squeeze | solution.py:105
  26.6 1.7 bitcast_dynamic-update-slice_fusion.9
  28.3 4.0 %collective-permute-done.8 = f32[256,256]{0,1:T(8,128)S(1)} collective-permute-done((f32[256,256]{0,1:T(8,128)S(1)}, f32[256,256]{0,1:T(8,128)S(1)}, u32[]{:S(2)}, u32[]{:S(2)}) %collective-permute-start.8) | collective-permute-done | bytes 262176 | tf_op jit(solution)/shard_map/ppermute | solution.py:34
  36.4 1.6 collective-permute-done.10
  38.0 5.5 %collective-permute-start.5 = (f32[256,2,256]{2,1,0:T(2,128)S(1)}, f32[256,2,256]{2,1,0:T(2,128)S(1)}, u32[]{:S(2)}, u32[]{:S(2)}) collective-permute-start(f32[256,2,256]{2,1,0:T(2,128)S(1)} %get-tuple-element.82), channel_id=1, source_target_pairs={{0,32},{32,0},{1,33},{33,1},{2,34},{34,2},{3,35},{35,3},{4,36},{36... | collective-permute-start | bytes 1572872 | tf_op jit(solution)/shard_map/ppermute | solution.py:12
  44.3 1.6 collective-permute-done.11
  45.9 1.4 collective-permute-start
  54.5 5.7 %collective-permute-start.6 = (f32[2,256,2,256]{3,2,1,0:T(2,128)S(1)}, f32[2,256,2,256]{3,2,1,0:T(2,128)S(1)}, u32[]{:S(2)}, u32[]{:S(2)}) collective-permute-start(f32[2,256,2,256]{3,2,1,0:T(2,128)S(1)} %maximum_select_fusion), channel_id=1, source_target_pairs={{0,128},{32,160},{1,129},{33,161},{2,130},{34,162},{3,131},{35,163... | collective-permute-start | bytes 3145736 | tf_op jit(solution)/shard_map/ppermute | solution.py:19
  60.2 15.8 %collective-permute-done.15 = f32[2,256,256]{1,2,0:T(8,128)S(1)} collective-permute-done((f32[2,256,256]{1,2,0:T(8,128)S(1)}, f32[2,256,256]{1,2,0:T(8,128)S(1)}, u32[]{:S(2)}, u32[]{:S(2)}) %collective-permute-start.15) | collective-permute-done | bytes 524320 | tf_op jit(solution)/shard_map/ppermute | solution.py:76
  79.4 9.6 %collective-permute-done.16 = f32[2,256,256]{1,2,0:T(8,128)S(1)} collective-permute-done((f32[2,256,256]{1,2,0:T(8,128)S(1)}, f32[2,256,256]{1,2,0:T(8,128)S(1)}, u32[]{:S(2)}, u32[]{:S(2)}) %collective-permute-start.16) | collective-permute-done | bytes 524320 | tf_op jit(solution)/shard_map/ppermute | solution.py:76
  92.4 1.5 broadcast_select_fusion
  93.8 2.3 collective-permute-start.7
  96.1 1.6 collective-permute-done.17
  97.7 1.5 broadcast_select_fusion.10
  99.2 2.1 collective-permute-start.18
  102.9 5.1 %collective-permute-start.1 = (f32[8,256,256]{1,2,0:T(8,128)S(1)}, f32[8,256,256]{1,2,0:T(8,128)}, u32[]{:S(2)}, u32[]{:S(2)}) collective-permute-start(f32[8,256,256]{1,2,0:T(8,128)S(1)} %broadcast_select_fusion.2), channel_id=1, source_target_pairs={{0,8},{16,24},{1,17},{9,25},{32,40},{48,56},{33,49},{41,57},{64,72... | collective-permute-start | bytes 6291464 | tf_op jit(solution)/shard_map/ppermute | solution.py:76
  108.0 1.8 broadcast_select_fusion.11
  109.8 13.8 %collective-permute-start.19 = (f32[2,256,256]{1,2,0:T(8,128)S(1)}, f32[2,256,256]{1,2,0:T(8,128)S(1)}, u32[]{:S(2)}, u32[]{:S(2)}) collective-permute-start(f32[2,256,256]{1,2,0:T(8,128)S(1)} %broadcast_select_fusion.11), channel_id=1, source_target_pairs={{0,1},{1,0},{2,3},{3,2},{4,5},{5,4},{6,7},{7,6},{8,9},{9,8},{10,11... | collective-permute-start | bytes 1572872 | tf_op jit(solution)/shard_map/ppermute | solution.py:80
  124.8 1.4 pad_maximum_fusion.3
  127.2 11.7 %cholesky.130 = f32[128,128]{1,0:T(8,128)S(1)} custom-call(f32[128,128]{1,0:T(8,128)S(1)} %cholesky.194), custom_call_target="Cholesky" | custom-call | tf_op jit(solution)/shard_map/jit(cholesky)/cholesky | solution.py:103
  139.0 9.8 %custom-call.13 = f32[1,128,128]{1,2,0:T(8,128)S(1)} custom-call(f32[1,128,128]{2,1,0:T(8,128)S(1)} %get-tuple-element.90), custom_call_target="InvertDiagBlocksLowerTriangular" | custom-call | tf_op jit(solution)/shard_map/jit(cholesky)/cholesky | solution.py:103
  149.0 2.2 broadcast_select_fusion.3
  151.3 5.8 %collective-permute-start.2 = (f32[8,256,256]{1,2,0:T(8,128)}, f32[8,256,256]{1,2,0:T(8,128)}, u32[]{:S(2)}, u32[]{:S(2)}) collective-permute-start(f32[8,256,256]{1,2,0:T(8,128)} %broadcast_select_fusion.3), channel_id=1, source_target_pairs={{0,4},{16,20},{8,12},{24,28},{1,13},{9,5},{17,29},{25,21},{32,36},... | collective-permute-start | bytes 6291464 | tf_op jit(solution)/shard_map/ppermute | solution.py:76
  157.5 11.7 %cholesky.147 = f32[128,128]{1,0:T(8,128)S(1)} custom-call(f32[128,128]{1,0:T(8,128)S(1)} %convolution_subtract_fusion.3), custom_call_target="Cholesky" | custom-call | tf_op jit(solution)/shard_map/jit(cholesky)/cholesky | solution.py:103
  172.2 4.4 %while.6 = (s32[]{:T(128)}, f32[256,256]{0,1:T(8,128)S(1)}, s32[2,2]{1,0:T(2,128)S(1)}, f32[2,128,128]{2,1,0:T(8,128)S(1)}, s32[]{:T(128)}) while((s32[]{:T(128)}, f32[256,256]{0,1:T(8,128)S(1)}, s32[2,2]{1,0:T(2,128)S(1)}, f32[2,128,128]{2,1,0:T(8,128)S(1)}, s32[]{:T(128)}) %tuple.56), condition=%wide.while_cond.2, body=%wide.while_body.2.sunk | while | flops 2 | bytes 393329 | solution.py:107
  172.9 1.4 dynamic-slice.28
  176.6 19.7 %custom-call.14 = f32[2,128,128]{1,2,0:T(8,128)S(1)} custom-call(f32[2,128,128]{2,1,0:T(8,128)S(1)} %get-tuple-element.45), custom_call_target="InvertDiagBlocksLowerTriangular" | custom-call | tf_op jit(solution)/shard_map/jit(_solve_triangular)/triangular_solve | solution.py:107
  196.9 2.6 broadcast_select_fusion.4
  199.5 3.1 %collective-permute-start.3 = (f32[8,256,256]{1,2,0:T(8,128)S(1)}, f32[8,256,256]{1,2,0:T(8,128)}, u32[]{:S(2)}, u32[]{:S(2)}) collective-permute-start(f32[8,256,256]{1,2,0:T(8,128)S(1)} %broadcast_select_fusion.4), channel_id=1, source_target_pairs={{0,2},{16,18},{8,10},{24,26},{4,6},{20,22},{12,14},{28,30},{1,15},... | collective-permute-start | bytes 6291464 | tf_op jit(solution)/shard_map/ppermute | solution.py:76
  205.8 11.7 %cholesky.164 = f32[128,128]{1,0:T(8,128)S(1)} custom-call(f32[128,128]{1,0:T(8,128)S(1)} %cholesky.197), custom_call_target="Cholesky" | custom-call | tf_op jit(solution)/shard_map/jit(cholesky)/cholesky | solution.py:110
  217.6 9.8 %custom-call.15 = f32[1,128,128]{1,2,0:T(8,128)S(1)} custom-call(f32[1,128,128]{2,1,0:T(8,128)S(1)} %get-tuple-element.88), custom_call_target="InvertDiagBlocksLowerTriangular" | custom-call | tf_op jit(solution)/shard_map/jit(cholesky)/cholesky | solution.py:110
  228.2 1.8 constant_dynamic-update-slice_fusion
  231.1 11.7 %cholesky.181 = f32[128,128]{1,0:T(8,128)S(1)} custom-call(f32[128,128]{1,0:T(8,128)S(1)} %convolution_subtract_fusion.2), custom_call_target="Cholesky" | custom-call | tf_op jit(solution)/shard_map/jit(cholesky)/cholesky | solution.py:110
  246.2 1.7 fusion.28
  247.9 2.3 broadcast_select_fusion.5
  250.2 4.1 %while.7 = (s32[]{:T(128)}, f32[256,256]{0,1:T(8,128)S(1)}, s32[2,2]{1,0:T(2,128)S(1)}, f32[2,128,128]{2,1,0:T(8,128)S(1)}, s32[]{:T(128)}) while((s32[]{:T(128)}, f32[256,256]{0,1:T(8,128)S(1)}, s32[2,2]{1,0:T(2,128)S(1)}, f32[2,128,128]{2,1,0:T(8,128)S(1)}, s32[]{:T(128)}) %tuple.62), condition=%wide.while_cond.2.clone, body=%wide.while_body.2.clone.sunk | while | flops 2 | bytes 393329 | solution.py:111
  254.3 19.9 %custom-call.16 = f32[2,128,128]{1,2,0:T(8,128)S(1)} custom-call(f32[2,128,128]{2,1,0:T(8,128)S(1)} %get-tuple-element.46), custom_call_target="InvertDiagBlocksLowerTriangular" | custom-call | tf_op jit(solution)/shard_map/jit(_solve_triangular)/triangular_solve | solution.py:111
  277.4 3.5 %fusion.9 = f32[2,256,512]{2,1,0:T(8,128)S(1)} fusion(f32[2,256,512]{1,0,2:T(2,128)S(1)} %copy-done.6, f32[256,256]{1,0:T(8,128)S(1)} %pad_maximum_fusion.5, f32[128,256]{1,0:T(8,128)S(1)} %fusion.36, f32[128,256]{1,0:T(8,128)S(1)} %fusion.31, f32[256,256]{1,0:T(8,128)S(1)} %convolution_negate_fusion), kind=kOutput, calls=%fused_computation.28 | convolution fusion | flops 1611923456 | bytes 2883584 | tf_op jit(solution)/shard_map/cak,bk->cab/dot_general | solution.py:126
  280.9 1.9 convolution_bitcast_fusion
  282.8 2.0 broadcast_select_fusion.7
  284.8 3.9 %fusion.2 = f32[8,256,256]{1,2,0:T(8,128)S(1)} fusion(f32[8,256,256]{1,2,0:T(8,128)S(1)} %get-tuple-element.80, f32[8,256,256]{1,2,0:T(8,128)S(1)} %get-tuple-element.79, f32[512,512]{1,0:T(8,128)S(1)} %select_maximum_fusion, s32[]{:T(128)S(6)} %select_n.182), kind=kOutput, calls=%fused_computation.8 | convolution fusion | flops 3222274048 | bytes 6815748 | tf_op jit(solution)/shard_map/rak,bk->rab/dot_general | solution.py:140
  288.7 7.5 %subtract_select_fusion = f32[8,256,2,256]{1,3,2,0:T(8,128)S(1)} fusion(pred[8,2]{1,0:T(8,128)(4,1)S(1)} %broadcast_and_fusion, f32[2,512,256,1]{2,1,0,3:T(8,128)S(1)} %convolution_bitcast_fusion, f32[8,256,256]{1,2,0:T(8,128)S(1)} %get-tuple-element.80, f32[8,256,256]{1,2,0:T(8,128)S(1)} %get-tuple-element.79, f32[1,8,256,1,2,256]{2,5,4,1,3,0:T(8,128)S(1)} %copy-done.1), kind=kOutput, calls=%fused_computation.7 | convolution fusion | flops 6445596672 | bytes 13631504 | tf_op jit(solution)/shard_map/rak,ckb->racb/dot_general | solution.py:128
  296.2 1.9 copy.74
  298.4 1.6 fusion.5
  300.0 7.2 %copy.30 = f32[1,8,256,1,2,256]{5,4,3,2,1,0:T(2,128)} copy(f32[1,8,256,1,2,256]{2,5,4,1,3,0:T(8,128)} %fusion.5) | data formatting | bytes 8388608 | tf_op jit(solution)/shard_map/scatter | solution.py:143
  (148 shorter events, 49.1 us)
Async XLA Ops:
  8.2 41.3 %collective-permute-start.14 = (f32[256,256]{0,1:T(8,128)S(1)}, f32[256,256]{0,1:T(8,128)S(1)}, u32[]{:S(2)}, u32[]{:S(2)}) collective-permute-start(f32[256,256]{0,1:T(8,128)S(1)} %slice_bitcast_fusion.10), channel_id=1, source_target_pairs={{0,224},{32,0},{1,225},{33,1}} | collective-permute-start | bytes 786440 | tf_op jit(solution)/shard_map/ppermute | solution.py:34
  16.1 32.7 %collective-permute-start.13 = (f32[256,256]{0,1:T(8,128)S(1)}, f32[256,256]{0,1:T(8,128)S(1)}, u32[]{:S(2)}, u32[]{:S(2)}) collective-permute-start(f32[256,256]{0,1:T(8,128)S(1)} %slice_bitcast_fusion.10), channel_id=1, source_target_pairs={{0,192},{32,224},{1,193},{33,225}} | collective-permute-start | bytes 786440 | tf_op jit(solution)/shard_map/ppermute | solution.py:34
  17.4 30.6 %collective-permute-start.12 = (f32[256,256]{0,1:T(8,128)S(1)}, f32[256,256]{0,1:T(8,128)S(1)}, u32[]{:S(2)}, u32[]{:S(2)}) collective-permute-start(f32[256,256]{0,1:T(8,128)S(1)} %slice_bitcast_fusion.10), channel_id=1, source_target_pairs={{0,160},{32,192},{1,161},{33,193}} | collective-permute-start | bytes 786440 | tf_op jit(solution)/shard_map/ppermute | solution.py:34
  18.7 15.6 %collective-permute-start.9 = (f32[256,256]{0,1:T(8,128)S(1)}, f32[256,256]{0,1:T(8,128)S(1)}, u32[]{:S(2)}, u32[]{:S(2)}) collective-permute-start(f32[256,256]{0,1:T(8,128)S(1)} %slice_bitcast_fusion.10), channel_id=1, source_target_pairs={{0,64},{32,96},{1,65},{33,97}} | collective-permute-start | bytes 786440 | tf_op jit(solution)/shard_map/ppermute | solution.py:34
  20.0 12.3 %collective-permute-start.8 = (f32[256,256]{0,1:T(8,128)S(1)}, f32[256,256]{0,1:T(8,128)S(1)}, u32[]{:S(2)}, u32[]{:S(2)}) collective-permute-start(f32[256,256]{0,1:T(8,128)S(1)} %slice_bitcast_fusion.10), channel_id=1, source_target_pairs={{0,32},{32,64},{1,33},{33,65}} | collective-permute-start | bytes 786440 | tf_op jit(solution)/shard_map/ppermute | solution.py:34
  32.3 5.7 %collective-permute-start.10 = (f32[256,256]{0,1:T(8,128)S(1)}, f32[256,256]{0,1:T(8,128)S(1)}, u32[]{:S(2)}, u32[]{:S(2)}) collective-permute-start(f32[256,256]{0,1:T(8,128)S(1)} %slice_bitcast_fusion.10), channel_id=1, source_target_pairs={{0,96},{32,128},{1,97},{33,129}} | collective-permute-start | bytes 786440 | tf_op jit(solution)/shard_map/ppermute | solution.py:34
  34.3 11.5 %collective-permute-start.11 = (f32[256,256]{0,1:T(8,128)S(1)}, f32[256,256]{0,1:T(8,128)S(1)}, u32[]{:S(2)}, u32[]{:S(2)}) collective-permute-start(f32[256,256]{0,1:T(8,128)S(1)} %slice_bitcast_fusion.10), channel_id=1, source_target_pairs={{0,128},{32,160},{1,129},{33,161}} | collective-permute-start | bytes 786440 | tf_op jit(solution)/shard_map/ppermute | solution.py:34
  38.0 16.0 %collective-permute-start.5 = (f32[256,2,256]{2,1,0:T(2,128)S(1)}, f32[256,2,256]{2,1,0:T(2,128)S(1)}, u32[]{:S(2)}, u32[]{:S(2)}) collective-permute-start(f32[256,2,256]{2,1,0:T(2,128)S(1)} %get-tuple-element.82), channel_id=1, source_target_pairs={{0,32},{32,0},{1,33},{33,1},{2,34},{34,2},{3,35},{35,3},{4,36},{36... | collective-permute-start | bytes 1572872 | tf_op jit(solution)/shard_map/ppermute | solution.py:12
  44.3 8.4 %copy-start.15 = (s32[4]{0:T(128)S(1)}, s32[4]{0:T(128)}, u32[]{:S(2)}) copy-start(s32[4]{0:T(128)} %constant.182.clone) | copy-start | bytes 52
  44.3 9.0 %copy-start.14 = (s32[2]{0:T(128)S(1)}, s32[2]{0:T(128)}, u32[]{:S(2)}) copy-start(s32[2]{0:T(128)} %constant.177.clone) | copy-start | bytes 28
  45.9 56.1 %collective-permute-start = (f32[8,256,256]{1,2,0:T(8,128)}, f32[8,256,256]{1,2,0:T(8,128)S(1)}, u32[]{:S(2)}, u32[]{:S(2)}) collective-permute-start(f32[8,256,256]{1,2,0:T(8,128)} %slice_bitcast_fusion.1), channel_id=1, source_target_pairs={{0,16},{1,9},{32,48},{33,41},{64,80},{65,73},{96,112},{97,105},{12... | collective-permute-start | bytes 6291464 | tf_op jit(solution)/shard_map/ppermute | solution.py:76
  51.3 26.7 %copy-start.13 = (s32[2]{0:T(128)S(1)}, s32[2]{0:T(128)}, u32[]{:S(2)}) copy-start(s32[2]{0:T(128)} %constant.181.clone) | copy-start | bytes 28
  51.3 27.4 %copy-start.12 = (s32[4]{0:T(128)S(1)}, s32[4]{0:T(128)}, u32[]{:S(2)}) copy-start(s32[4]{0:T(128)} %constant.178.clone) | copy-start | bytes 52
  51.3 24.6 %collective-permute-start.15 = (f32[2,256,256]{1,2,0:T(8,128)S(1)}, f32[2,256,256]{1,2,0:T(8,128)S(1)}, u32[]{:S(2)}, u32[]{:S(2)}) collective-permute-start(f32[2,256,256]{1,2,0:T(8,128)S(1)} %pad_maximum_fusion.4), channel_id=1, source_target_pairs={{0,16},{1,9},{32,48},{33,41},{64,80},{65,73},{96,112},{97,105},{12... | collective-permute-start | bytes 1572872 | tf_op jit(solution)/shard_map/ppermute | solution.py:76
  54.5 37.2 %copy-start.11 = (s32[8]{0:T(128)S(1)}, s32[8]{0:T(128)}, u32[]{:S(2)}) copy-start(s32[8]{0:T(128)} %constant.179.clone) | copy-start | bytes 100
  54.5 37.9 %collective-permute-start.6 = (f32[2,256,2,256]{3,2,1,0:T(2,128)S(1)}, f32[2,256,2,256]{3,2,1,0:T(2,128)S(1)}, u32[]{:S(2)}, u32[]{:S(2)}) collective-permute-start(f32[2,256,2,256]{3,2,1,0:T(2,128)S(1)} %maximum_select_fusion), channel_id=1, source_target_pairs={{0,128},{32,160},{1,129},{33,161},{2,130},{34,162},{3,131},{35,163... | collective-permute-start | bytes 3145736 | tf_op jit(solution)/shard_map/ppermute | solution.py:19
  76.6 12.4 %collective-permute-start.16 = (f32[2,256,256]{1,2,0:T(8,128)S(1)}, f32[2,256,256]{1,2,0:T(8,128)S(1)}, u32[]{:S(2)}, u32[]{:S(2)}) collective-permute-start(f32[2,256,256]{1,2,0:T(8,128)S(1)} %broadcast_select_fusion.8), channel_id=1, source_target_pairs={{0,8},{16,24},{1,17},{9,25},{32,40},{48,56},{33,49},{41,57},{64,72... | collective-permute-start | bytes 1572872 | tf_op jit(solution)/shard_map/ppermute | solution.py:76
  90.3 7.4 %collective-permute-start.17 = (f32[2,256,256]{1,2,0:T(8,128)S(1)}, f32[2,256,256]{1,2,0:T(8,128)S(1)}, u32[]{:S(2)}, u32[]{:S(2)}) collective-permute-start(f32[2,256,256]{1,2,0:T(8,128)S(1)} %broadcast_select_fusion.9), channel_id=1, source_target_pairs={{0,4},{16,20},{8,12},{24,28},{1,13},{9,5},{17,29},{25,21},{32,36},... | collective-permute-start | bytes 1572872 | tf_op jit(solution)/shard_map/ppermute | solution.py:76
  92.3 8.9 %copy-start.10 = (s32[16]{0:T(128)S(1)}, s32[16]{0:T(128)}, u32[]{:S(2)}) copy-start(s32[16]{0:T(128)} %constant.180.clone) | copy-start | bytes 196
  92.4 9.6 %copy-start = (f32[1,8,256,1,2,256]{2,5,4,1,3,0:T(8,128)S(1)}, f32[1,8,256,1,2,256]{2,5,4,1,3,0:T(8,128)}, u32[]{:S(2)}) copy-start(f32[1,8,256,1,2,256]{2,5,4,1,3,0:T(8,128)} %copy.12) | copy-start | bytes 12582916
  93.8 29.8 %collective-permute-start.7 = (f32[2,256,2,256]{3,2,1,0:T(2,128)S(1)}, f32[2,256,2,256]{3,2,1,0:T(2,128)}, u32[]{:S(2)}, u32[]{:S(2)}) collective-permute-start(f32[2,256,2,256]{3,2,1,0:T(2,128)S(1)} %broadcast_select_fusion), channel_id=1, source_target_pairs={{0,64},{32,96},{128,192},{160,224},{1,65},{33,97},{129,193},{161,2... | collective-permute-start | bytes 3145736 | tf_op jit(solution)/shard_map/ppermute | solution.py:19
  99.2 8.8 %collective-permute-start.18 = (f32[2,256,256]{1,2,0:T(8,128)}, f32[2,256,256]{1,2,0:T(8,128)}, u32[]{:S(2)}, u32[]{:S(2)}) collective-permute-start(f32[2,256,256]{1,2,0:T(8,128)} %broadcast_select_fusion.10), channel_id=1, source_target_pairs={{0,2},{16,18},{8,10},{24,26},{4,6},{20,22},{12,14},{28,30},{1,15},... | collective-permute-start | bytes 1572872 | tf_op jit(solution)/shard_map/ppermute | solution.py:76
  102.9 46.1 %collective-permute-start.1 = (f32[8,256,256]{1,2,0:T(8,128)S(1)}, f32[8,256,256]{1,2,0:T(8,128)}, u32[]{:S(2)}, u32[]{:S(2)}) collective-permute-start(f32[8,256,256]{1,2,0:T(8,128)S(1)} %broadcast_select_fusion.2), channel_id=1, source_target_pairs={{0,8},{16,24},{1,17},{9,25},{32,40},{48,56},{33,49},{41,57},{64,72... | collective-permute-start | bytes 6291464 | tf_op jit(solution)/shard_map/ppermute | solution.py:76
  109.8 16.4 %copy-start.2 = (f32[2,256,256]{1,2,0:T(8,128)}, f32[2,256,256]{1,2,0:T(8,128)S(1)}, u32[]{:S(2)}) copy-start(f32[2,256,256]{1,2,0:T(8,128)S(1)} %broadcast_select_fusion.11) | copy-start | bytes 1572868
  109.8 16.4 %collective-permute-start.19 = (f32[2,256,256]{1,2,0:T(8,128)S(1)}, f32[2,256,256]{1,2,0:T(8,128)S(1)}, u32[]{:S(2)}, u32[]{:S(2)}) collective-permute-start(f32[2,256,256]{1,2,0:T(8,128)S(1)} %broadcast_select_fusion.11), channel_id=1, source_target_pairs={{0,1},{1,0},{2,3},{3,2},{4,5},{5,4},{6,7},{7,6},{8,9},{9,8},{10,11... | collective-permute-start | bytes 1572872 | tf_op jit(solution)/shard_map/ppermute | solution.py:80
  126.2 0.8 copy-start.4
  151.3 45.7 %collective-permute-start.2 = (f32[8,256,256]{1,2,0:T(8,128)}, f32[8,256,256]{1,2,0:T(8,128)}, u32[]{:S(2)}, u32[]{:S(2)}) collective-permute-start(f32[8,256,256]{1,2,0:T(8,128)} %broadcast_select_fusion.3), channel_id=1, source_target_pairs={{0,4},{16,20},{8,12},{24,28},{1,13},{9,5},{17,29},{25,21},{32,36},... | collective-permute-start | bytes 6291464 | tf_op jit(solution)/shard_map/ppermute | solution.py:76
  196.9 6.5 %copy-start.3 = (f32[2,256,256]{1,2,0:T(8,128)S(1)}, f32[2,256,256]{1,2,0:T(8,128)}, u32[]{:S(2)}) copy-start(f32[2,256,256]{1,2,0:T(8,128)} %copy-done.2) | copy-start | bytes 1572868
  196.9 6.5 %copy-start.5 = (f32[2,256,256]{1,2,0:T(8,128)S(1)}, f32[2,256,256]{1,2,0:T(8,128)}, u32[]{:S(2)}) copy-start(f32[2,256,256]{1,2,0:T(8,128)} %copy-done.4) | copy-start | bytes 1572868
  199.5 48.4 %collective-permute-start.3 = (f32[8,256,256]{1,2,0:T(8,128)S(1)}, f32[8,256,256]{1,2,0:T(8,128)}, u32[]{:S(2)}, u32[]{:S(2)}) collective-permute-start(f32[8,256,256]{1,2,0:T(8,128)S(1)} %broadcast_select_fusion.4), channel_id=1, source_target_pairs={{0,2},{16,18},{8,10},{24,26},{4,6},{20,22},{12,14},{28,30},{1,15},... | collective-permute-start | bytes 6291464 | tf_op jit(solution)/shard_map/ppermute | solution.py:76
  250.2 32.7 %collective-permute-start.4 = (f32[8,256,256]{1,2,0:T(8,128)}, f32[8,256,256]{1,2,0:T(8,128)S(1)}, u32[]{:S(2)}, u32[]{:S(2)}) collective-permute-start(f32[8,256,256]{1,2,0:T(8,128)} %broadcast_select_fusion.5), channel_id=1, source_target_pairs={{0,1},{1,0},{2,3},{3,2},{4,5},{5,4},{6,7},{7,6},{8,9},{9,8},{10,11... | collective-permute-start | bytes 6291464 | tf_op jit(solution)/shard_map/ppermute | solution.py:80
  274.2 0.7 copy-start.9
  274.8 2.6 copy-start.6
  284.8 3.9 %copy-start.1 = (f32[1,8,256,1,2,256]{2,5,4,1,3,0:T(8,128)S(1)}, f32[1,8,256,1,2,256]{2,5,4,1,3,0:T(8,128)}, u32[]{:S(2)}) copy-start(f32[1,8,256,1,2,256]{2,5,4,1,3,0:T(8,128)} %copy.12) | copy-start | bytes 12582916
  296.2 2.0 copy-start.7
  296.2 2.0 copy-start.8

commit v8 on v7

--- a/solution.py
+++ b/solution.py
@@ -82,6 +82,18 @@
     return jnp.where(core0, buf, other), jnp.where(core0, other, buf)
 
 
+def lower_inverse(factor):
+    h = factor.shape[0] // 2
+    eye = jnp.eye(h, dtype=factor.dtype)
+    top = jax.scipy.linalg.solve_triangular(factor[:h, :h], eye, lower=True)
+    bottom = jax.scipy.linalg.solve_triangular(factor[h:, h:], eye, lower=True)
+    low = -jnp.dot(bottom, jnp.dot(factor[h:, :h], top, precision=HI), precision=HI)
+    zero = jnp.zeros_like(eye)
+    return jnp.concatenate(
+        [jnp.concatenate([top, zero], axis=1), jnp.concatenate([low, bottom], axis=1)], axis=0
+    )
+
+
 def per_device(covariance):
     prows = lax.axis_size("prow")
     pcols = lax.axis_size("pcol")
@@ -104,11 +116,11 @@
 
     col0, col1 = pcol_broadcast_pair(tiles[:, :, 0, :], pcols)
 
-    l00_inv = jax.scipy.linalg.solve_triangular(l00, eye, lower=True)
+    l00_inv = lower_inverse(l00)
     l10 = jnp.dot(a10, l00_inv.T, precision=HI)
     schur = a11 - jnp.dot(l10, l10.T, precision=HI)
     l11 = jnp.tril(jnp.linalg.cholesky(schur))
-    l11_inv = jax.scipy.linalg.solve_triangular(l11, eye, lower=True)
+    l11_inv = lower_inverse(l11)
     low_inv = -jnp.dot(l11_inv, jnp.dot(l10, l00_inv, precision=HI), precision=HI)
     zero = jnp.zeros_like(eye)
     factor = jnp.concatenate(

time: 313 us -> 316 us (level)
  the two profiles are of different devices: /device:TPU:1 before, /device:TPU:5 now
where the time goes in v8:
time: 316 us; the launch traced here: 310 us
  other arithmetic  137 us (43%)
  starting transfers between devices  67.2 us (21%)
  local copies, waits for them, and re-layouts  36 us (11%)
  waiting for transfers between devices  35.6 us (11%)
  matrix products  30.7 us (10%)
  between operations  3.53 us (1%)
    another operation x7, other arithmetic, per_device(): l11 = jnp.tril(jnp.linalg.cholesky(schur))  34.7 us
    another operation x6, other arithmetic, per_device(): l00 = jnp.tril(jnp.linalg.cholesky(a00))  34 us
    ppermute x2, starting transfers between devices, pcol_broadcast_pair(): other = lax.ppermute(buf, 'pcol', [(i, i ^ 1) for i in range(pcols)])  27.1 us
    another operation x3, other arithmetic, lower_inverse(): bottom = jax.scipy.linalg.solve_triangular(factor[h:, h:], eye, lower=True)  20.5 us
    another operation x3, other arithmetic, lower_inverse(): top = jax.scipy.linalg.solve_triangular(factor[:h, :h], eye, lower=True)  20.4 us
    unnamed x45, local copies, waits for them, and re-layouts  19.1 us
    ppermute x8, starting transfers between devices, pcol_broadcast_pair(): got = lax.ppermute(buf, 'pcol', pairs)  17.2 us
    ppermute x7, waiting for transfers between devices, diag_to_first_pcols(): got.append(lax.ppermute(tile0, ('prow', 'pcol'), pairs))  16 us
  transfers between devices with their start and end apart: 20, of which 7 were waited for; matrix products, arithmetic and copies ran while one was open for 48% of the time, Pallas kernels for 0%

profile of v8, /device:TPU:5, one launch (start us, length us, event | category | flops | bytes accessed | tf_op | source)
XLA Modules:
  0.0 310.0 jit_solution(12304695315231745810)
XLA Ops:
  0.0 7.2 %copy.12 = f32[1,8,256,1,2,256]{2,5,4,1,3,0:T(8,128)} copy(f32[1,8,256,1,2,256]{5,4,3,2,1,0:T(2,128)} %param.18) | data formatting | bytes 8388608 | tf_op args[0]
  9.5 4.6 %collective-permute-start.13 = (f32[256,256]{0,1:T(8,128)S(1)}, f32[256,256]{0,1:T(8,128)S(1)}, u32[]{:S(2)}, u32[]{:S(2)}) collective-permute-start(f32[256,256]{0,1:T(8,128)S(1)} %slice_bitcast_fusion.10), channel_id=1, source_target_pairs={{0,192},{32,224},{1,193},{33,225}} | collective-permute-start | bytes 786440 | tf_op jit(solution)/shard_map/ppermute | solution.py:34
  16.7 1.9 collective-permute-start.8
  20.0 1.7 bitcast_dynamic-update-slice_fusion.7
  21.7 10.8 %collective-permute-done.8 = f32[256,256]{0,1:T(8,128)S(1)} collective-permute-done((f32[256,256]{0,1:T(8,128)S(1)}, f32[256,256]{0,1:T(8,128)S(1)}, u32[]{:S(2)}, u32[]{:S(2)}) %collective-permute-start.8) | collective-permute-done | bytes 262176 | tf_op jit(solution)/shard_map/ppermute | solution.py:34
  36.5 1.6 collective-permute-done.10
  38.1 1.9 collective-permute-start.5
  40.7 3.6 %collective-permute-done.11 = f32[256,256]{0,1:T(8,128)S(1)} collective-permute-done((f32[256,256]{0,1:T(8,128)S(1)}, f32[256,256]{0,1:T(8,128)S(1)}, u32[]{:S(2)}, u32[]{:S(2)}) %collective-permute-start.11) | collective-permute-done | bytes 262176 | tf_op jit(solution)/shard_map/ppermute | solution.py:34
  49.7 1.5 slice_bitcast_fusion.1
  51.2 2.7 collective-permute-start
  55.1 5.7 %collective-permute-start.6 = (f32[2,256,2,256]{3,2,1,0:T(2,128)S(1)}, f32[2,256,2,256]{3,2,1,0:T(2,128)S(1)}, u32[]{:S(2)}, u32[]{:S(2)}) collective-permute-start(f32[2,256,2,256]{3,2,1,0:T(2,128)S(1)} %maximum_select_fusion), channel_id=1, source_target_pairs={{0,128},{32,160},{1,129},{33,161},{2,130},{34,162},{3,131},{35,163... | collective-permute-start | bytes 3145736 | tf_op jit(solution)/shard_map/ppermute | solution.py:19
  63.6 10.9 %collective-permute-done.16 = f32[2,256,256]{1,2,0:T(8,128)S(1)} collective-permute-done((f32[2,256,256]{1,2,0:T(8,128)S(1)}, f32[2,256,256]{1,2,0:T(8,128)S(1)}, u32[]{:S(2)}, u32[]{:S(2)}) %collective-permute-start.16) | collective-permute-done | bytes 524320 | tf_op jit(solution)/shard_map/ppermute | solution.py:76
  74.5 1.4 broadcast_select_fusion.9
  78.6 4.1 %collective-permute-done.6 = f32[2,256,2,256]{3,2,1,0:T(2,128)S(1)} collective-permute-done((f32[2,256,2,256]{3,2,1,0:T(2,128)S(1)}, f32[2,256,2,256]{3,2,1,0:T(2,128)S(1)}, u32[]{:S(2)}, u32[]{:S(2)}) %collective-permute-start.6) | collective-permute-done | bytes 1048608 | tf_op jit(solution)/shard_map/ppermute | solution.py:19
  84.0 2.3 collective-permute-start.7
  86.3 1.6 broadcast_select_fusion.10
  87.9 2.1 collective-permute-start.18
  91.6 2.6 collective-permute-start.1
  95.6 1.8 broadcast_select_fusion.11
  97.4 5.5 %collective-permute-start.19 = (f32[2,256,256]{1,2,0:T(8,128)S(1)}, f32[2,256,256]{1,2,0:T(8,128)S(1)}, u32[]{:S(2)}, u32[]{:S(2)}) collective-permute-start(f32[2,256,256]{1,2,0:T(8,128)S(1)} %broadcast_select_fusion.11), channel_id=1, source_target_pairs={{0,1},{1,0},{2,3},{3,2},{4,5},{5,4},{6,7},{7,6},{8,9},{9,8},{10,11... | collective-permute-start | bytes 1572872 | tf_op jit(solution)/shard_map/ppermute | solution.py:80
  102.9 3.9 %collective-permute-done.7 = f32[2,256,2,256]{3,2,1,0:T(2,128)} collective-permute-done((f32[2,256,2,256]{3,2,1,0:T(2,128)S(1)}, f32[2,256,2,256]{3,2,1,0:T(2,128)}, u32[]{:S(2)}, u32[]{:S(2)}) %collective-permute-start.7) | collective-permute-done | bytes 1048608 | tf_op jit(solution)/shard_map/ppermute | solution.py:19
  107.9 1.4 pad_maximum_fusion.3
  110.3 11.7 %cholesky.130 = f32[128,128]{1,0:T(8,128)S(1)} custom-call(f32[128,128]{1,0:T(8,128)S(1)} %cholesky.194), custom_call_target="Cholesky" | custom-call | tf_op jit(solution)/shard_map/jit(cholesky)/cholesky | solution.py:115
  122.1 9.8 %custom-call.15 = f32[1,128,128]{1,2,0:T(8,128)S(1)} custom-call(f32[1,128,128]{2,1,0:T(8,128)S(1)} %get-tuple-element.50), custom_call_target="InvertDiagBlocksLowerTriangular" | custom-call | tf_op jit(solution)/shard_map/jit(cholesky)/cholesky | solution.py:115
  132.1 2.2 broadcast_select_fusion.3
  134.3 2.8 collective-permute-start.2
  137.4 11.7 %cholesky.147 = f32[128,128]{1,0:T(8,128)S(1)} custom-call(f32[128,128]{1,0:T(8,128)S(1)} %convolution_subtract_fusion.1), custom_call_target="Cholesky" | custom-call | tf_op jit(solution)/shard_map/jit(cholesky)/cholesky | solution.py:115
  151.2 9.8 %custom-call.17 = f32[1,128,128]{1,2,0:T(8,128)S(1)} custom-call(f32[1,128,128]{2,1,0:T(8,128)S(1)} %get-tuple-element.41), custom_call_target="InvertDiagBlocksLowerTriangular" | custom-call | tf_op jit(solution)/shard_map/jit(_solve_triangular)/triangular_solve | solution.py:89
  161.4 9.8 %custom-call.16 = f32[1,128,128]{1,2,0:T(8,128)S(1)} custom-call(f32[1,128,128]{2,1,0:T(8,128)S(1)} %get-tuple-element.42), custom_call_target="InvertDiagBlocksLowerTriangular" | custom-call | tf_op jit(solution)/shard_map/jit(_solve_triangular)/triangular_solve | solution.py:88
  172.5 2.7 broadcast_select_fusion.4
  175.3 3.0 collective-permute-start.3
  179.8 11.7 %cholesky.164 = f32[128,128]{1,0:T(8,128)S(1)} custom-call(f32[128,128]{1,0:T(8,128)S(1)} %cholesky.197), custom_call_target="Cholesky" | custom-call | tf_op jit(solution)/shard_map/jit(cholesky)/cholesky | solution.py:122
  191.6 9.8 %custom-call.18 = f32[1,128,128]{1,2,0:T(8,128)S(1)} custom-call(f32[1,128,128]{2,1,0:T(8,128)S(1)} %get-tuple-element.46), custom_call_target="InvertDiagBlocksLowerTriangular" | custom-call | tf_op jit(solution)/shard_map/jit(cholesky)/cholesky | solution.py:122
  203.8 11.7 %cholesky.181 = f32[128,128]{1,0:T(8,128)S(1)} custom-call(f32[128,128]{1,0:T(8,128)S(1)} %convolution_subtract_fusion), custom_call_target="Cholesky" | custom-call | tf_op jit(solution)/shard_map/jit(cholesky)/cholesky | solution.py:122
  218.8 9.9 %custom-call.19 = f32[1,128,128]{1,2,0:T(8,128)S(1)} custom-call(f32[1,128,128]{2,1,0:T(8,128)S(1)} %get-tuple-element.39), custom_call_target="InvertDiagBlocksLowerTriangular" | custom-call | tf_op jit(solution)/shard_map/jit(_solve_triangular)/triangular_solve | solution.py:88
  228.8 2.2 broadcast_select_fusion.5
  231.1 21.5 %collective-permute-start.4 = (f32[8,256,256]{1,2,0:T(8,128)}, f32[8,256,256]{1,2,0:T(8,128)}, u32[]{:S(2)}, u32[]{:S(2)}) collective-permute-start(f32[8,256,256]{1,2,0:T(8,128)} %broadcast_select_fusion.5), channel_id=1, source_target_pairs={{0,1},{1,0},{2,3},{3,2},{4,5},{5,4},{6,7},{7,6},{8,9},{9,8},{10,11... | collective-permute-start | bytes 6291464 | tf_op jit(solution)/shard_map/ppermute | solution.py:80
  252.9 10.6 %custom-call.20 = f32[1,128,128]{1,2,0:T(8,128)S(1)} custom-call(f32[1,128,128]{2,1,0:T(8,128)} %get-tuple-element.40), custom_call_target="InvertDiagBlocksLowerTriangular" | custom-call | tf_op jit(solution)/shard_map/jit(_solve_triangular)/triangular_solve | solution.py:89
  265.6 3.5 %fusion.9 = f32[2,256,512]{2,1,0:T(8,128)S(1)} fusion(f32[2,256,512]{1,0,2:T(2,128)S(1)} %copy-done.8, f32[256,256]{1,0:T(8,128)S(1)} %select_maximum_fusion.1, f32[128,128]{1,0:T(8,128)S(1)} %copy.20, f32[128,128]{1,0:T(8,128)S(1)} %convolution_negate_fusion.1, f32[128,256]{1,0:T(8,128)S(1)} %concatenate.52, f32[256,256]{1,0:T(8,128)S(1)} %convolution_negate_fusion), kind=kOutput, calls=%fused_computation.24 | convolution fusion | flops 1612185600 | bytes 2883584 | tf_op jit(solution)/shard_map/cak,bk->cab/dot_general | solution.py:138
  269.1 2.9 convolution_bitcast_fusion
  271.9 2.7 broadcast_select_fusion.7
  274.7 1.3 copy-done.2
  276.0 8.2 %fusion.2 = f32[8,256,256]{2,1,0:T(8,128)} fusion(f32[8,256,256]{1,2,0:T(8,128)S(1)} %get-tuple-element.32, f32[8,256,256]{1,2,0:T(8,128)S(1)} %get-tuple-element.31, f32[512,512]{1,0:T(8,128)S(1)} %select_maximum_fusion, s32[]{:T(128)S(6)} %select_n.182), kind=kOutput, calls=%fused_computation.4 | convolution fusion | flops 3222274048 | bytes 6815748 | tf_op jit(solution)/shard_map/rak,bk->rab/dot_general | solution.py:152
  284.2 2.9 copy.26
  288.5 9.4 %subtract_select_fusion = f32[8,256,2,256]{1,3,2,0:T(8,128)S(1)} fusion(pred[8,2]{1,0:T(8,128)(4,1)S(1)} %broadcast_and_fusion, f32[2,512,256,1]{2,1,0,3:T(8,128)} %convolution_bitcast_fusion, f32[8,256,256]{1,2,0:T(8,128)} %copy-done.2, f32[8,256,256]{1,2,0:T(8,128)S(1)} %get-tuple-element.31, f32[1,8,256,1,2,256]{2,5,4,1,3,0:T(8,128)} %copy.12), kind=kOutput, calls=%fused_computation.3 | convolution fusion | flops 6445596672 | bytes 13631504 | tf_op jit(solution)/shard_map/rak,ckb->racb/dot_general | solution.py:140
  297.9 2.1 copy.54
  301.0 1.6 fusion.5
  302.6 7.2 %copy.29 = f32[1,8,256,1,2,256]{5,4,3,2,1,0:T(2,128)} copy(f32[1,8,256,1,2,256]{2,5,4,1,3,0:T(8,128)} %fusion.5) | data formatting | bytes 8388608 | tf_op jit(solution)/shard_map/scatter | solution.py:155
  (131 shorter events, 42.7 us)
Async XLA Ops:
  8.2 38.4 %collective-permute-start.14 = (f32[256,256]{0,1:T(8,128)S(1)}, f32[256,256]{0,1:T(8,128)S(1)}, u32[]{:S(2)}, u32[]{:S(2)}) collective-permute-start(f32[256,256]{0,1:T(8,128)S(1)} %slice_bitcast_fusion.10), channel_id=1, source_target_pairs={{0,224},{32,0},{1,225},{33,1}} | collective-permute-start | bytes 786440 | tf_op jit(solution)/shard_map/ppermute | solution.py:34
  9.5 36.3 %collective-permute-start.13 = (f32[256,256]{0,1:T(8,128)S(1)}, f32[256,256]{0,1:T(8,128)S(1)}, u32[]{:S(2)}, u32[]{:S(2)}) collective-permute-start(f32[256,256]{0,1:T(8,128)S(1)} %slice_bitcast_fusion.10), channel_id=1, source_target_pairs={{0,192},{32,224},{1,193},{33,225}} | collective-permute-start | bytes 786440 | tf_op jit(solution)/shard_map/ppermute | solution.py:34
  14.1 31.0 %collective-permute-start.12 = (f32[256,256]{0,1:T(8,128)S(1)}, f32[256,256]{0,1:T(8,128)S(1)}, u32[]{:S(2)}, u32[]{:S(2)}) collective-permute-start(f32[256,256]{0,1:T(8,128)S(1)} %slice_bitcast_fusion.10), channel_id=1, source_target_pairs={{0,160},{32,192},{1,161},{33,193}} | collective-permute-start | bytes 786440 | tf_op jit(solution)/shard_map/ppermute | solution.py:34
  15.4 19.1 %collective-permute-start.9 = (f32[256,256]{0,1:T(8,128)S(1)}, f32[256,256]{0,1:T(8,128)S(1)}, u32[]{:S(2)}, u32[]{:S(2)}) collective-permute-start(f32[256,256]{0,1:T(8,128)S(1)} %slice_bitcast_fusion.10), channel_id=1, source_target_pairs={{0,64},{32,96},{1,65},{33,97}} | collective-permute-start | bytes 786440 | tf_op jit(solution)/shard_map/ppermute | solution.py:34
  16.7 15.7 %collective-permute-start.8 = (f32[256,256]{0,1:T(8,128)S(1)}, f32[256,256]{0,1:T(8,128)S(1)}, u32[]{:S(2)}, u32[]{:S(2)}) collective-permute-start(f32[256,256]{0,1:T(8,128)S(1)} %slice_bitcast_fusion.10), channel_id=1, source_target_pairs={{0,32},{32,64},{1,33},{33,65}} | collective-permute-start | bytes 786440 | tf_op jit(solution)/shard_map/ppermute | solution.py:34
  32.5 5.6 %collective-permute-start.10 = (f32[256,256]{0,1:T(8,128)S(1)}, f32[256,256]{0,1:T(8,128)S(1)}, u32[]{:S(2)}, u32[]{:S(2)}) collective-permute-start(f32[256,256]{0,1:T(8,128)S(1)} %slice_bitcast_fusion.10), channel_id=1, source_target_pairs={{0,96},{32,128},{1,97},{33,129}} | collective-permute-start | bytes 786440 | tf_op jit(solution)/shard_map/ppermute | solution.py:34
  34.5 9.9 %collective-permute-start.11 = (f32[256,256]{0,1:T(8,128)S(1)}, f32[256,256]{0,1:T(8,128)S(1)}, u32[]{:S(2)}, u32[]{:S(2)}) collective-permute-start(f32[256,256]{0,1:T(8,128)S(1)} %slice_bitcast_fusion.10), channel_id=1, source_target_pairs={{0,128},{32,160},{1,129},{33,161}} | collective-permute-start | bytes 786440 | tf_op jit(solution)/shard_map/ppermute | solution.py:34
  38.1 16.5 %collective-permute-start.5 = (f32[256,2,256]{2,1,0:T(2,128)S(1)}, f32[256,2,256]{2,1,0:T(2,128)S(1)}, u32[]{:S(2)}, u32[]{:S(2)}) collective-permute-start(f32[256,2,256]{2,1,0:T(2,128)S(1)} %get-tuple-element.34), channel_id=1, source_target_pairs={{0,32},{32,0},{1,33},{33,1},{2,34},{34,2},{3,35},{35,3},{4,36},{36... | collective-permute-start | bytes 1572872 | tf_op jit(solution)/shard_map/ppermute | solution.py:12
  40.7 9.0 %copy-start = (f32[1,8,256,1,2,256]{2,5,4,1,3,0:T(8,128)S(1)}, f32[1,8,256,1,2,256]{2,5,4,1,3,0:T(8,128)}, u32[]{:S(2)}) copy-start(f32[1,8,256,1,2,256]{2,5,4,1,3,0:T(8,128)} %copy.12) | copy-start | bytes 12582916
  48.4 5.6 %copy-start.17 = (s32[2]{0:T(128)S(1)}, s32[2]{0:T(128)}, u32[]{:S(2)}) copy-start(s32[2]{0:T(128)} %constant.175.clone) | copy-start | bytes 28
  48.4 12.4 %collective-permute-start.15 = (f32[2,256,256]{1,2,0:T(8,128)S(1)}, f32[2,256,256]{1,2,0:T(8,128)S(1)}, u32[]{:S(2)}, u32[]{:S(2)}) collective-permute-start(f32[2,256,256]{1,2,0:T(8,128)S(1)} %pad_maximum_fusion.4), channel_id=1, source_target_pairs={{0,16},{1,9},{32,48},{33,41},{64,80},{65,73},{96,112},{97,105},{12... | collective-permute-start | bytes 1572872 | tf_op jit(solution)/shard_map/ppermute | solution.py:76
  51.2 11.6 %copy-start.16 = (s32[4]{0:T(128)S(1)}, s32[4]{0:T(128)}, u32[]{:S(2)}) copy-start(s32[4]{0:T(128)} %constant.176.clone) | copy-start | bytes 52
  51.2 39.4 %collective-permute-start = (f32[8,256,256]{1,2,0:T(8,128)}, f32[8,256,256]{1,2,0:T(8,128)}, u32[]{:S(2)}, u32[]{:S(2)}) collective-permute-start(f32[8,256,256]{1,2,0:T(8,128)} %slice_bitcast_fusion.1), channel_id=1, source_target_pairs={{0,16},{1,9},{32,48},{33,41},{64,80},{65,73},{96,112},{97,105},{12... | collective-permute-start | bytes 6291464 | tf_op jit(solution)/shard_map/ppermute | solution.py:76
  55.1 22.1 %copy-start.15 = (s32[2]{0:T(128)S(1)}, s32[2]{0:T(128)}, u32[]{:S(2)}) copy-start(s32[2]{0:T(128)} %constant.179.clone) | copy-start | bytes 28
  55.1 22.8 %copy-start.14 = (s32[8]{0:T(128)S(1)}, s32[8]{0:T(128)}, u32[]{:S(2)}) copy-start(s32[8]{0:T(128)} %constant.177.clone) | copy-start | bytes 100
  55.1 27.6 %collective-permute-start.6 = (f32[2,256,2,256]{3,2,1,0:T(2,128)S(1)}, f32[2,256,2,256]{3,2,1,0:T(2,128)S(1)}, u32[]{:S(2)}, u32[]{:S(2)}) collective-permute-start(f32[2,256,2,256]{3,2,1,0:T(2,128)S(1)} %maximum_select_fusion), channel_id=1, source_target_pairs={{0,128},{32,160},{1,129},{33,161},{2,130},{34,162},{3,131},{35,163... | collective-permute-start | bytes 3145736 | tf_op jit(solution)/shard_map/ppermute | solution.py:19
  61.5 13.0 %collective-permute-start.16 = (f32[2,256,256]{1,2,0:T(8,128)S(1)}, f32[2,256,256]{1,2,0:T(8,128)S(1)}, u32[]{:S(2)}, u32[]{:S(2)}) collective-permute-start(f32[2,256,256]{1,2,0:T(8,128)S(1)} %broadcast_select_fusion.8), channel_id=1, source_target_pairs={{0,8},{16,24},{1,17},{9,25},{32,40},{48,56},{33,49},{41,57},{64,72... | collective-permute-start | bytes 1572872 | tf_op jit(solution)/shard_map/ppermute | solution.py:76
  75.9 10.4 %collective-permute-start.17 = (f32[2,256,256]{1,2,0:T(8,128)S(1)}, f32[2,256,256]{1,2,0:T(8,128)S(1)}, u32[]{:S(2)}, u32[]{:S(2)}) collective-permute-start(f32[2,256,256]{1,2,0:T(8,128)S(1)} %broadcast_select_fusion.9), channel_id=1, source_target_pairs={{0,4},{16,20},{8,12},{24,28},{1,13},{9,5},{17,29},{25,21},{32,36},... | collective-permute-start | bytes 1572872 | tf_op jit(solution)/shard_map/ppermute | solution.py:76
  78.6 11.4 %copy-start.13 = (s32[4]{0:T(128)S(1)}, s32[4]{0:T(128)}, u32[]{:S(2)}) copy-start(s32[4]{0:T(128)} %constant.180.clone) | copy-start | bytes 52
  78.6 12.0 %copy-start.1 = (f32[1,8,256,1,2,256]{2,5,4,1,3,0:T(8,128)S(1)}, f32[1,8,256,1,2,256]{2,5,4,1,3,0:T(8,128)}, u32[]{:S(2)}) copy-start(f32[1,8,256,1,2,256]{2,5,4,1,3,0:T(8,128)} %copy.12) | copy-start | bytes 12582916
  84.0 22.7 %collective-permute-start.7 = (f32[2,256,2,256]{3,2,1,0:T(2,128)S(1)}, f32[2,256,2,256]{3,2,1,0:T(2,128)}, u32[]{:S(2)}, u32[]{:S(2)}) collective-permute-start(f32[2,256,2,256]{3,2,1,0:T(2,128)S(1)} %broadcast_select_fusion), channel_id=1, source_target_pairs={{0,64},{32,96},{128,192},{160,224},{1,65},{33,97},{129,193},{161,2... | collective-permute-start | bytes 3145736 | tf_op jit(solution)/shard_map/ppermute | solution.py:19
  87.9 7.7 %collective-permute-start.18 = (f32[2,256,256]{1,2,0:T(8,128)}, f32[2,256,256]{1,2,0:T(8,128)}, u32[]{:S(2)}, u32[]{:S(2)}) collective-permute-start(f32[2,256,256]{1,2,0:T(8,128)} %broadcast_select_fusion.10), channel_id=1, source_target_pairs={{0,2},{16,18},{8,10},{24,26},{4,6},{20,22},{12,14},{28,30},{1,15},... | collective-permute-start | bytes 1572872 | tf_op jit(solution)/shard_map/ppermute | solution.py:76
  90.6 3.6 %copy-start.12 = (s32[16]{0:T(128)S(1)}, s32[16]{0:T(128)}, u32[]{:S(2)}) copy-start(s32[16]{0:T(128)} %constant.178.clone) | copy-start | bytes 196
  91.6 40.5 %collective-permute-start.1 = (f32[8,256,256]{1,2,0:T(8,128)S(1)}, f32[8,256,256]{1,2,0:T(8,128)}, u32[]{:S(2)}, u32[]{:S(2)}) collective-permute-start(f32[8,256,256]{1,2,0:T(8,128)S(1)} %broadcast_select_fusion.2), channel_id=1, source_target_pairs={{0,8},{16,24},{1,17},{9,25},{32,40},{48,56},{33,49},{41,57},{64,72... | collective-permute-start | bytes 6291464 | tf_op jit(solution)/shard_map/ppermute | solution.py:76
  97.3 12.0 %copy-start.4 = (f32[2,256,256]{1,2,0:T(8,128)}, f32[2,256,256]{1,2,0:T(8,128)S(1)}, u32[]{:S(2)}) copy-start(f32[2,256,256]{1,2,0:T(8,128)S(1)} %broadcast_select_fusion.11) | copy-start | bytes 1572868
  97.4 12.0 %collective-permute-start.19 = (f32[2,256,256]{1,2,0:T(8,128)S(1)}, f32[2,256,256]{1,2,0:T(8,128)S(1)}, u32[]{:S(2)}, u32[]{:S(2)}) collective-permute-start(f32[2,256,256]{1,2,0:T(8,128)S(1)} %broadcast_select_fusion.11), channel_id=1, source_target_pairs={{0,1},{1,0},{2,3},{3,2},{4,5},{5,4},{6,7},{7,6},{8,9},{9,8},{10,11... | collective-permute-start | bytes 1572872 | tf_op jit(solution)/shard_map/ppermute | solution.py:80
  109.3 0.8 copy-start.6
  134.3 38.2 %collective-permute-start.2 = (f32[8,256,256]{1,2,0:T(8,128)}, f32[8,256,256]{1,2,0:T(8,128)}, u32[]{:S(2)}, u32[]{:S(2)}) collective-permute-start(f32[8,256,256]{1,2,0:T(8,128)} %broadcast_select_fusion.3), channel_id=1, source_target_pairs={{0,4},{16,20},{8,12},{24,28},{1,13},{9,5},{17,29},{25,21},{32,36},... | collective-permute-start | bytes 6291464 | tf_op jit(solution)/shard_map/ppermute | solution.py:76
  161.3 10.6 %copy-start.9 = (f32[128,128]{1,0:T(8,128)}, f32[128,128]{1,0:T(8,128)S(1)}, u32[]{:S(2)}) copy-start(f32[128,128]{1,0:T(8,128)S(1)} %copy.15) | copy-start | bytes 196612
  172.5 5.8 %copy-start.5 = (f32[2,256,256]{1,2,0:T(8,128)S(1)}, f32[2,256,256]{1,2,0:T(8,128)}, u32[]{:S(2)}) copy-start(f32[2,256,256]{1,2,0:T(8,128)} %copy-done.4) | copy-start | bytes 1572868
  172.5 5.8 %copy-start.7 = (f32[2,256,256]{1,2,0:T(8,128)S(1)}, f32[2,256,256]{1,2,0:T(8,128)}, u32[]{:S(2)}) copy-start(f32[2,256,256]{1,2,0:T(8,128)} %copy-done.6) | copy-start | bytes 1572868
  175.3 53.5 %collective-permute-start.3 = (f32[8,256,256]{1,2,0:T(8,128)S(1)}, f32[8,256,256]{1,2,0:T(8,128)}, u32[]{:S(2)}, u32[]{:S(2)}) collective-permute-start(f32[8,256,256]{1,2,0:T(8,128)S(1)} %broadcast_select_fusion.4), channel_id=1, source_target_pairs={{0,2},{16,18},{8,10},{24,26},{4,6},{20,22},{12,14},{28,30},{1,15},... | collective-permute-start | bytes 6291464 | tf_op jit(solution)/shard_map/ppermute | solution.py:76
  179.1 0.7 copy-start.11
  228.8 35.1 %copy-start.10 = (f32[128,128]{1,0:T(8,128)S(1)}, f32[128,128]{1,0:T(8,128)}, u32[]{:S(2)}) copy-start(f32[128,128]{1,0:T(8,128)} %copy-done.9) | copy-start | bytes 196612
  231.1 40.9 %collective-permute-start.4 = (f32[8,256,256]{1,2,0:T(8,128)}, f32[8,256,256]{1,2,0:T(8,128)}, u32[]{:S(2)}, u32[]{:S(2)}) collective-permute-start(f32[8,256,256]{1,2,0:T(8,128)} %broadcast_select_fusion.5), channel_id=1, source_target_pairs={{0,1},{1,0},{2,3},{3,2},{4,5},{5,4},{6,7},{7,6},{8,9},{9,8},{10,11... | collective-permute-start | bytes 6291464 | tf_op jit(solution)/shard_map/ppermute | solution.py:80
  263.9 1.6 copy-start.8
  274.6 1.3 copy-start.2
  297.9 3.1 %copy-start.3 = (f32[8,256,256]{1,2,0:T(8,128)S(1)}, f32[8,256,256]{1,2,0:T(8,128)}, u32[]{:S(2)}) copy-start(f32[8,256,256]{1,2,0:T(8,128)} %copy.26) | copy-start | bytes 6291460

commit v9 on v7

--- a/solution.py
+++ b/solution.py
@@ -92,10 +92,8 @@
     ct = covariance.shape[4]
     tiles = covariance.reshape(rt, tile, ct, tile)
 
-    first, second = diag_to_first_pcols(tiles[0, :, 0, :], prows, pcols)
-    diag_a, diag_b = pcol_broadcast_pair(jnp.stack([first, second]), pcols)
-
     t0, t1 = prow_from_first_two(tiles[0], prows)
+    diag_a, diag_b = pcol_broadcast_pair(jnp.stack([t0[:, 0, :], t1[:, 0, :]]), pcols)
 
     a00, a10 = diag_a[0], diag_a[1]
     a11 = diag_b[1]

time: 313 us -> 319 us (1.019)
  waiting for transfers between devices: 34.3 us -> 53 us
  local copies, waits for them, and re-layouts: 42.3 us -> 25.5 us
    ppermute x2, waiting for transfers between devices: 0.01 us -> 24.6 us  [prow_from_first_two(): got = lax.ppermute(pair, 'prow', pairs)]
    ppermute x7 -> x0, starting transfers between devices: 16.6 us -> none  [diag_to_first_pcols(): got.append(lax.ppermute(tile0, ('prow', 'pcol'), pairs))]
    ppermute x8, starting transfers between devices: 21.5 us -> 35.6 us  [pcol_broadcast_pair(): got = lax.ppermute(buf, 'pcol', pairs)]
    unnamed x41, local copies, waits for them, and re-layouts: 16.2 us -> 4.33 us
    ppermute x1, waiting for transfers between devices: 0.01 us -> 10.6 us  [prow_from_first_two(): other = lax.ppermute(x, 'prow', [(0, 1), (1, 0)])]
    ppermute x8, waiting for transfers between devices: 27.1 us -> 17.7 us  [pcol_broadcast_pair(): got = lax.ppermute(buf, 'pcol', pairs)]
    ppermute x2, starting transfers between devices: 13.8 us -> 21.1 us  [pcol_broadcast_pair(): other = lax.ppermute(buf, 'pcol', [(i, i ^ 1) for i in range(pcols)])]
    ppermute x7 -> x0, waiting for transfers between devices: 7.23 us -> none  [diag_to_first_pcols(): got.append(lax.ppermute(tile0, ('prow', 'pcol'), pairs))]
  transfers between devices with their start and end apart: 20 -> 13, of which waited for: 6 -> 6; matrix products, arithmetic and copies ran while one was open for 53% -> 52% of each run, Pallas kernels for 0% -> 0%
where the time goes in v9:
time: 319 us; the launch traced here: 312 us
  other arithmetic  138 us (43%)
  starting transfers between devices  65.2 us (20%)
  waiting for transfers between devices  53 us (17%)
  matrix products  26.8 us (8%)
  local copies, waits for them, and re-layouts  25.5 us (8%)
  between operations  3.56 us (1%)
    another operation x7, other arithmetic, per_device(): l00 = jnp.tril(jnp.linalg.cholesky(a00))  35.9 us
    ppermute x8, starting transfers between devices, pcol_broadcast_pair(): got = lax.ppermute(buf, 'pcol', pairs)  35.6 us
    another operation x7, other arithmetic, per_device(): l11 = jnp.tril(jnp.linalg.cholesky(schur))  34.7 us
    ppermute x2, waiting for transfers between devices, prow_from_first_two(): got = lax.ppermute(pair, 'prow', pairs)  24.6 us
    another operation x4, other arithmetic, per_device(): l00_inv = jax.scipy.linalg.solve_triangular(l00, eye, lower=True)  22.1 us
    ppermute x2, starting transfers between devices, pcol_broadcast_pair(): other = lax.ppermute(buf, 'pcol', [(i, i ^ 1) for i in range(pcols)])  21.1 us
    another operation x2, other arithmetic, per_device(): l11_inv = jax.scipy.linalg.solve_triangular(l11, eye, lower=True)  21 us
    ppermute x8, waiting for transfers between devices, pcol_broadcast_pair(): got = lax.ppermute(buf, 'pcol', pairs)  17.7 us
  transfers between devices with their start and end apart: 13, of which 6 were waited for; matrix products, arithmetic and copies ran while one was open for 52% of the time, Pallas kernels for 0%

profile of v9, /device:TPU:1, one launch (start us, length us, event | category | flops | bytes accessed | tf_op | source)
XLA Modules:
  0.0 312.5 jit_solution(6089785775332090717)
XLA Ops:
  1.5 5.5 %collective-permute-start.5 = (f32[256,2,256]{0,2,1:T(8,128)S(1)}, f32[256,2,256]{0,2,1:T(8,128)S(1)}, u32[]{:S(2)}, u32[]{:S(2)}) collective-permute-start(f32[256,2,256]{0,2,1:T(8,128)S(1)} %bitcast.143), channel_id=1, source_target_pairs={{0,32},{32,0},{1,33},{33,1},{2,34},{34,2},{3,35},{35,3},{4,36},{36... | collective-permute-start | bytes 1572872 | tf_op jit(solution)/shard_map/ppermute | solution.py:12
  7.0 10.6 %collective-permute-done.5 = f32[256,2,256]{0,2,1:T(8,128)S(1)} collective-permute-done((f32[256,2,256]{0,2,1:T(8,128)S(1)}, f32[256,2,256]{0,2,1:T(8,128)S(1)}, u32[]{:S(2)}, u32[]{:S(2)}) %collective-permute-start.5) | collective-permute-done | bytes 524320 | tf_op jit(solution)/shard_map/ppermute | solution.py:12
  17.6 1.6 collective-permute-start.6
  19.9 19.8 %collective-permute-done.6 = f32[2,256,2,256]{1,3,2,0:T(8,128)S(1)} collective-permute-done((f32[2,256,2,256]{1,3,2,0:T(8,128)S(1)}, f32[2,256,2,256]{1,3,2,0:T(8,128)S(1)}, u32[]{:S(2)}, u32[]{:S(2)}) %collective-permute-start.6) | collective-permute-done | bytes 1048608 | tf_op jit(solution)/shard_map/ppermute | solution.py:19
  40.5 1.4 collective-permute-start.7
  42.5 1.9 copy-done.2
  44.4 11.8 %collective-permute-start = (f32[8,256,256]{2,1,0:T(8,128)S(1)}, f32[8,256,256]{2,1,0:T(8,128)}, u32[]{:S(2)}, u32[]{:S(2)}) collective-permute-start(f32[8,256,256]{2,1,0:T(8,128)S(1)} %slice_bitcast_fusion.1), channel_id=1, source_target_pairs={{0,16},{1,9},{32,48},{33,41},{64,80},{65,73},{96,112},{97,105},{12... | collective-permute-start | bytes 6291464 | tf_op jit(solution)/shard_map/ppermute | solution.py:76
  56.9 4.8 %collective-permute-done.7 = f32[2,256,2,256]{1,3,2,0:T(8,128)S(1)} collective-permute-done((f32[2,256,2,256]{1,3,2,0:T(8,128)S(1)}, f32[2,256,2,256]{1,3,2,0:T(8,128)S(1)}, u32[]{:S(2)}, u32[]{:S(2)}) %collective-permute-start.7) | collective-permute-done | bytes 1048608 | tf_op jit(solution)/shard_map/ppermute | solution.py:19
  64.5 11.3 %collective-permute-start.8 = (f32[2,256,256]{1,2,0:T(8,128)}, f32[2,256,256]{1,2,0:T(8,128)S(1)}, u32[]{:S(2)}, u32[]{:S(2)}) collective-permute-start(f32[2,256,256]{1,2,0:T(8,128)} %pad_maximum_fusion.3), channel_id=1, source_target_pairs={{0,16},{1,9},{32,48},{33,41},{64,80},{65,73},{96,112},{97,105},{12... | collective-permute-start | bytes 1572872 | tf_op jit(solution)/shard_map/ppermute | solution.py:76
  76.6 7.0 %collective-permute-done.8 = f32[2,256,256]{1,2,0:T(8,128)S(1)} collective-permute-done((f32[2,256,256]{1,2,0:T(8,128)}, f32[2,256,256]{1,2,0:T(8,128)S(1)}, u32[]{:S(2)}, u32[]{:S(2)}) %collective-permute-start.8) | collective-permute-done | bytes 524320 | tf_op jit(solution)/shard_map/ppermute | solution.py:76
  84.3 1.3 collective-permute-start.9
  86.3 2.6 broadcast_select_fusion
  89.0 2.8 collective-permute-start.1
  91.7 1.3 broadcast_select_fusion.9
  95.0 5.5 %collective-permute-done.10 = f32[2,256,256]{1,2,0:T(8,128)S(1)} collective-permute-done((f32[2,256,256]{1,2,0:T(8,128)S(1)}, f32[2,256,256]{1,2,0:T(8,128)S(1)}, u32[]{:S(2)}, u32[]{:S(2)}) %collective-permute-start.10) | collective-permute-done | bytes 524320 | tf_op jit(solution)/shard_map/ppermute | solution.py:76
  101.1 1.3 collective-permute-start.11
  103.3 5.3 %collective-permute-done.11 = f32[2,256,256]{1,2,0:T(8,128)S(1)} collective-permute-done((f32[2,256,256]{1,2,0:T(8,128)S(1)}, f32[2,256,256]{1,2,0:T(8,128)S(1)}, u32[]{:S(2)}, u32[]{:S(2)}) %collective-permute-start.11) | collective-permute-done | bytes 524320 | tf_op jit(solution)/shard_map/ppermute | solution.py:76
  109.3 17.8 %collective-permute-start.12 = (f32[2,256,256]{1,2,0:T(8,128)S(1)}, f32[2,256,256]{1,2,0:T(8,128)}, u32[]{:S(2)}, u32[]{:S(2)}) collective-permute-start(f32[2,256,256]{1,2,0:T(8,128)S(1)} %broadcast_select_fusion.11), channel_id=1, source_target_pairs={{0,1},{1,0},{2,3},{3,2},{4,5},{5,4},{6,7},{7,6},{8,9},{9,8},{10,11... | collective-permute-start | bytes 1572872 | tf_op jit(solution)/shard_map/ppermute | solution.py:80
  127.2 2.5 broadcast_select_fusion.1
  129.7 2.8 collective-permute-start.2
  134.3 1.8 copy.14
  137.8 11.7 %cholesky.130 = f32[128,128]{1,0:T(8,128)S(1)} custom-call(f32[128,128]{1,0:T(8,128)S(1)} %cholesky.194), custom_call_target="Cholesky" | custom-call | tf_op jit(solution)/shard_map/jit(cholesky)/cholesky | solution.py:101
  149.5 10.4 %custom-call.13 = f32[1,128,128]{1,2,0:T(8,128)} custom-call(f32[1,128,128]{2,1,0:T(8,128)S(1)} %get-tuple-element.84), custom_call_target="InvertDiagBlocksLowerTriangular" | custom-call | tf_op jit(solution)/shard_map/jit(cholesky)/cholesky | solution.py:101
  160.7 1.7 constant_dynamic-update-slice_fusion.1
  163.5 11.7 %cholesky.147 = f32[128,128]{1,0:T(8,128)S(1)} custom-call(f32[128,128]{1,0:T(8,128)S(1)} %convolution_subtract_fusion.3), custom_call_target="Cholesky" | custom-call | tf_op jit(solution)/shard_map/jit(cholesky)/cholesky | solution.py:101
  178.4 1.8 fusion.31
  180.3 5.6 %while.6 = (s32[]{:T(128)}, f32[256,256]{1,0:T(8,128)}, s32[2,2]{1,0:T(2,128)S(1)}, f32[2,128,128]{2,1,0:T(8,128)S(1)}, s32[]{:T(128)}) while((s32[]{:T(128)}, f32[256,256]{1,0:T(8,128)}, s32[2,2]{1,0:T(2,128)S(1)}, f32[2,128,128]{2,1,0:T(8,128)S(1)}, s32[]{:T(128)}) %tuple.56), condition=%wide.while_cond.2, body=%wide.while_body.2.sunk | while | flops 2 | bytes 131189 | solution.py:105
  180.9 2.2 bitcast_dynamic-update-slice_fusion.4
  183.8 2.2 bitcast_dynamic-update-slice_fusion.4
  185.9 20.3 %custom-call.14 = f32[2,128,128]{1,2,0:T(8,128)} custom-call(f32[2,128,128]{2,1,0:T(8,128)S(1)} %get-tuple-element.45), custom_call_target="InvertDiagBlocksLowerTriangular" | custom-call | tf_op jit(solution)/shard_map/jit(_solve_triangular)/triangular_solve | solution.py:105
  209.7 2.2 broadcast_select_fusion.2
  211.8 3.0 collective-permute-start.3
  215.3 1.5 fusion.24
  217.0 11.7 %cholesky.164 = f32[128,128]{1,0:T(8,128)S(1)} custom-call(f32[128,128]{1,0:T(8,128)S(1)} %cholesky.197), custom_call_target="Cholesky" | custom-call | tf_op jit(solution)/shard_map/jit(cholesky)/cholesky | solution.py:108
  228.8 9.8 %custom-call.15 = f32[1,128,128]{1,2,0:T(8,128)S(1)} custom-call(f32[1,128,128]{2,1,0:T(8,128)S(1)} %get-tuple-element.80), custom_call_target="InvertDiagBlocksLowerTriangular" | custom-call | tf_op jit(solution)/shard_map/jit(cholesky)/cholesky | solution.py:108
  239.3 11.7 %cholesky.181 = f32[128,128]{1,0:T(8,128)S(1)} custom-call(f32[128,128]{1,0:T(8,128)S(1)} %convolution_subtract_fusion.2), custom_call_target="Cholesky" | custom-call | tf_op jit(solution)/shard_map/jit(cholesky)/cholesky | solution.py:108
  254.5 2.7 broadcast_select_fusion.3
  257.2 3.3 %collective-permute-start.4 = (f32[8,256,256]{2,1,0:T(8,128)S(1)}, f32[8,256,256]{2,1,0:T(8,128)}, u32[]{:S(2)}, u32[]{:S(2)}) collective-permute-start(f32[8,256,256]{2,1,0:T(8,128)S(1)} %broadcast_select_fusion.3), channel_id=1, source_target_pairs={{0,1},{1,0},{2,3},{3,2},{4,5},{5,4},{6,7},{7,6},{8,9},{9,8},{10,11... | collective-permute-start | bytes 6291464 | tf_op jit(solution)/shard_map/ppermute | solution.py:80
  260.5 4.1 %while.7 = (s32[]{:T(128)}, f32[256,256]{1,0:T(8,128)S(1)}, s32[2,2]{1,0:T(2,128)S(1)}, f32[2,128,128]{2,1,0:T(8,128)S(1)}, s32[]{:T(128)}) while((s32[]{:T(128)}, f32[256,256]{1,0:T(8,128)S(1)}, s32[2,2]{1,0:T(2,128)S(1)}, f32[2,128,128]{2,1,0:T(8,128)S(1)}, s32[]{:T(128)}) %tuple.62), condition=%wide.while_cond.2.clone, body=%wide.while_body.2.clone.sunk | while | flops 2 | bytes 131189 | solution.py:109
  261.1 1.4 bitcast_dynamic-update-slice_fusion.5
  263.2 1.4 bitcast_dynamic-update-slice_fusion.5
  264.8 20.3 %custom-call.16 = f32[2,128,128]{1,2,0:T(8,128)} custom-call(f32[2,128,128]{2,1,0:T(8,128)S(1)} %get-tuple-element.46), custom_call_target="InvertDiagBlocksLowerTriangular" | custom-call | tf_op jit(solution)/shard_map/jit(_solve_triangular)/triangular_solve | solution.py:109
  288.9 1.9 fusion.8
  290.7 1.9 convolution_bitcast_fusion
  292.7 2.0 broadcast_select_fusion.5
  294.7 3.5 %fusion.2 = f32[8,256,256]{2,1,0:T(8,128)S(1)} fusion(f32[8,256,256]{2,1,0:T(8,128)S(1)} %get-tuple-element.72, f32[8,256,256]{2,1,0:T(8,128)S(1)} %get-tuple-element.71, f32[512,512]{1,0:T(8,128)S(1)} %select_maximum_fusion, s32[]{:T(128)S(6)} %select_n.169), kind=kOutput, calls=%fused_computation.9 | convolution fusion | flops 3222274048 | bytes 6815748 | tf_op jit(solution)/shard_map/rak,bk->rab/dot_general | solution.py:138
  298.2 7.2 %subtract_select_fusion = f32[8,256,2,256]{3,1,0,2:T(8,128)S(1)} fusion(pred[8,2]{0,1:T(4,128)(4,1)S(1)} %broadcast_and_fusion, f32[2,512,256,1]{2,1,3,0:T(8,128)S(1)} %convolution_bitcast_fusion, f32[8,256,256]{2,1,0:T(8,128)S(1)} %get-tuple-element.72, f32[8,256,256]{2,1,0:T(8,128)S(1)} %get-tuple-element.71, f32[1,8,256,1,2,256]{5,4,3,2,1,0:T(2,128)S(1)} %copy-done.1), kind=kOutput, calls=%fused_computation.8 | convolution fusion | flops 6445596672 | bytes 13631504 | tf_op jit(solution)/shard_map/rak,ckb->racb/dot_general | solution.py:126
  307.0 5.2 %copy.21 = f32[1,8,256,1,2,256]{5,4,3,2,1,0:T(2,128)} copy(f32[1,8,256,1,2,256]{5,2,1,4,3,0:T(8,128)S(1)} %fusion.5) | data formatting | bytes 8388608 | tf_op jit(solution)/shard_map/scatter | solution.py:141
  (119 shorter events, 35.4 us)
Async XLA Ops:
  0.0 19.2 %copy-start.18 = (s32[2]{0:T(128)S(1)}, s32[2]{0:T(128)}, u32[]{:S(2)}) copy-start(s32[2]{0:T(128)} %constant.166.clone) | copy-start | bytes 28
  1.5 16.1 %collective-permute-start.5 = (f32[256,2,256]{0,2,1:T(8,128)S(1)}, f32[256,2,256]{0,2,1:T(8,128)S(1)}, u32[]{:S(2)}, u32[]{:S(2)}) collective-permute-start(f32[256,2,256]{0,2,1:T(8,128)S(1)} %bitcast.143), channel_id=1, source_target_pairs={{0,32},{32,0},{1,33},{33,1},{2,34},{34,2},{3,35},{35,3},{4,36},{36... | collective-permute-start | bytes 1572872 | tf_op jit(solution)/shard_map/ppermute | solution.py:12
  17.5 24.3 %copy-start = (f32[1,8,256,1,2,256]{5,4,3,2,1,0:T(2,128)S(1)}, f32[1,8,256,1,2,256]{5,4,3,2,1,0:T(2,128)}, u32[]{:S(2)}) copy-start(f32[1,8,256,1,2,256]{5,4,3,2,1,0:T(2,128)} %param.18) | copy-start | bytes 12582916
  17.6 22.1 %collective-permute-start.6 = (f32[2,256,2,256]{1,3,2,0:T(8,128)S(1)}, f32[2,256,2,256]{1,3,2,0:T(8,128)S(1)}, u32[]{:S(2)}, u32[]{:S(2)}) collective-permute-start(f32[2,256,2,256]{1,3,2,0:T(8,128)S(1)} %maximum_select_fusion), channel_id=1, source_target_pairs={{0,128},{32,160},{1,129},{33,161},{2,130},{34,162},{3,131},{35,163... | collective-permute-start | bytes 3145736 | tf_op jit(solution)/shard_map/ppermute | solution.py:19
  40.5 21.2 %collective-permute-start.7 = (f32[2,256,2,256]{1,3,2,0:T(8,128)S(1)}, f32[2,256,2,256]{1,3,2,0:T(8,128)S(1)}, u32[]{:S(2)}, u32[]{:S(2)}) collective-permute-start(f32[2,256,2,256]{1,3,2,0:T(8,128)S(1)} %broadcast_select_fusion.6), channel_id=1, source_target_pairs={{0,64},{32,96},{128,192},{160,224},{1,65},{33,97},{129,193},{161,2... | collective-permute-start | bytes 3145736 | tf_op jit(solution)/shard_map/ppermute | solution.py:19
  42.3 2.0 copy-start.2
  42.4 13.9 %copy-start.17 = (s32[4]{0:T(128)S(1)}, s32[4]{0:T(128)}, u32[]{:S(2)}) copy-start(s32[4]{0:T(128)} %constant.167.clone) | copy-start | bytes 52
  44.4 41.9 %collective-permute-start = (f32[8,256,256]{2,1,0:T(8,128)S(1)}, f32[8,256,256]{2,1,0:T(8,128)}, u32[]{:S(2)}, u32[]{:S(2)}) collective-permute-start(f32[8,256,256]{2,1,0:T(8,128)S(1)} %slice_bitcast_fusion.1), channel_id=1, source_target_pairs={{0,16},{1,9},{32,48},{33,41},{64,80},{65,73},{96,112},{97,105},{12... | collective-permute-start | bytes 6291464 | tf_op jit(solution)/shard_map/ppermute | solution.py:76
  62.5 13.4 %copy-start.16 = (s32[2]{0:T(128)S(1)}, s32[2]{0:T(128)}, u32[]{:S(2)}) copy-start(s32[2]{0:T(128)} %constant.168.clone) | copy-start | bytes 28
  63.7 22.0 %copy-start.15 = (s32[4]{0:T(128)S(1)}, s32[4]{0:T(128)}, u32[]{:S(2)}) copy-start(s32[4]{0:T(128)} %constant.169.clone) | copy-start | bytes 52
  64.5 19.0 %collective-permute-start.8 = (f32[2,256,256]{1,2,0:T(8,128)}, f32[2,256,256]{1,2,0:T(8,128)S(1)}, u32[]{:S(2)}, u32[]{:S(2)}) collective-permute-start(f32[2,256,256]{1,2,0:T(8,128)} %pad_maximum_fusion.3), channel_id=1, source_target_pairs={{0,16},{1,9},{32,48},{33,41},{64,80},{65,73},{96,112},{97,105},{12... | collective-permute-start | bytes 1572872 | tf_op jit(solution)/shard_map/ppermute | solution.py:76
  84.3 7.4 %collective-permute-start.9 = (f32[2,256,256]{1,2,0:T(8,128)S(1)}, f32[2,256,256]{1,2,0:T(8,128)S(1)}, u32[]{:S(2)}, u32[]{:S(2)}) collective-permute-start(f32[2,256,256]{1,2,0:T(8,128)S(1)} %broadcast_select_fusion.8), channel_id=1, source_target_pairs={{0,8},{16,24},{1,17},{9,25},{32,40},{48,56},{33,49},{41,57},{64,72... | collective-permute-start | bytes 1572872 | tf_op jit(solution)/shard_map/ppermute | solution.py:76
  88.9 20.3 %copy-start.3 = (f32[8,256,256]{2,1,0:T(8,128)}, f32[8,256,256]{2,1,0:T(8,128)S(1)}, u32[]{:S(2)}) copy-start(f32[8,256,256]{2,1,0:T(8,128)S(1)} %broadcast_select_fusion) | copy-start | bytes 6291460
  88.9 5.5 %copy-start.14 = (s32[8]{0:T(128)S(1)}, s32[8]{0:T(128)}, u32[]{:S(2)}) copy-start(s32[8]{0:T(128)} %constant.170.clone) | copy-start | bytes 100
  89.0 13.5 %copy-start.13 = (s32[16]{0:T(128)S(1)}, s32[16]{0:T(128)}, u32[]{:S(2)}) copy-start(s32[16]{0:T(128)} %constant.171.clone) | copy-start | bytes 196
  89.0 38.2 %collective-permute-start.1 = (f32[8,256,256]{2,1,0:T(8,128)S(1)}, f32[8,256,256]{2,1,0:T(8,128)}, u32[]{:S(2)}, u32[]{:S(2)}) collective-permute-start(f32[8,256,256]{2,1,0:T(8,128)S(1)} %broadcast_select_fusion), channel_id=1, source_target_pairs={{0,8},{16,24},{1,17},{9,25},{32,40},{48,56},{33,49},{41,57},{64,72... | collective-permute-start | bytes 6291464 | tf_op jit(solution)/shard_map/ppermute | solution.py:76
  93.1 7.4 %collective-permute-start.10 = (f32[2,256,256]{1,2,0:T(8,128)S(1)}, f32[2,256,256]{1,2,0:T(8,128)S(1)}, u32[]{:S(2)}, u32[]{:S(2)}) collective-permute-start(f32[2,256,256]{1,2,0:T(8,128)S(1)} %broadcast_select_fusion.9), channel_id=1, source_target_pairs={{0,4},{16,20},{8,12},{24,28},{1,13},{9,5},{17,29},{25,21},{32,36},... | collective-permute-start | bytes 1572872 | tf_op jit(solution)/shard_map/ppermute | solution.py:76
  101.1 7.4 %collective-permute-start.11 = (f32[2,256,256]{1,2,0:T(8,128)S(1)}, f32[2,256,256]{1,2,0:T(8,128)S(1)}, u32[]{:S(2)}, u32[]{:S(2)}) collective-permute-start(f32[2,256,256]{1,2,0:T(8,128)S(1)} %broadcast_select_fusion.10), channel_id=1, source_target_pairs={{0,2},{16,18},{8,10},{24,26},{4,6},{20,22},{12,14},{28,30},{1,15},... | collective-permute-start | bytes 1572872 | tf_op jit(solution)/shard_map/ppermute | solution.py:76
  109.3 23.2 %collective-permute-start.12 = (f32[2,256,256]{1,2,0:T(8,128)S(1)}, f32[2,256,256]{1,2,0:T(8,128)}, u32[]{:S(2)}, u32[]{:S(2)}) collective-permute-start(f32[2,256,256]{1,2,0:T(8,128)S(1)} %broadcast_select_fusion.11), channel_id=1, source_target_pairs={{0,1},{1,0},{2,3},{3,2},{4,5},{5,4},{6,7},{7,6},{8,9},{9,8},{10,11... | collective-permute-start | bytes 1572872 | tf_op jit(solution)/shard_map/ppermute | solution.py:80
  127.1 80.2 %copy-start.4 = (f32[256,256]{1,0:T(8,128)}, f32[256,256]{1,0:T(8,128)S(1)}, u32[]{:S(2)}) copy-start(f32[256,256]{1,0:T(8,128)S(1)} %fusion.32) | copy-start | bytes 786436
  129.7 80.0 %collective-permute-start.2 = (f32[8,256,256]{2,1,0:T(8,128)S(1)}, f32[8,256,256]{2,1,0:T(8,128)}, u32[]{:S(2)}, u32[]{:S(2)}) collective-permute-start(f32[8,256,256]{2,1,0:T(8,128)S(1)} %broadcast_select_fusion.1), channel_id=1, source_target_pairs={{0,4},{16,20},{8,12},{24,28},{1,13},{9,5},{17,29},{25,21},{32,36},... | collective-permute-start | bytes 6291464 | tf_op jit(solution)/shard_map/ppermute | solution.py:76
  137.1 0.7 copy-start.10
  209.7 5.2 %copy-start.6 = (f32[128,256]{1,0:T(8,128)}, f32[128,256]{1,0:T(8,128)S(1)}, u32[]{:S(2)}) copy-start(f32[128,256]{1,0:T(8,128)S(1)} %fusion.42) | copy-start | bytes 393220
  211.8 42.7 %collective-permute-start.3 = (f32[8,256,256]{2,1,0:T(8,128)}, f32[8,256,256]{2,1,0:T(8,128)}, u32[]{:S(2)}, u32[]{:S(2)}) collective-permute-start(f32[8,256,256]{2,1,0:T(8,128)} %broadcast_select_fusion.2), channel_id=1, source_target_pairs={{0,2},{16,18},{8,10},{24,26},{4,6},{20,22},{12,14},{28,30},{1,15},... | collective-permute-start | bytes 6291464 | tf_op jit(solution)/shard_map/ppermute | solution.py:76
  254.5 30.5 %copy-start.7 = (f32[128,256]{1,0:T(8,128)S(1)}, f32[128,256]{1,0:T(8,128)}, u32[]{:S(2)}) copy-start(f32[128,256]{1,0:T(8,128)} %copy-done.6) | copy-start | bytes 393220
  257.2 27.9 %copy-start.5 = (f32[256,256]{1,0:T(8,128)S(1)}, f32[256,256]{1,0:T(8,128)}, u32[]{:S(2)}) copy-start(f32[256,256]{1,0:T(8,128)} %copy-done.4) | copy-start | bytes 786436
  257.2 35.4 %collective-permute-start.4 = (f32[8,256,256]{2,1,0:T(8,128)S(1)}, f32[8,256,256]{2,1,0:T(8,128)}, u32[]{:S(2)}, u32[]{:S(2)}) collective-permute-start(f32[8,256,256]{2,1,0:T(8,128)S(1)} %broadcast_select_fusion.3), channel_id=1, source_target_pairs={{0,1},{1,0},{2,3},{3,2},{4,5},{5,4},{6,7},{7,6},{8,9},{9,8},{10,11... | collective-permute-start | bytes 6291464 | tf_op jit(solution)/shard_map/ppermute | solution.py:80
  286.2 2.6 copy-start.11
  286.3 2.6 copy-start.12
  294.7 3.6 %copy-start.1 = (f32[1,8,256,1,2,256]{5,4,3,2,1,0:T(2,128)S(1)}, f32[1,8,256,1,2,256]{5,4,3,2,1,0:T(2,128)}, u32[]{:S(2)}) copy-start(f32[1,8,256,1,2,256]{5,4,3,2,1,0:T(2,128)} %param.18) | copy-start | bytes 12582916
  305.4 1.0 copy-start.8
  305.4 1.0 copy-start.9

commit v10 on v7

--- a/solution.py
+++ b/solution.py
@@ -125,19 +125,30 @@
     )
     cols_solved = jnp.einsum("cak,bk->cab", cols_panel, inverse, precision=HI)
     folded = jnp.einsum("mk,cbm->ckb", inverse, cols_solved, precision=HI)
-    update = tiles - jnp.einsum("rak,ckb->racb", rows_panel, folded, precision=HI)
 
     row_index = jnp.arange(rt, dtype=jnp.int32) * prows + p
     col_index = jnp.arange(ct, dtype=jnp.int32) * pcols + q
     trailing = (row_index >= PANELS)[:, None, None, None] & (col_index >= PANELS)[
         None, None, :, None
     ]
+    qc = jnp.minimum(q, PANELS - 1)
+
+    def panel_branch(_):
+        inverse_rows = lax.dynamic_slice_in_dim(inverse, qc * tile, tile, axis=0)
+        solved = jnp.einsum("rak,bk->rab", rows_panel, inverse_rows, precision=HI)
+        rest = tiles[:, :, 1:, :] - jnp.einsum(
+            "rak,ckb->racb", rows_panel, folded[1:], precision=HI
+        )
+        return jnp.concatenate([solved[:, :, None, :], rest], axis=2)
+
+    def trailing_branch(_):
+        return tiles - jnp.einsum("rak,ckb->racb", rows_panel, folded, precision=HI)
+
+    update = lax.cond(q < PANELS, panel_branch, trailing_branch, None)
     out = jnp.where(trailing, update, 0.0)
 
-    qc = jnp.minimum(q, PANELS - 1)
     pc = jnp.minimum(p, PANELS - 1)
-    inverse_rows = lax.dynamic_slice_in_dim(inverse, qc * tile, tile, axis=0)
-    panel_vals = jnp.einsum("rak,bk->rab", rows_panel, inverse_rows, precision=HI)
+    panel_vals = update[:, :, 0, :]
     diag_tile = lax.dynamic_slice(factor, (pc * tile, qc * tile), (tile, tile))
     panel_vals = panel_vals.at[0].set(jnp.where(p < PANELS, diag_tile, panel_vals[0]))
     out = out.at[:, :, 0, :].set(jnp.where(q < PANELS, panel_vals, out[:, :, 0, :]))

time: 313 us -> 340 us (1.086)
  the two profiles are of different devices: /device:TPU:1 before, /device:TPU:7 now
where the time goes in v10:
time: 340 us; the launch traced here: 334 us
  other arithmetic  147 us (43%)
  local copies, waits for them, and re-layouts  59.1 us (17%)
  waiting for transfers between devices  49.4 us (15%)
  starting transfers between devices  45.7 us (13%)
  matrix products  28.8 us (8%)
  between operations  3.64 us (1%)
    ppermute x8, waiting for transfers between devices, pcol_broadcast_pair(): got = lax.ppermute(buf, 'pcol', pairs)  44 us
    another operation x7, other arithmetic, per_device(): l11 = jnp.tril(jnp.linalg.cholesky(schur))  34.7 us
    another operation x6, other arithmetic, per_device(): l00 = jnp.tril(jnp.linalg.cholesky(a00))  34 us
    another operation x4, other arithmetic, per_device(): l00_inv = jax.scipy.linalg.solve_triangular(l00, eye, lower=True)  20.4 us
    another operation x2, other arithmetic, per_device(): l11_inv = jax.scipy.linalg.solve_triangular(l11, eye, lower=True)  20.4 us
    ppermute x2, starting transfers between devices, pcol_broadcast_pair(): other = lax.ppermute(buf, 'pcol', [(i, i ^ 1) for i in range(pcols)])  19.5 us
    dot_general x1, matrix products, trailing_branch(): return tiles - jnp.einsum('rak,ckb->racb', rows_panel, folded, precision=HI)  17.1 us
    unnamed x43, local copies, waits for them, and re-layouts  15.7 us
  transfers between devices with their start and end apart: 20, of which 4 were waited for; matrix products, arithmetic and copies ran while one was open for 48% of the time, Pallas kernels for 0%

profile of v10, /device:TPU:7, one launch (start us, length us, event | category | flops | bytes accessed | tf_op | source)
XLA Modules:
  0.0 334.2 jit_solution(12312443307871348610)
XLA Ops:
  0.0 7.2 %copy.33 = f32[1,8,256,1,2,256]{2,5,4,1,3,0:T(8,128)} copy(f32[1,8,256,1,2,256]{5,4,3,2,1,0:T(2,128)} %param.20) | data formatting | bytes 8388608 | tf_op args[0]
  11.6 3.1 slice_bitcast_fusion.4
  16.0 1.7 bitcast_dynamic-update-slice_fusion.9
  20.5 3.0 collective-permute-start.5
  31.3 5.3 %collective-permute-done.5 = f32[256,2,256]{2,1,0:T(2,128)S(1)} collective-permute-done((f32[256,2,256]{2,1,0:T(2,128)S(1)}, f32[256,2,256]{2,1,0:T(2,128)S(1)}, u32[]{:S(2)}, u32[]{:S(2)}) %collective-permute-start.5) | collective-permute-done | bytes 524320 | tf_op jit(solution)/shard_map/ppermute | solution.py:12
  37.1 1.4 collective-permute-start.6
  42.0 39.8 %collective-permute-done.16 = f32[2,256,256]{1,2,0:T(8,128)S(1)} collective-permute-done((f32[2,256,256]{1,2,0:T(8,128)S(1)}, f32[2,256,256]{1,2,0:T(8,128)S(1)}, u32[]{:S(2)}, u32[]{:S(2)}) %collective-permute-start.16) | collective-permute-done | bytes 524320 | tf_op jit(solution)/shard_map/ppermute | solution.py:76
  81.8 1.4 broadcast_select_fusion.10
  85.3 1.4 broadcast_select_fusion.1
  86.7 2.3 collective-permute-start.7
  89.0 1.6 collective-permute-done.17
  90.6 1.5 broadcast_select_fusion.11
  92.1 2.1 collective-permute-start.18
  97.3 2.6 collective-permute-done.18
  99.9 1.7 broadcast_select_fusion.12
  101.6 19.4 %collective-permute-start.19 = (f32[2,256,256]{1,2,0:T(8,128)S(1)}, f32[2,256,256]{1,2,0:T(8,128)S(1)}, u32[]{:S(2)}, u32[]{:S(2)}) collective-permute-start(f32[2,256,256]{1,2,0:T(8,128)S(1)} %broadcast_select_fusion.12), channel_id=1, source_target_pairs={{0,1},{1,0},{2,3},{3,2},{4,5},{5,4},{6,7},{7,6},{8,9},{9,8},{10,11... | collective-permute-start | bytes 1572872 | tf_op jit(solution)/shard_map/ppermute | solution.py:80
  122.1 1.4 pad_maximum_fusion.2
  124.6 11.7 %cholesky.130 = f32[128,128]{1,0:T(8,128)S(1)} custom-call(f32[128,128]{1,0:T(8,128)S(1)} %cholesky.194), custom_call_target="Cholesky" | custom-call | tf_op jit(solution)/shard_map/jit(cholesky)/cholesky | solution.py:103
  136.3 9.8 %custom-call.13 = f32[1,128,128]{1,2,0:T(8,128)S(1)} custom-call(f32[1,128,128]{2,1,0:T(8,128)S(1)} %get-tuple-element.129), custom_call_target="InvertDiagBlocksLowerTriangular" | custom-call | tf_op jit(solution)/shard_map/jit(cholesky)/cholesky | solution.py:103
  146.4 3.8 %broadcast_select_fusion.4 = f32[8,256,256]{1,2,0:T(8,128)} fusion(f32[8,256,256]{1,2,0:T(8,128)} %collective-permute-done.1, f32[8,256,256]{1,2,0:T(8,128)S(1)} %broadcast_select_fusion.3, pred[]{:T(512)} %compare_reduce_fusion.7), kind=kLoop, calls=%fused_computation.43 | loop fusion | flops 524288 | bytes 6291457 | tf_op jit(solution)/shard_map/jit(_where)/select_n | solution.py:79
  150.2 3.8 %collective-permute-start.2 = (f32[8,256,256]{1,2,0:T(8,128)}, f32[8,256,256]{1,2,0:T(8,128)}, u32[]{:S(2)}, u32[]{:S(2)}) collective-permute-start(f32[8,256,256]{1,2,0:T(8,128)} %broadcast_select_fusion.4), channel_id=1, source_target_pairs={{0,4},{16,20},{8,12},{24,28},{1,13},{9,5},{17,29},{25,21},{32,36},... | collective-permute-start | bytes 6291464 | tf_op jit(solution)/shard_map/ppermute | solution.py:76
  154.3 11.7 %cholesky.147 = f32[128,128]{1,0:T(8,128)S(1)} custom-call(f32[128,128]{1,0:T(8,128)S(1)} %convolution_subtract_fusion.3), custom_call_target="Cholesky" | custom-call | tf_op jit(solution)/shard_map/jit(cholesky)/cholesky | solution.py:103
  168.8 4.1 %while.6 = (s32[]{:T(128)}, f32[256,256]{1,0:T(8,128)S(1)}, s32[2,2]{1,0:T(2,128)S(1)}, f32[2,128,128]{2,1,0:T(8,128)S(1)}, s32[]{:T(128)}) while((s32[]{:T(128)}, f32[256,256]{1,0:T(8,128)S(1)}, s32[2,2]{1,0:T(2,128)S(1)}, f32[2,128,128]{2,1,0:T(8,128)S(1)}, s32[]{:T(128)}) %tuple.68), condition=%wide.while_cond.2, body=%wide.while_body.2.sunk | while | flops 2 | bytes 131181 | solution.py:107
  172.9 19.7 %custom-call.14 = f32[2,128,128]{1,2,0:T(8,128)S(1)} custom-call(f32[2,128,128]{2,1,0:T(8,128)S(1)} %get-tuple-element.72), custom_call_target="InvertDiagBlocksLowerTriangular" | custom-call | tf_op jit(solution)/shard_map/jit(_solve_triangular)/triangular_solve | solution.py:107
  193.5 2.7 broadcast_select_fusion.5
  196.2 3.4 %collective-permute-start.3 = (f32[8,256,256]{1,2,0:T(8,128)S(1)}, f32[8,256,256]{1,2,0:T(8,128)}, u32[]{:S(2)}, u32[]{:S(2)}) collective-permute-start(f32[8,256,256]{1,2,0:T(8,128)S(1)} %broadcast_select_fusion.5), channel_id=1, source_target_pairs={{0,2},{16,18},{8,10},{24,26},{4,6},{20,22},{12,14},{28,30},{1,15},... | collective-permute-start | bytes 6291464 | tf_op jit(solution)/shard_map/ppermute | solution.py:76
  201.5 11.7 %cholesky.164 = f32[128,128]{1,0:T(8,128)S(1)} custom-call(f32[128,128]{1,0:T(8,128)S(1)} %cholesky.197), custom_call_target="Cholesky" | custom-call | tf_op jit(solution)/shard_map/jit(cholesky)/cholesky | solution.py:110
  213.2 9.8 %custom-call.15 = f32[1,128,128]{1,2,0:T(8,128)S(1)} custom-call(f32[1,128,128]{2,1,0:T(8,128)S(1)} %get-tuple-element.125), custom_call_target="InvertDiagBlocksLowerTriangular" | custom-call | tf_op jit(solution)/shard_map/jit(cholesky)/cholesky | solution.py:110
  225.5 11.7 %cholesky.181 = f32[128,128]{1,0:T(8,128)S(1)} custom-call(f32[128,128]{1,0:T(8,128)S(1)} %convolution_subtract_fusion.2), custom_call_target="Cholesky" | custom-call | tf_op jit(solution)/shard_map/jit(cholesky)/cholesky | solution.py:110
  240.7 2.2 broadcast_select_fusion.6
  243.1 4.0 %while.7 = (s32[]{:T(128)}, f32[256,256]{1,0:T(8,128)S(1)}, s32[2,2]{1,0:T(2,128)S(1)}, f32[2,128,128]{2,1,0:T(8,128)S(1)}, s32[]{:T(128)}) while((s32[]{:T(128)}, f32[256,256]{1,0:T(8,128)S(1)}, s32[2,2]{1,0:T(2,128)S(1)}, f32[2,128,128]{2,1,0:T(8,128)S(1)}, s32[]{:T(128)}) %tuple.78), condition=%wide.while_cond.2.clone, body=%wide.while_body.2.clone.sunk | while | flops 2 | bytes 131181 | solution.py:111
  243.7 1.4 bitcast_dynamic-update-slice_fusion.13
  245.7 1.4 bitcast_dynamic-update-slice_fusion.13
  248.0 19.7 %custom-call.16 = f32[2,128,128]{1,2,0:T(8,128)S(1)} custom-call(f32[2,128,128]{2,1,0:T(8,128)S(1)} %get-tuple-element.73), custom_call_target="InvertDiagBlocksLowerTriangular" | custom-call | tf_op jit(solution)/shard_map/jit(_solve_triangular)/triangular_solve | solution.py:111
  270.8 3.5 %fusion.13 = f32[2,256,512]{2,1,0:T(8,128)S(1)} fusion(f32[2,256,512]{1,0,2:T(2,128)S(1)} %copy-done.7, f32[256,256]{1,0:T(8,128)S(1)} %pad_maximum_fusion.4, f32[128,256]{1,0:T(8,128)S(1)} %fusion.38, f32[128,256]{1,0:T(8,128)S(1)} %fusion.33, f32[256,256]{1,0:T(8,128)S(1)} %convolution_negate_fusion), kind=kOutput, calls=%fused_computation.37 | convolution fusion | flops 1611923456 | bytes 2883584 | tf_op jit(solution)/shard_map/cak,bk->cab/dot_general | solution.py:126
  274.3 1.8 convolution_bitcast_fusion.1
  276.1 1.9 broadcast_select_fusion.8
  278.0 2.2 pad_maximum_fusion.1
  280.2 28.3 %conditional.1 = (f32[8,256,2,256]{1,3,0,2:T(8,128)}) conditional(s32[]{:T(128)} %convert_element_type.8, (f32[8,256,512]{1,2,0:T(8,128)}, f32[2,512,256]{1,2,0:T(8,128)S(1)}, f32[8,256,2,256]{1,3,2,0:T(8,128)}) %tuple.76, (s32[]{:T(128)}, f32[512,512]{1,0:T(8,128)}, f32[8,256,512]{1,2,0:T(8,128)}, f32[8,256,2,256]{1,3,2,0:T(8,128)}, ...), branch_computations={%region_14.17_spmd, %region_15.18_spmd} | conditional | flops 6444023808 | bytes 30408712 | solution.py:147
  280.4 5.4 %copy.41 = f32[8,256,2,256]{3,1,2,0:T(8,128)} copy(f32[8,256,2,256]{1,3,2,0:T(8,128)} %get-tuple-element.84) | data formatting | bytes 8388608 | tf_op jit(solution)/shard_map
  285.8 17.1 %fusion.2 = f32[8,256,2,256]{3,1,2,0:T(8,128)} fusion(f32[8,256,2,256]{3,1,2,0:T(8,128)} %copy.41, f32[8,256,512]{1,2,0:T(8,128)} %get-tuple-element.82, f32[2,512,256]{1,2,0:T(8,128)S(1)} %get-tuple-element.83), kind=kOutput, calls=%fused_computation.2 | convolution fusion | flops 6443499520 | bytes 13631488 | tf_op jit(solution)/shard_map/cond/branch_0_fun/rak,ckb->racb/dot_general | solution.py:145
  302.8 5.4 %copy.31 = f32[8,256,2,256]{1,3,0,2:T(8,128)} copy(f32[8,256,2,256]{3,1,2,0:T(8,128)} %fusion.2) | data formatting | bytes 8388608 | tf_op jit(solution)/shard_map/cond/branch_0_fun/sub | solution.py:145
  308.5 5.4 %copy.45 = f32[8,256,2,256]{3,1,0,2:T(8,128)} copy(f32[8,256,2,256]{1,3,0,2:T(8,128)} %get-tuple-element.222) | data formatting | bytes 8388608 | tf_op jit(solution)/shard_map/cond | solution.py:147
  314.8 2.0 slice_bitcast_fusion.3
  317.6 2.7 broadcast_select_fusion
  320.3 2.6 fusion.66
  323.3 3.2 fusion.11
  326.5 7.4 %copy.49 = f32[1,8,256,1,2,256]{5,4,3,2,1,0:T(2,128)} copy(f32[1,8,256,1,2,256]{5,2,1,4,3,0:T(8,128)} %fusion.11) | data formatting | bytes 8388608 | tf_op jit(solution)/shard_map/scatter | solution.py:154
  (144 shorter events, 48.2 us)
Async XLA Ops:
  8.2 9.5 %collective-permute-start.8 = (f32[256,256]{0,1:T(8,128)S(1)}, f32[256,256]{0,1:T(8,128)S(1)}, u32[]{:S(2)}, u32[]{:S(2)}) collective-permute-start(f32[256,256]{0,1:T(8,128)S(1)} %slice_bitcast_fusion.12), channel_id=1, source_target_pairs={{0,32},{32,64},{1,33},{33,65}} | collective-permute-start | bytes 786440 | tf_op jit(solution)/shard_map/ppermute | solution.py:34
  8.8 10.2 %collective-permute-start.9 = (f32[256,256]{0,1:T(8,128)S(1)}, f32[256,256]{0,1:T(8,128)S(1)}, u32[]{:S(2)}, u32[]{:S(2)}) collective-permute-start(f32[256,256]{0,1:T(8,128)S(1)} %slice_bitcast_fusion.12), channel_id=1, source_target_pairs={{0,64},{32,96},{1,65},{33,97}} | collective-permute-start | bytes 786440 | tf_op jit(solution)/shard_map/ppermute | solution.py:34
  9.5 10.9 %collective-permute-start.10 = (f32[256,256]{0,1:T(8,128)S(1)}, f32[256,256]{0,1:T(8,128)S(1)}, u32[]{:S(2)}, u32[]{:S(2)}) collective-permute-start(f32[256,256]{0,1:T(8,128)S(1)} %slice_bitcast_fusion.12), channel_id=1, source_target_pairs={{0,96},{32,128},{1,97},{33,129}} | collective-permute-start | bytes 786440 | tf_op jit(solution)/shard_map/ppermute | solution.py:34
  10.2 14.0 %collective-permute-start.11 = (f32[256,256]{0,1:T(8,128)S(1)}, f32[256,256]{0,1:T(8,128)S(1)}, u32[]{:S(2)}, u32[]{:S(2)}) collective-permute-start(f32[256,256]{0,1:T(8,128)S(1)} %slice_bitcast_fusion.12), channel_id=1, source_target_pairs={{0,128},{32,160},{1,129},{33,161}} | collective-permute-start | bytes 786440 | tf_op jit(solution)/shard_map/ppermute | solution.py:34
  10.9 15.0 %collective-permute-start.12 = (f32[256,256]{0,1:T(8,128)S(1)}, f32[256,256]{0,1:T(8,128)S(1)}, u32[]{:S(2)}, u32[]{:S(2)}) collective-permute-start(f32[256,256]{0,1:T(8,128)S(1)} %slice_bitcast_fusion.12), channel_id=1, source_target_pairs={{0,160},{32,192},{1,161},{33,193}} | collective-permute-start | bytes 786440 | tf_op jit(solution)/shard_map/ppermute | solution.py:34
  17.7 8.9 %collective-permute-start.13 = (f32[256,256]{0,1:T(8,128)S(1)}, f32[256,256]{0,1:T(8,128)S(1)}, u32[]{:S(2)}, u32[]{:S(2)}) collective-permute-start(f32[256,256]{0,1:T(8,128)S(1)} %slice_bitcast_fusion.12), channel_id=1, source_target_pairs={{0,192},{32,224},{1,193},{33,225}} | collective-permute-start | bytes 786440 | tf_op jit(solution)/shard_map/ppermute | solution.py:34
  19.1 8.3 %collective-permute-start.14 = (f32[256,256]{0,1:T(8,128)S(1)}, f32[256,256]{0,1:T(8,128)S(1)}, u32[]{:S(2)}, u32[]{:S(2)}) collective-permute-start(f32[256,256]{0,1:T(8,128)S(1)} %slice_bitcast_fusion.12), channel_id=1, source_target_pairs={{0,224},{32,0},{1,225},{33,1}} | collective-permute-start | bytes 786440 | tf_op jit(solution)/shard_map/ppermute | solution.py:34
  20.5 16.2 %collective-permute-start.5 = (f32[256,2,256]{2,1,0:T(2,128)S(1)}, f32[256,2,256]{2,1,0:T(2,128)S(1)}, u32[]{:S(2)}, u32[]{:S(2)}) collective-permute-start(f32[256,2,256]{2,1,0:T(2,128)S(1)} %get-tuple-element.115), channel_id=1, source_target_pairs={{0,32},{32,0},{1,33},{33,1},{2,34},{34,2},{3,35},{35,3},{4,36},{36... | collective-permute-start | bytes 1572872 | tf_op jit(solution)/shard_map/ppermute | solution.py:12
  24.2 5.7 %copy-start.16 = (s32[2]{0:T(128)S(1)}, s32[2]{0:T(128)}, u32[]{:S(2)}) copy-start(s32[2]{0:T(128)} %constant.184.clone) | copy-start | bytes 28
  24.2 6.4 %copy-start.15 = (s32[4]{0:T(128)S(1)}, s32[4]{0:T(128)}, u32[]{:S(2)}) copy-start(s32[4]{0:T(128)} %constant.185.clone) | copy-start | bytes 52
  24.2 70.7 %collective-permute-start = (f32[8,256,256]{1,2,0:T(8,128)}, f32[8,256,256]{1,2,0:T(8,128)S(1)}, u32[]{:S(2)}, u32[]{:S(2)}) collective-permute-start(f32[8,256,256]{1,2,0:T(8,128)} %slice_bitcast_fusion.4), channel_id=1, source_target_pairs={{0,16},{1,9},{32,48},{33,41},{64,80},{65,73},{96,112},{97,105},{12... | collective-permute-start | bytes 6291464 | tf_op jit(solution)/shard_map/ppermute | solution.py:76
  29.2 11.4 %copy-start.14 = (s32[8]{0:T(128)S(1)}, s32[8]{0:T(128)}, u32[]{:S(2)}) copy-start(s32[8]{0:T(128)} %constant.186.clone) | copy-start | bytes 100
  29.2 12.1 %copy-start.13 = (s32[16]{0:T(128)S(1)}, s32[16]{0:T(128)}, u32[]{:S(2)}) copy-start(s32[16]{0:T(128)} %constant.187.clone) | copy-start | bytes 196
  29.2 9.3 %collective-permute-start.15 = (f32[2,256,256]{1,2,0:T(8,128)S(1)}, f32[2,256,256]{1,2,0:T(8,128)S(1)}, u32[]{:S(2)}, u32[]{:S(2)}) collective-permute-start(f32[2,256,256]{1,2,0:T(8,128)S(1)} %pad_maximum_fusion.3), channel_id=1, source_target_pairs={{0,16},{1,9},{32,48},{33,41},{64,80},{65,73},{96,112},{97,105},{12... | collective-permute-start | bytes 1572872 | tf_op jit(solution)/shard_map/ppermute | solution.py:76
  37.1 47.4 %copy-start.12 = (s32[2]{0:T(128)S(1)}, s32[2]{0:T(128)}, u32[]{:S(2)}) copy-start(s32[2]{0:T(128)} %constant.188.clone) | copy-start | bytes 28
  37.1 48.1 %collective-permute-start.6 = (f32[2,256,2,256]{3,2,1,0:T(2,128)S(1)}, f32[2,256,2,256]{3,2,1,0:T(2,128)S(1)}, u32[]{:S(2)}, u32[]{:S(2)}) collective-permute-start(f32[2,256,2,256]{3,2,1,0:T(2,128)S(1)} %maximum_select_fusion), channel_id=1, source_target_pairs={{0,128},{32,160},{1,129},{33,161},{2,130},{34,162},{3,131},{35,163... | collective-permute-start | bytes 3145736 | tf_op jit(solution)/shard_map/ppermute | solution.py:19
  39.2 42.6 %collective-permute-start.16 = (f32[2,256,256]{1,2,0:T(8,128)S(1)}, f32[2,256,256]{1,2,0:T(8,128)S(1)}, u32[]{:S(2)}, u32[]{:S(2)}) collective-permute-start(f32[2,256,256]{1,2,0:T(8,128)S(1)} %broadcast_select_fusion.9), channel_id=1, source_target_pairs={{0,8},{16,24},{1,17},{9,25},{32,40},{48,56},{33,49},{41,57},{64,72... | collective-permute-start | bytes 1572872 | tf_op jit(solution)/shard_map/ppermute | solution.py:76
  83.2 7.4 %collective-permute-start.17 = (f32[2,256,256]{1,2,0:T(8,128)S(1)}, f32[2,256,256]{1,2,0:T(8,128)S(1)}, u32[]{:S(2)}, u32[]{:S(2)}) collective-permute-start(f32[2,256,256]{1,2,0:T(8,128)S(1)} %broadcast_select_fusion.10), channel_id=1, source_target_pairs={{0,4},{16,20},{8,12},{24,28},{1,13},{9,5},{17,29},{25,21},{32,36},... | collective-permute-start | bytes 1572872 | tf_op jit(solution)/shard_map/ppermute | solution.py:76
  85.2 9.0 %copy-start.11 = (s32[4]{0:T(128)S(1)}, s32[4]{0:T(128)}, u32[]{:S(2)}) copy-start(s32[4]{0:T(128)} %constant.189.clone) | copy-start | bytes 52
  85.3 9.7 %copy-start = (f32[1,8,256,1,2,256]{2,5,4,1,3,0:T(8,128)S(1)}, f32[1,8,256,1,2,256]{2,5,4,1,3,0:T(8,128)}, u32[]{:S(2)}) copy-start(f32[1,8,256,1,2,256]{2,5,4,1,3,0:T(8,128)} %copy.33) | copy-start | bytes 12582916
  86.7 34.3 %collective-permute-start.7 = (f32[2,256,2,256]{3,2,1,0:T(2,128)S(1)}, f32[2,256,2,256]{3,2,1,0:T(2,128)}, u32[]{:S(2)}, u32[]{:S(2)}) collective-permute-start(f32[2,256,2,256]{3,2,1,0:T(2,128)S(1)} %broadcast_select_fusion.1), channel_id=1, source_target_pairs={{0,64},{32,96},{128,192},{160,224},{1,65},{33,97},{129,193},{161,2... | collective-permute-start | bytes 3145736 | tf_op jit(solution)/shard_map/ppermute | solution.py:19
  92.1 7.7 %collective-permute-start.18 = (f32[2,256,256]{1,2,0:T(8,128)}, f32[2,256,256]{1,2,0:T(8,128)}, u32[]{:S(2)}, u32[]{:S(2)}) collective-permute-start(f32[2,256,256]{1,2,0:T(8,128)} %broadcast_select_fusion.11), channel_id=1, source_target_pairs={{0,2},{16,18},{8,10},{24,26},{4,6},{20,22},{12,14},{28,30},{1,15},... | collective-permute-start | bytes 1572872 | tf_op jit(solution)/shard_map/ppermute | solution.py:76
  96.0 50.4 %collective-permute-start.1 = (f32[8,256,256]{1,2,0:T(8,128)S(1)}, f32[8,256,256]{1,2,0:T(8,128)}, u32[]{:S(2)}, u32[]{:S(2)}) collective-permute-start(f32[8,256,256]{1,2,0:T(8,128)S(1)} %broadcast_select_fusion.3), channel_id=1, source_target_pairs={{0,8},{16,24},{1,17},{9,25},{32,40},{48,56},{33,49},{41,57},{64,72... | collective-permute-start | bytes 6291464 | tf_op jit(solution)/shard_map/ppermute | solution.py:76
  101.6 21.9 %copy-start.2 = (f32[2,256,256]{1,2,0:T(8,128)}, f32[2,256,256]{1,2,0:T(8,128)S(1)}, u32[]{:S(2)}) copy-start(f32[2,256,256]{1,2,0:T(8,128)S(1)} %broadcast_select_fusion.12) | copy-start | bytes 1572868
  101.6 21.9 %collective-permute-start.19 = (f32[2,256,256]{1,2,0:T(8,128)S(1)}, f32[2,256,256]{1,2,0:T(8,128)S(1)}, u32[]{:S(2)}, u32[]{:S(2)}) collective-permute-start(f32[2,256,256]{1,2,0:T(8,128)S(1)} %broadcast_select_fusion.12), channel_id=1, source_target_pairs={{0,1},{1,0},{2,3},{3,2},{4,5},{5,4},{6,7},{7,6},{8,9},{9,8},{10,11... | collective-permute-start | bytes 1572872 | tf_op jit(solution)/shard_map/ppermute | solution.py:80
  123.5 0.8 copy-start.4
  150.2 43.3 %collective-permute-start.2 = (f32[8,256,256]{1,2,0:T(8,128)}, f32[8,256,256]{1,2,0:T(8,128)}, u32[]{:S(2)}, u32[]{:S(2)}) collective-permute-start(f32[8,256,256]{1,2,0:T(8,128)} %broadcast_select_fusion.4), channel_id=1, source_target_pairs={{0,4},{16,20},{8,12},{24,28},{1,13},{9,5},{17,29},{25,21},{32,36},... | collective-permute-start | bytes 6291464 | tf_op jit(solution)/shard_map/ppermute | solution.py:76
  193.5 6.5 %copy-start.3 = (f32[2,256,256]{1,2,0:T(8,128)S(1)}, f32[2,256,256]{1,2,0:T(8,128)}, u32[]{:S(2)}) copy-start(f32[2,256,256]{1,2,0:T(8,128)} %copy-done.2) | copy-start | bytes 1572868
  193.5 6.5 %copy-start.5 = (f32[2,256,256]{1,2,0:T(8,128)S(1)}, f32[2,256,256]{1,2,0:T(8,128)}, u32[]{:S(2)}) copy-start(f32[2,256,256]{1,2,0:T(8,128)} %copy-done.4) | copy-start | bytes 1572868
  196.2 44.5 %collective-permute-start.3 = (f32[8,256,256]{1,2,0:T(8,128)S(1)}, f32[8,256,256]{1,2,0:T(8,128)}, u32[]{:S(2)}, u32[]{:S(2)}) collective-permute-start(f32[8,256,256]{1,2,0:T(8,128)S(1)} %broadcast_select_fusion.5), channel_id=1, source_target_pairs={{0,2},{16,18},{8,10},{24,26},{4,6},{20,22},{12,14},{28,30},{1,15},... | collective-permute-start | bytes 6291464 | tf_op jit(solution)/shard_map/ppermute | solution.py:76
  200.8 0.7 copy-start.10
  242.9 33.2 %collective-permute-start.4 = (f32[8,256,256]{1,2,0:T(8,128)}, f32[8,256,256]{1,2,0:T(8,128)S(1)}, u32[]{:S(2)}, u32[]{:S(2)}) collective-permute-start(f32[8,256,256]{1,2,0:T(8,128)} %broadcast_select_fusion.6), channel_id=1, source_target_pairs={{0,1},{1,0},{2,3},{3,2},{4,5},{5,4},{6,7},{7,6},{8,9},{9,8},{10,11... | collective-permute-start | bytes 6291464 | tf_op jit(solution)/shard_map/ppermute | solution.py:80
  268.0 2.8 copy-start.7
  314.8 2.8 copy-start.1
  320.3 2.7 copy-start.6
  320.3 2.7 copy-start.8
  320.3 2.7 copy-start.9
